TPU v7x, 768 devices: a whole 4x8x12 slice. The times are simulated.
768 devices in a mesh: ctx: 96 (over y, z), section: 2 (over core), tp: 4 (over x).
Axes of the slice: x: 4, y: 8, z: 12, core: 2. Of those that a mesh axis runs over, the one named last changes fastest.
Arguments:
- residual: bfloat16 [24576, 3584], P('ctx', 'tp'), may hold values from -6 to 6
- queries: bfloat16 [2, 24576, 2048], P('section', 'ctx', 'tp'), may hold values from -5 to 5
- keys: bfloat16 [2, 24576, 512], P('section', 'ctx', 'tp'), may hold values from -5 to 5
- window_values: bfloat16 [24576, 512], P('ctx', 'tp'), may hold values from -6 to 6
- mixing: bfloat16 [2, 2048, 3584], P('section', 'tp'), may hold values from -0.125 to 0.125
- norm_gain: bfloat16 [3584], replicated, may hold values from 0.5 to 1.5
- log_decay: float32 [24576, 16], P('ctx', 'tp'), may hold values from -1 to 0
- spike_counts: int32 [24576, 2048], P('ctx', 'tp'), may hold values from 0 to 3
- thresholds: float32 [2048], P('tp'), may hold values from 0.5 to 2
- lengths: int32 [96], replicated, may hold values from 128 to 256, as said below
Outputs:
- head_outputs: bfloat16 [2, 24576, 2048], P('section', 'ctx', 'tp')
- hidden: bfloat16 [24576, 3584], P('ctx', 'tp')
Inputs may be any that keep to these rules, and one draw needn't show every extreme that they name: `lengths`: the valid tokens of a shard come first; some shard is full in every draw.
All inputs are finite; a program needn't handle non-finite values.
Results may differ from a plain program's by a relative error of at most 0.015.
Values may be sent and summed in bfloat16 or wider, within the bound.
No kernel may reach another device: no remote copies, remote signals or barrier semaphores. Data moves between devices by JAX's collectives and lax.ppermute only.
A program may use at most 128 MiB of HBM per device.

v0:
```python
import math

import jax
import jax.numpy as jnp
from jax import lax
from jax.sharding import PartitionSpec as P

HEAD = 128
WINDOW = 4096


def passed_along(x, axis, by):
    devices = lax.axis_size(axis)
    pairs = [(i, i + by) for i in range(devices) if 0 <= i + by < devices]
    return lax.ppermute(x, axis, pairs)


def entering(x, axis, join, neutral):
    place = lax.axis_index(axis)
    gathered = jax.tree.map(
        lambda a, kind: lax.all_gather(a.astype(kind), axis), x, (jnp.bfloat16, jnp.bfloat16)
    )
    state = jax.tree.map(lambda a, e: jnp.zeros_like(a) + jnp.asarray(e, a.dtype), x, neutral)

    def one(step, state):
        return join(
            state,
            jax.tree.map(
                lambda a, own: lax.dynamic_index_in_dim(a, step, 0, False).astype(own.dtype),
                gathered,
                x,
            ),
        )

    return lax.fori_loop(0, place, one, state)


def body(
    residual,
    queries,
    keys,
    window_values,
    mixing,
    norm_gain,
    log_decay,
    spike_counts,
    thresholds,
    lengths,
):
    section_index = lax.axis_index("section")
    shard_index = lax.axis_index("ctx")
    row_count = keys.shape[1]
    head_size = HEAD
    key_heads = keys.shape[2] // head_size
    query_head_rows = queries.shape[2] // head_size
    group_size = query_head_rows // key_heads
    span_blocks = WINDOW // row_count
    feature_count = mixing.shape[2]
    scale = 1.0 / math.sqrt(head_size)
    positions = jnp.arange(row_count, dtype=jnp.int32)
    valid_rows = positions < lengths[shard_index]
    own_keys = keys[0]
    earlier = [
        passed_along((own_keys, window_values), "ctx", distance + 1)
        for distance in range(span_blocks)
    ]
    key_blocks = jnp.stack([pair[0] for pair in earlier[::-1]] + [own_keys], 0)
    value_blocks = jnp.stack([pair[1] for pair in earlier[::-1]] + [window_values], 0)

    def window_layer(dummy_arg):
        query_rows = queries[0].reshape(row_count, key_heads, group_size, head_size)
        sources = shard_index - span_blocks + jnp.arange(span_blocks + 1, dtype=jnp.int32)
        block_valid = (sources[:, None] >= 0) & (
            positions[None, :] < lengths[jnp.clip(sources, 0, None)][:, None]
        )
        offsets = (span_blocks - jnp.arange(span_blocks + 1, dtype=jnp.int32)) * row_count
        base_distance = positions[:, None] - positions[None, :]

        def weight_step(carry, items):
            running, totals, best = carry
            scores = (
                jnp.einsum(
                    "rgjd,kgd->gjrk",
                    query_rows,
                    items[0].reshape(row_count, key_heads, head_size),
                    preferred_element_type=jnp.float32,
                )
                * scale
            )
            distance = base_distance + items[3]
            allowed = items[2][None, :] & (distance >= 0) & (distance < WINDOW)
            scores = jnp.where(allowed, scores, -1e30)
            new_best = jnp.maximum(best, jnp.max(scores, axis=-1))
            factor = jnp.exp(best - new_best)
            weights = jnp.where(allowed, jnp.exp(scores - new_best[..., None]), 0.0)
            blended = jnp.einsum(
                "gjrk,kgd->gjrd",
                weights.astype(jnp.bfloat16),
                items[1].reshape(row_count, key_heads, head_size),
                preferred_element_type=jnp.float32,
            )
            return (
                (
                    running * factor[..., None] + blended,
                    totals * factor + jnp.sum(weights, axis=-1),
                    new_best,
                ),
                None,
            )

        start_sums = (
            jnp.zeros((key_heads, group_size, row_count, head_size), jnp.float32),
            jnp.zeros((key_heads, group_size, row_count), jnp.float32),
            jnp.full((key_heads, group_size, row_count), -1e30, jnp.float32),
        )
        (blended, totals, unused_best), unused_sum = lax.scan(
            weight_step, start_sums, (key_blocks, value_blocks, block_valid, offsets)
        )
        attention = blended / jnp.maximum(totals, 1.0)[..., None]
        attention = attention.transpose(2, 0, 1, 3).reshape(row_count, query_head_rows * head_size)
        attention = jnp.where(valid_rows[:, None], attention, 0.0).astype(jnp.bfloat16)
        projected = jnp.dot(attention, mixing[0], preferred_element_type=jnp.float32)
        return (attention, projected)

    def window_skip(dummy_arg):
        return (
            jnp.zeros((row_count, query_head_rows * head_size), jnp.bfloat16),
            jnp.zeros((row_count, feature_count), jnp.float32),
        )

    attention, projected = lax.cond(section_index == 0, window_layer, window_skip, 0)
    share = lax.psum_scatter(
        projected.astype(jnp.bfloat16), "tp", scatter_dimension=1, tiled=True
    ).astype(jnp.float32)
    own_hidden = (share + residual.astype(jnp.float32)).astype(jnp.bfloat16)
    moved_share = passed_along(own_hidden, "section", 1)
    local_activations = jnp.where(section_index == 0, own_hidden, moved_share)
    complete_hidden_matrix = lax.all_gather(local_activations, "tp", axis=1, tiled=True)
    masked_keys = jnp.where(valid_rows[:, None], own_keys, jnp.zeros_like(own_keys)).reshape(
        row_count, key_heads, head_size
    )
    wide_keys = masked_keys.astype(jnp.float32)
    decays = log_decay * valid_rows[:, None].astype(jnp.float32)

    def linear_prepare(dummy_arg):
        wide = complete_hidden_matrix.astype(jnp.float32)
        normed = (
            wide
            * lax.rsqrt(jnp.mean(wide * wide, axis=-1, keepdims=True) + 1e-05)
            * norm_gain.astype(jnp.float32)
        ).astype(jnp.bfloat16)
        payload_vectors = lax.dot_general(
            normed, mixing[0], (((1,), (1,)), ((), ())), preferred_element_type=jnp.float32
        ).astype(jnp.bfloat16)
        cumulated = jnp.cumsum(decays, axis=0).reshape(row_count, key_heads, group_size)
        value_rows = payload_vectors.astype(jnp.float32).reshape(
            row_count, key_heads, group_size, head_size
        )
        fresh_state = jnp.einsum(
            "sgd,sgje->gdje",
            wide_keys,
            value_rows * jnp.exp(cumulated[-1] - cumulated)[..., None],
            precision=lax.Precision.HIGHEST,
        )
        return (payload_vectors, cumulated, fresh_state)

    def linear_skip(dummy_arg):
        return (
            jnp.zeros((row_count, query_head_rows * head_size), jnp.bfloat16),
            jnp.zeros((row_count, key_heads, group_size), jnp.float32),
            jnp.zeros((key_heads, head_size, group_size, head_size), jnp.float32),
        )

    payload_vectors, cumulated, fresh_state = lax.cond(
        section_index == 1, linear_prepare, linear_skip, 0
    )

    def chain(previous_entry, latter):
        return (
            previous_entry[0] + latter[0],
            previous_entry[1] * jnp.exp(latter[0])[:, None, :, None] + latter[1],
        )

    identity = (jnp.zeros((key_heads, group_size), jnp.float32), jnp.zeros_like(fresh_state))
    unused_total, incoming = entering((cumulated[-1], fresh_state), "ctx", chain, identity)

    def linear_finish(dummy_arg):
        query_narrow = queries[0].reshape(row_count, key_heads, group_size, head_size)
        query_rows = query_narrow.astype(jnp.float32)
        value_rows = payload_vectors.astype(jnp.float32).reshape(
            row_count, key_heads, group_size, head_size
        )
        inter = (
            jnp.einsum("rgjd,gdje->rgje", query_rows, incoming, precision=lax.Precision.HIGHEST)
            * jnp.exp(cumulated)[..., None]
        )
        products = jnp.einsum(
            "rgjd,sgd->gjrs", query_narrow, masked_keys, preferred_element_type=jnp.float32
        )
        ordered = cumulated.transpose(1, 2, 0)
        spread = ordered[..., :, None] - ordered[..., None, :]
        triangle = positions[:, None] >= positions[None, :]
        damping = jnp.where(triangle, jnp.exp(jnp.minimum(spread, 0.0)), 0.0)
        intra = jnp.einsum(
            "gjrs,sgje->rgje", products * damping, value_rows, precision=lax.Precision.HIGHEST
        )
        mixed = (inter + intra).reshape(row_count, query_head_rows, head_size)
        scaled = mixed * lax.rsqrt(jnp.mean(mixed * mixed, axis=-1, keepdims=True) + 1e-05)
        gating = spike_counts.astype(jnp.float32).reshape(
            row_count, query_head_rows, head_size
        ) * thresholds.reshape(query_head_rows, head_size)
        return jnp.where(
            valid_rows[:, None],
            (scaled * gating).reshape(row_count, query_head_rows * head_size),
            0.0,
        ).astype(jnp.bfloat16)

    def finish_skip(dummy_arg):
        return jnp.zeros((row_count, query_head_rows * head_size), jnp.bfloat16)

    gated = lax.cond(section_index == 1, linear_finish, finish_skip, 0)
    head_outputs = jnp.where(section_index == 0, attention, gated)[None]
    return (head_outputs, local_activations)


def solution(mesh):
    return jax.shard_map(
        body,
        mesh=mesh,
        in_specs=(
            P("ctx", "tp"),
            P("section", "ctx", "tp"),
            P("section", "ctx", "tp"),
            P("ctx", "tp"),
            P("section", "tp", None),
            P(),
            P("ctx", "tp"),
            P("ctx", "tp"),
            P("tp"),
            P(),
        ),
        out_specs=(P("section", "ctx", "tp"), P("ctx", "tp")),
        check_vma=False,
    )
```

profile of v0, /device:TPU:760, one launch (start us, length us, event | category | flops | bytes accessed | tf_op | source)
XLA Modules:
  0.0 583.3 jit_solution(11373159453194868979)
XLA Ops:
  13.7 1.3 dynamic_slice.28
  15.8 6.7 %collective-permute-done = bf16[256,128]{1,0:T(8,128)(2,1)S(1)} collective-permute-done((bf16[256,128]{1,0:T(8,128)(2,1)}, bf16[256,128]{1,0:T(8,128)(2,1)S(1)}, u32[]{:S(2)}, u32[]{:S(2)}) %collective-permute-start) | collective-permute-done | bytes 65568 | tf_op jit(solution)/shard_map/ppermute | solution.py:15
  24.4 10.3 %collective-permute-done.16 = bf16[256,128]{1,0:T(8,128)(2,1)S(1)} collective-permute-done((bf16[256,128]{1,0:T(8,128)(2,1)}, bf16[256,128]{1,0:T(8,128)(2,1)S(1)}, u32[]{:S(2)}, u32[]{:S(2)}) %collective-permute-start.16) | collective-permute-done | bytes 65568 | tf_op jit(solution)/shard_map/ppermute | solution.py:15
  52.9 1.8 collective-permute-done.9
  58.5 1.5 collective-permute-done.11
  63.8 9.7 %collective-permute-done.13 = bf16[256,128]{1,0:T(8,128)(2,1)S(1)} collective-permute-done((bf16[256,128]{1,0:T(8,128)(2,1)S(1)}, bf16[256,128]{1,0:T(8,128)(2,1)S(1)}, u32[]{:S(2)}, u32[]{:S(2)}) %collective-permute-start.13) | collective-permute-done | bytes 65568 | tf_op jit(solution)/shard_map/ppermute | solution.py:15
  79.6 13.8 %collective-permute-done.17 = bf16[256,128]{1,0:T(8,128)(2,1)S(1)} collective-permute-done((bf16[256,128]{1,0:T(8,128)(2,1)S(1)}, bf16[256,128]{1,0:T(8,128)(2,1)S(1)}, u32[]{:S(2)}, u32[]{:S(2)}) %collective-permute-start.17) | collective-permute-done | bytes 65568 | tf_op jit(solution)/shard_map/ppermute | solution.py:15
  97.4 1.3 collective-permute-start.25
  98.7 13.5 %collective-permute-done.21 = bf16[256,128]{1,0:T(8,128)(2,1)S(1)} collective-permute-done((bf16[256,128]{1,0:T(8,128)(2,1)S(1)}, bf16[256,128]{1,0:T(8,128)(2,1)S(1)}, u32[]{:S(2)}, u32[]{:S(2)}) %collective-permute-start.21) | collective-permute-done | bytes 65568 | tf_op jit(solution)/shard_map/ppermute | solution.py:15
  113.5 1.3 collective-permute-start.27
  118.8 5.8 %collective-permute-done.26 = bf16[256,128]{1,0:T(8,128)(2,1)S(1)} collective-permute-done((bf16[256,128]{1,0:T(8,128)(2,1)S(1)}, bf16[256,128]{1,0:T(8,128)(2,1)S(1)}, u32[]{:S(2)}, u32[]{:S(2)}) %collective-permute-start.26) | collective-permute-done | bytes 65568 | tf_op jit(solution)/shard_map/ppermute | solution.py:15
  126.0 2.6 collective-permute-done.28
  128.6 2.1 collective-permute-done.29
  131.4 65.5 %conditional.3 = (bf16[256,3584]{1,0:T(8,128)(2,1)}, bf16[256,512]{1,0:T(8,128)(2,1)S(1)}) conditional(s32[]{:T(128)} %convert_element_type.108, () %tuple.41, (pred[256]{0:T(512)(128)(4,1)S(1)}, s32[]{:T(128)}, s32[256]{0:T(256)S(1)}, s32[96]{0:T(128)S(1)}, bf16[1,256,512]{2,1,0:T(8,128)(2,1)S(1)}, /*index=5*/s32[256]{0:T(256)S(1)}, ...), branch_computations={%region_0.0_spmd, %region_1.6_spmd} | conditional | flops 1077428864 | bytes 14901551 | solution.py:131
  132.6 59.4 %while.26 = (s32[]{:T(128)}, f32[1,4,256,128]{3,2,1,0:T(8,128)S(1)}, f32[1,4,256]{2,1,0:T(4,128)S(1)}, f32[1,4,256]{2,1,0:T(4,128)S(1)}, pred[17,256]{1,0:T(8,12...) while((s32[]{:T(128)}, ...), condition=%wide.region_5.5_spmd.clone, body=%wide.region_2.4_spmd.clone.sunk | while | flops 137369600 | bytes 4917157 | solution.py:116
  192.3 4.4 fusion.50
  196.9 3.8 copy.95
  200.8 59.6 %reduce-scatter.4.cloned.1.call-done = bf16[896,256]{1,0:T(8,128)(2,1)} async-done(((bf16[3584,256]{1,0:T(8,128)(2,1)}), bf16[896,256]{1,0:T(8,128)(2,1)}) %reduce-scatter.4.cloned.1.call-update) | async-done | bytes 458768
  261.8 1.8 collective-permute-start.32
  263.6 1.4 collective-permute-done.32
  266.7 35.9 %all-gather.4.cloned.1.call-done = bf16[256,3584]{1,0:T(8,128)(2,1)} async-done(((bf16[256,896]{1,0:T(8,128)(2,1)}), bf16[256,3584]{1,0:T(8,128)(2,1)}) %all-gather.4.cloned.1.call-update) | async-done | bytes 1835024 | tf_op jit(solution)/shard_map/all_gather | solution.py:138
  303.5 58.5 %all_gather.14 = bf16[96,1,4]{2,1,0:T(2,128)(2,1)S(1)} all-gather(bf16[1,1,4]{2,1,0:T(2,128)(2,1)S(1)} %fusion.54), channel_id=1, replica_groups=mesh['ctx'=96,'section'=2,'tp'=4] {'ctx'}, dimensions={0}, use_global_device_ids=true | all-gather | bytes 776 | tf_op jit(solution)/shard_map/all_gather | solution.py:21
  362.0 99.3 %all-gather.6.cloned.1.call-done = bf16[96,128,4,128]{3,1,2,0:T(8,128)(2,1)} async-done(((bf16[1,128,4,128]{3,1,2,0:T(8,128)(2,1)}), bf16[96,128,4,128]{3,1,2,0:T(8,128)(2,1)}) %all-gather.6.cloned.1.call-update) | async-done | bytes 12582928 | tf_op jit(solution)/shard_map/all_gather | solution.py:21
  461.4 114.6 %while.27 = (s32[]{:T(128)}, f32[1,128,4,128]{3,2,1,0:T(4,128)S(1)}, s32[]{:T(128)}, bf16[96,1,4]{2,1,0:T(2,128)(2,1)S(1)}, bf16[96,1,128,4,128]{4,2,3,0,1:T(8,128)(2,1)}, /*index=5*/s32[]{:T(128)}, s32[]{:T(128)}, s32[]{:T(128)}) while((s32[]{:T(128)}, f32[1,128,4,128]{3,2,1,0:T(4,128)S(1)}, s32[]{:T(128)}, ...), condition=%wide.region_13.14_spmd, body=%wide.region_12.13_spmd.sunk | while | flops 196617 | bytes 917679 | solution.py:35
  (582 shorter events, 229.4 us)
Async XLA Ops:
  7.2 253.2 %reduce-scatter.4.cloned.1.call-start = ((), (), s32[]{:S(2)}) async-start(), calls=%async_computation.3 | async-start | bytes 2293760
  7.2 15.3 %collective-permute-start = (bf16[256,128]{1,0:T(8,128)(2,1)}, bf16[256,128]{1,0:T(8,128)(2,1)S(1)}, u32[]{:S(2)}, u32[]{:S(2)}) collective-permute-start(bf16[256,128]{1,0:T(8,128)(2,1)} %bitcast.257), channel_id=1, source_target_pairs={{0,128},{8,136},{16,144},{24,152},{32,160},{40,168},{48,176},{56,1... | collective-permute-start | bytes 196616 | tf_op jit(solution)/shard_map/ppermute | solution.py:15
  8.5 27.5 %collective-permute-start.1 = (bf16[256,128]{1,0:T(8,128)(2,1)}, bf16[256,128]{1,0:T(8,128)(2,1)S(1)}, u32[]{:S(2)}, u32[]{:S(2)}) collective-permute-start(bf16[256,128]{1,0:T(8,128)(2,1)} %bitcast.258), channel_id=1, source_target_pairs={{0,120},{8,128},{16,136},{24,144},{32,152},{40,160},{48,168},{56,1... | collective-permute-start | bytes 196616 | tf_op jit(solution)/shard_map/ppermute | solution.py:15
  9.8 28.2 %collective-permute-start.2 = (bf16[256,128]{1,0:T(8,128)(2,1)}, bf16[256,128]{1,0:T(8,128)(2,1)S(1)}, u32[]{:S(2)}, u32[]{:S(2)}) collective-permute-start(bf16[256,128]{1,0:T(8,128)(2,1)} %bitcast.259), channel_id=1, source_target_pairs={{0,112},{8,120},{16,128},{24,136},{32,144},{40,152},{48,160},{56,1... | collective-permute-start | bytes 196616 | tf_op jit(solution)/shard_map/ppermute | solution.py:15
  11.1 28.8 %collective-permute-start.3 = (bf16[256,128]{1,0:T(8,128)(2,1)}, bf16[256,128]{1,0:T(8,128)(2,1)S(1)}, u32[]{:S(2)}, u32[]{:S(2)}) collective-permute-start(bf16[256,128]{1,0:T(8,128)(2,1)} %bitcast.260), channel_id=1, source_target_pairs={{0,104},{8,112},{16,120},{24,128},{32,136},{40,144},{48,152},{56,1... | collective-permute-start | bytes 196616 | tf_op jit(solution)/shard_map/ppermute | solution.py:15
  12.4 29.4 %collective-permute-start.4 = (bf16[256,128]{1,0:T(8,128)(2,1)}, bf16[256,128]{1,0:T(8,128)(2,1)S(1)}, u32[]{:S(2)}, u32[]{:S(2)}) collective-permute-start(bf16[256,128]{1,0:T(8,128)(2,1)} %bitcast.261), channel_id=1, source_target_pairs={{0,96},{8,104},{16,112},{24,120},{32,128},{40,136},{48,144},{56,15... | collective-permute-start | bytes 196616 | tf_op jit(solution)/shard_map/ppermute | solution.py:15
  46.0 14.0 %collective-permute-start.11 = (bf16[256,128]{1,0:T(8,128)(2,1)}, bf16[256,128]{1,0:T(8,128)(2,1)S(1)}, u32[]{:S(2)}, u32[]{:S(2)}) collective-permute-start(bf16[256,128]{1,0:T(8,128)(2,1)} %bitcast.268), channel_id=1, source_target_pairs={{0,40},{8,48},{16,56},{24,64},{32,72},{40,80},{48,88},{56,96},{64,... | collective-permute-start | bytes 196616 | tf_op jit(solution)/shard_map/ppermute | solution.py:15
  51.0 22.6 %collective-permute-start.13 = (bf16[256,128]{1,0:T(8,128)(2,1)S(1)}, bf16[256,128]{1,0:T(8,128)(2,1)S(1)}, u32[]{:S(2)}, u32[]{:S(2)}) collective-permute-start(bf16[256,128]{1,0:T(8,128)(2,1)S(1)} %bitcast.270), channel_id=1, source_target_pairs={{0,24},{8,32},{16,40},{24,48},{32,56},{40,64},{48,72},{56,80},{64,... | collective-permute-start | bytes 196616 | tf_op jit(solution)/shard_map/ppermute | solution.py:15
  54.7 21.2 %collective-permute-start.14 = (bf16[256,128]{1,0:T(8,128)(2,1)S(1)}, bf16[256,128]{1,0:T(8,128)(2,1)S(1)}, u32[]{:S(2)}, u32[]{:S(2)}) collective-permute-start(bf16[256,128]{1,0:T(8,128)(2,1)S(1)} %bitcast.271), channel_id=1, source_target_pairs={{0,16},{8,24},{16,32},{24,40},{32,48},{40,56},{48,64},{56,72},{64,... | collective-permute-start | bytes 196616 | tf_op jit(solution)/shard_map/ppermute | solution.py:15
  56.6 21.1 %collective-permute-start.15 = (bf16[256,128]{1,0:T(8,128)(2,1)S(1)}, bf16[256,128]{1,0:T(8,128)(2,1)S(1)}, u32[]{:S(2)}, u32[]{:S(2)}) collective-permute-start(bf16[256,128]{1,0:T(8,128)(2,1)S(1)} %bitcast.272), channel_id=1, source_target_pairs={{0,8},{8,16},{16,24},{24,32},{32,40},{40,48},{48,56},{56,64},{64,7... | collective-permute-start | bytes 196616 | tf_op jit(solution)/shard_map/ppermute | solution.py:15
  60.0 33.4 %collective-permute-start.17 = (bf16[256,128]{1,0:T(8,128)(2,1)S(1)}, bf16[256,128]{1,0:T(8,128)(2,1)S(1)}, u32[]{:S(2)}, u32[]{:S(2)}) collective-permute-start(bf16[256,128]{1,0:T(8,128)(2,1)S(1)} %copy-done.8), channel_id=1, source_target_pairs={{0,120},{8,128},{16,136},{24,144},{32,152},{40,160},{48,168},{56,1... | collective-permute-start | bytes 196616 | tf_op jit(solution)/shard_map/ppermute | solution.py:15
  61.9 32.8 %collective-permute-start.18 = (bf16[256,128]{1,0:T(8,128)(2,1)S(1)}, bf16[256,128]{1,0:T(8,128)(2,1)S(1)}, u32[]{:S(2)}, u32[]{:S(2)}) collective-permute-start(bf16[256,128]{1,0:T(8,128)(2,1)S(1)} %copy-done.8), channel_id=1, source_target_pairs={{0,112},{8,120},{16,128},{24,136},{32,144},{40,152},{48,160},{56,1... | collective-permute-start | bytes 196616 | tf_op jit(solution)/shard_map/ppermute | solution.py:15
  73.5 22.5 %collective-permute-start.19 = (bf16[256,128]{1,0:T(8,128)(2,1)S(1)}, bf16[256,128]{1,0:T(8,128)(2,1)S(1)}, u32[]{:S(2)}, u32[]{:S(2)}) collective-permute-start(bf16[256,128]{1,0:T(8,128)(2,1)S(1)} %copy-done.8), channel_id=1, source_target_pairs={{0,104},{8,112},{16,120},{24,128},{32,136},{40,144},{48,152},{56,1... | collective-permute-start | bytes 196616 | tf_op jit(solution)/shard_map/ppermute | solution.py:15
  75.8 21.6 %collective-permute-start.20 = (bf16[256,128]{1,0:T(8,128)(2,1)S(1)}, bf16[256,128]{1,0:T(8,128)(2,1)S(1)}, u32[]{:S(2)}, u32[]{:S(2)}) collective-permute-start(bf16[256,128]{1,0:T(8,128)(2,1)S(1)} %copy-done.8), channel_id=1, source_target_pairs={{0,96},{8,104},{16,112},{24,120},{32,128},{40,136},{48,144},{56,15... | collective-permute-start | bytes 196616 | tf_op jit(solution)/shard_map/ppermute | solution.py:15
  77.7 34.4 %collective-permute-start.21 = (bf16[256,128]{1,0:T(8,128)(2,1)S(1)}, bf16[256,128]{1,0:T(8,128)(2,1)S(1)}, u32[]{:S(2)}, u32[]{:S(2)}) collective-permute-start(bf16[256,128]{1,0:T(8,128)(2,1)S(1)} %copy-done.8), channel_id=1, source_target_pairs={{0,88},{8,96},{16,104},{24,112},{32,120},{40,128},{48,136},{56,144... | collective-permute-start | bytes 196616 | tf_op jit(solution)/shard_map/ppermute | solution.py:15
  93.4 20.1 %collective-permute-start.22 = (bf16[256,128]{1,0:T(8,128)(2,1)S(1)}, bf16[256,128]{1,0:T(8,128)(2,1)S(1)}, u32[]{:S(2)}, u32[]{:S(2)}) collective-permute-start(bf16[256,128]{1,0:T(8,128)(2,1)S(1)} %copy-done.8), channel_id=1, source_target_pairs={{0,80},{8,88},{16,96},{24,104},{32,112},{40,120},{48,128},{56,136}... | collective-permute-start | bytes 196616 | tf_op jit(solution)/shard_map/ppermute | solution.py:15
  94.7 20.1 %collective-permute-start.23 = (bf16[256,128]{1,0:T(8,128)(2,1)S(1)}, bf16[256,128]{1,0:T(8,128)(2,1)S(1)}, u32[]{:S(2)}, u32[]{:S(2)}) collective-permute-start(bf16[256,128]{1,0:T(8,128)(2,1)S(1)} %copy-done.8), channel_id=1, source_target_pairs={{0,72},{8,80},{16,88},{24,96},{32,104},{40,112},{48,120},{56,128},... | collective-permute-start | bytes 196616 | tf_op jit(solution)/shard_map/ppermute | solution.py:15
  96.0 20.1 %collective-permute-start.24 = (bf16[256,128]{1,0:T(8,128)(2,1)S(1)}, bf16[256,128]{1,0:T(8,128)(2,1)S(1)}, u32[]{:S(2)}, u32[]{:S(2)}) collective-permute-start(bf16[256,128]{1,0:T(8,128)(2,1)S(1)} %copy-done.8), channel_id=1, source_target_pairs={{0,64},{8,72},{16,80},{24,88},{32,96},{40,104},{48,112},{56,120},{... | collective-permute-start | bytes 196616 | tf_op jit(solution)/shard_map/ppermute | solution.py:15
  97.4 20.1 %collective-permute-start.25 = (bf16[256,128]{1,0:T(8,128)(2,1)S(1)}, bf16[256,128]{1,0:T(8,128)(2,1)S(1)}, u32[]{:S(2)}, u32[]{:S(2)}) collective-permute-start(bf16[256,128]{1,0:T(8,128)(2,1)S(1)} %copy-done.8), channel_id=1, source_target_pairs={{0,56},{8,64},{16,72},{24,80},{32,88},{40,96},{48,104},{56,112},{6... | collective-permute-start | bytes 196616 | tf_op jit(solution)/shard_map/ppermute | solution.py:15
  114.8 13.8 %collective-permute-start.28 = (bf16[256,128]{1,0:T(8,128)(2,1)S(1)}, bf16[256,128]{1,0:T(8,128)(2,1)S(1)}, u32[]{:S(2)}, u32[]{:S(2)}) collective-permute-start(bf16[256,128]{1,0:T(8,128)(2,1)S(1)} %copy-done.8), channel_id=1, source_target_pairs={{0,32},{8,40},{16,48},{24,56},{32,64},{40,72},{48,80},{56,88},{64,... | collective-permute-start | bytes 196616 | tf_op jit(solution)/shard_map/ppermute | solution.py:15
  116.1 14.5 %collective-permute-start.29 = (bf16[256,128]{1,0:T(8,128)(2,1)S(1)}, bf16[256,128]{1,0:T(8,128)(2,1)S(1)}, u32[]{:S(2)}, u32[]{:S(2)}) collective-permute-start(bf16[256,128]{1,0:T(8,128)(2,1)S(1)} %copy-done.8), channel_id=1, source_target_pairs={{0,24},{8,32},{16,40},{24,48},{32,56},{40,64},{48,72},{56,80},{64,... | collective-permute-start | bytes 196616 | tf_op jit(solution)/shard_map/ppermute | solution.py:15
  117.5 13.2 %collective-permute-start.30 = (bf16[256,128]{1,0:T(8,128)(2,1)S(1)}, bf16[256,128]{1,0:T(8,128)(2,1)S(1)}, u32[]{:S(2)}, u32[]{:S(2)}) collective-permute-start(bf16[256,128]{1,0:T(8,128)(2,1)S(1)} %copy-done.8), channel_id=1, source_target_pairs={{0,16},{8,24},{16,32},{24,40},{32,48},{40,56},{48,64},{56,72},{64,... | collective-permute-start | bytes 196616 | tf_op jit(solution)/shard_map/ppermute | solution.py:15
  200.7 101.9 %all-gather.4.cloned.1.call-start = ((), (), s32[]{:S(2)}) async-start(), calls=%async_computation.1 | async-start | bytes 2293760 | tf_op jit(solution)/shard_map/all_gather | solution.py:138
  265.9 195.4 %all-gather.6.cloned.1.call-start = ((), (), s32[]{:S(2)}) async-start(), calls=%async_computation.2 | async-start | bytes 12713984 | tf_op jit(solution)/shard_map/all_gather | solution.py:21
  (21 other events, 698.5 us)
Sparse Core Ops, SparseCore 0:
  200.9 59.4 reduce-scatter.3
  266.0 36.5 all-gather.3
  306.9 154.3 all-gather.5
where the time goes:
time: 587 us; the launch traced here: 583 us
  waiting for transfers between devices  266 us (45%)
  local copies, waits for them, and re-layouts  119 us (20%)
  blocking collectives  58.5 us (10%)
  other arithmetic  46.8 us (8%)
  starting transfers between devices  43.1 us (7%)
  matrix products  32.9 us (6%)
  between operations  14.4 us (2%)
    all_gather x1, waiting for transfers between devices, entering(): lax.all_gather(a.astype(kind), axis)  99.3 us
    dynamic_slice x95, local copies, waits for them, and re-layouts, one(): lax.dynamic_index_in_dim(a, step, 0, False).astype(own.dtype)  87.3 us
    ppermute x33, waiting for transfers between devices, passed_along(): return lax.ppermute(x, axis, pairs)  71 us
    unnamed x4, waiting for transfers between devices  59.6 us
    all_gather x1, blocking collectives, entering(): lax.all_gather(a.astype(kind), axis)  58.5 us
    ppermute x33, starting transfers between devices, passed_along(): return lax.ppermute(x, axis, pairs)  43 us
    all_gather x1, waiting for transfers between devices, body(): lax.all_gather(local_activations, 'tp', axis=1, tiled=True)  35.9 us
    add x95, other arithmetic, chain(): previous_entry[1] * jnp.exp(latter[0])[:, None, :, None] + latter[1]  23.9 us
  transfers between devices with their start and end apart: 36, of which 18 were waited for; matrix products, arithmetic and copies ran while one was open for 2% of the time, Pallas kernels for 0%

commit v1 on v0

v1 whole, which is shorter than its diff:
```python
import math

import jax
import jax.numpy as jnp
from jax import lax
from jax.sharding import PartitionSpec as P

HEAD = 128
WINDOW = 4096


def passed_along(x, by, section):
    shards = lax.axis_size("ctx")
    sections = lax.axis_size("section")
    pairs = [
        (i * sections + section, (i + by) * sections + section)
        for i in range(shards)
        if 0 <= i + by < shards
    ]
    return lax.ppermute(x, ("ctx", "section"), pairs)


def body(
    residual,
    queries,
    keys,
    window_values,
    mixing,
    norm_gain,
    log_decay,
    spike_counts,
    thresholds,
    lengths,
):
    section_index = lax.axis_index("section")
    shard_index = lax.axis_index("ctx")
    shards = lax.axis_size("ctx")
    row_count = keys.shape[1]
    head_size = HEAD
    key_heads = keys.shape[2] // head_size
    query_head_rows = queries.shape[2] // head_size
    group_size = query_head_rows // key_heads
    span_blocks = WINDOW // row_count
    feature_count = mixing.shape[2]
    scale = 1.0 / math.sqrt(head_size)
    positions = jnp.arange(row_count, dtype=jnp.int32)
    valid_rows = positions < lengths[shard_index]
    own_keys = keys[0]

    query_rows = queries[0].reshape(row_count, key_heads, group_size, head_size)
    base_distance = positions[:, None] - positions[None, :]
    running = jnp.zeros((key_heads, group_size, row_count, head_size), jnp.float32)
    totals = jnp.zeros((key_heads, group_size, row_count), jnp.float32)
    best = jnp.full((key_heads, group_size, row_count), -1e30, jnp.float32)
    for distance_blocks in range(span_blocks + 1):
        if distance_blocks == 0:
            key_block, value_block = own_keys, window_values
        else:
            key_block, value_block = passed_along(
                (own_keys, window_values), distance_blocks, 0
            )
        source = shard_index - distance_blocks
        key_valid = (source >= 0) & (positions < lengths[jnp.maximum(source, 0)])
        scores = (
            jnp.einsum(
                "rgjd,kgd->gjrk",
                query_rows,
                key_block.reshape(row_count, key_heads, head_size),
                preferred_element_type=jnp.float32,
            )
            * scale
        )
        distance = base_distance + distance_blocks * row_count
        allowed = key_valid[None, :] & (distance >= 0) & (distance < WINDOW)
        scores = jnp.where(allowed, scores, -1e30)
        new_best = jnp.maximum(best, jnp.max(scores, axis=-1))
        factor = jnp.exp(best - new_best)
        weights = jnp.where(allowed, jnp.exp(scores - new_best[..., None]), 0.0)
        blended = jnp.einsum(
            "gjrk,kgd->gjrd",
            weights.astype(jnp.bfloat16),
            value_block.reshape(row_count, key_heads, head_size),
            preferred_element_type=jnp.float32,
        )
        running = running * factor[..., None] + blended
        totals = totals * factor + jnp.sum(weights, axis=-1)
        best = new_best
    attention = running / jnp.maximum(totals, 1.0)[..., None]
    attention = attention.transpose(2, 0, 1, 3).reshape(row_count, query_head_rows * head_size)
    attention = jnp.where(valid_rows[:, None], attention, 0.0).astype(jnp.bfloat16)
    projected = jnp.dot(attention, mixing[0], preferred_element_type=jnp.float32)

    share = lax.psum_scatter(
        projected.astype(jnp.bfloat16), "tp", scatter_dimension=1, tiled=True
    ).astype(jnp.float32)
    own_hidden = (share + residual.astype(jnp.float32)).astype(jnp.bfloat16)
    moved_share = lax.ppermute(own_hidden, "section", [(0, 1)])
    local_activations = jnp.where(section_index == 0, own_hidden, moved_share)
    complete_hidden_matrix = lax.all_gather(local_activations, "tp", axis=1, tiled=True)

    masked_keys = jnp.where(valid_rows[:, None], own_keys, jnp.zeros_like(own_keys)).reshape(
        row_count, key_heads, head_size
    )
    wide_keys = masked_keys.astype(jnp.float32)
    decays = log_decay * valid_rows[:, None].astype(jnp.float32)
    wide = complete_hidden_matrix.astype(jnp.float32)
    normed = (
        wide
        * lax.rsqrt(jnp.mean(wide * wide, axis=-1, keepdims=True) + 1e-05)
        * norm_gain.astype(jnp.float32)
    ).astype(jnp.bfloat16)
    payload_vectors = lax.dot_general(
        normed, mixing[0], (((1,), (1,)), ((), ())), preferred_element_type=jnp.float32
    ).astype(jnp.bfloat16)
    cumulated = jnp.cumsum(decays, axis=0).reshape(row_count, key_heads, group_size)
    value_rows = payload_vectors.astype(jnp.float32).reshape(
        row_count, key_heads, group_size, head_size
    )
    fresh_state = jnp.einsum(
        "sgd,sgje->gdje",
        wide_keys,
        value_rows * jnp.exp(cumulated[-1] - cumulated)[..., None],
        precision=lax.Precision.HIGHEST,
    )

    def chain(previous_entry, latter):
        return (
            previous_entry[0] + latter[0],
            previous_entry[1] * jnp.exp(latter[0])[:, None, :, None] + latter[1],
        )

    entry = passed_along((cumulated[-1], fresh_state), 1, 1)
    reach = 1
    while reach < shards:
        entry = chain(passed_along(entry, reach, 1), entry)
        reach *= 2
    incoming = entry[1]

    query_narrow = queries[0].reshape(row_count, key_heads, group_size, head_size)
    query_wide = query_narrow.astype(jnp.float32)
    products = jnp.einsum(
        "rgjd,sgd->gjrs", query_narrow, masked_keys, preferred_element_type=jnp.float32
    )
    ordered = cumulated.transpose(1, 2, 0)
    spread = ordered[..., :, None] - ordered[..., None, :]
    triangle = positions[:, None] >= positions[None, :]
    damping = jnp.where(triangle, jnp.exp(jnp.minimum(spread, 0.0)), 0.0)
    intra = jnp.einsum(
        "gjrs,sgje->rgje", products * damping, value_rows, precision=lax.Precision.HIGHEST
    )
    inter = (
        jnp.einsum("rgjd,gdje->rgje", query_wide, incoming, precision=lax.Precision.HIGHEST)
        * jnp.exp(cumulated)[..., None]
    )
    mixed = (inter + intra).reshape(row_count, query_head_rows, head_size)
    scaled = mixed * lax.rsqrt(jnp.mean(mixed * mixed, axis=-1, keepdims=True) + 1e-05)
    gating = spike_counts.astype(jnp.float32).reshape(
        row_count, query_head_rows, head_size
    ) * thresholds.reshape(query_head_rows, head_size)
    gated = jnp.where(
        valid_rows[:, None],
        (scaled * gating).reshape(row_count, query_head_rows * head_size),
        0.0,
    ).astype(jnp.bfloat16)
    head_outputs = jnp.where(section_index == 0, attention, gated)[None]
    return (head_outputs, local_activations)


def solution(mesh):
    return jax.shard_map(
        body,
        mesh=mesh,
        in_specs=(
            P("ctx", "tp"),
            P("section", "ctx", "tp"),
            P("section", "ctx", "tp"),
            P("ctx", "tp"),
            P("section", "tp", None),
            P(),
            P("ctx", "tp"),
            P("ctx", "tp"),
            P("tp"),
            P(),
        ),
        out_specs=(P("section", "ctx", "tp"), P("ctx", "tp")),
        check_vma=False,
    )
```

time: 587 us -> 399 us (0.68)
  the two profiles are of different devices: /device:TPU:760 before, /device:TPU:113 now
where the time goes in v1:
time: 399 us; the launch traced here: 397 us
  waiting for transfers between devices  252 us (63%)
  starting transfers between devices  76.6 us (19%)
  other arithmetic  23.7 us (6%)
  matrix products  19.5 us (5%)
  between operations  15.5 us (4%)
  local copies, waits for them, and re-layouts  10.6 us (3%)
    unnamed x3, waiting for transfers between devices  137 us
    ppermute x47, waiting for transfers between devices, passed_along(): return lax.ppermute(x, ('ctx', 'section'), pairs)  78.8 us
    ppermute x47, starting transfers between devices, passed_along(): return lax.ppermute(x, ('ctx', 'section'), pairs)  75.3 us
    all_gather x1, waiting for transfers between devices, body(): lax.all_gather(local_activations, 'tp', axis=1, tiled=True)  33.5 us
    and x17, other arithmetic, body(): key_valid = (source >= 0) & (positions < lengths[jnp.maximum(source, 0)])  10.7 us
  transfers between devices with their start and end apart: 50, of which 15 were waited for; matrix products, arithmetic and copies ran while one was open for 9% of the time, Pallas kernels for 0%

profile of v1, /device:TPU:113, one launch (start us, length us, event | category | flops | bytes accessed | tf_op | source)
XLA Modules:
  0.0 397.5 jit_solution(3135882620331585518)
XLA Ops:
  67.8 136.9 %reduce-scatter.4.cloned.1.call-done = bf16[896,256]{1,0:T(8,128)(2,1)} async-done(((bf16[3584,256]{1,0:T(8,128)(2,1)}), bf16[896,256]{1,0:T(8,128)(2,1)}) %reduce-scatter.4.cloned.1.call-update) | async-done | bytes 458768
  207.4 2.4 collective-permute-done.32
  213.4 33.5 %all-gather.2.cloned.1.call-done = bf16[256,3584]{1,0:T(8,128)(2,1)} async-done(((bf16[256,896]{1,0:T(8,128)(2,1)}), bf16[256,3584]{1,0:T(8,128)(2,1)}) %all-gather.2.cloned.1.call-update) | async-done | bytes 1835024 | tf_op jit(solution)/shard_map/all_gather | solution.py:99
  248.8 3.8 fusion.79
  253.3 3.3 collective-permute-start.33
  256.6 3.8 collective-permute-done.33
  260.4 3.3 collective-permute-start.34
  263.7 3.9 collective-permute-start.35
  270.0 3.3 collective-permute-start.37
  273.4 3.1 collective-permute-done.37
  276.7 3.1 collective-permute-start.36
  279.8 7.2 %collective-permute-done.36 = f32[1,128,4,128]{3,1,2,0:T(8,128)S(1)} collective-permute-done((f32[1,128,4,128]{3,1,2,0:T(8,128)S(1)}, f32[1,128,4,128]{3,1,2,0:T(8,128)S(1)}, u32[]{:S(2)}, u32[]{:S(2)}) %collective-permute-start.36) | collective-permute-done | bytes 262176 | tf_op jit(solution)/shard_map/ppermute | solution.py:20
  287.0 3.3 collective-permute-start.38
  290.4 4.0 collective-permute-start.39
  294.3 3.5 collective-permute-done.39
  300.4 6.7 %collective-permute-start.40 = (f32[1,128,4,128]{3,1,2,0:T(8,128)S(1)}, f32[1,128,4,128]{3,1,2,0:T(8,128)S(1)}, u32[]{:S(2)}, u32[]{:S(2)}) collective-permute-start(f32[1,128,4,128]{3,1,2,0:T(8,128)S(1)} %multiply_add_fusion.3), channel_id=1, source_target_pairs={{4,68},{12,76},{20,84},{28,92},{36,100},{44,108},{52,116},{60,124}... | collective-permute-start | bytes 786440 | tf_op jit(solution)/shard_map/ppermute | solution.py:20
  307.1 6.2 %collective-permute-start.41 = (f32[1,4]{0,1:T(4,128)S(1)}, f32[1,4]{0,1:T(4,128)S(1)}, u32[]{:S(2)}, u32[]{:S(2)}) collective-permute-start(f32[1,4]{0,1:T(4,128)S(1)} %get-tuple-element.9), channel_id=1, source_target_pairs={{4,36},{12,44},{20,52},{28,60},{36,68},{44,76},{52,84},{60,92},{68... | collective-permute-start | bytes 56 | tf_op jit(solution)/shard_map/ppermute | solution.py:20
  313.3 2.9 collective-permute-done.41
  316.4 9.0 %collective-permute-start.42 = (f32[1,128,4,128]{3,1,2,0:T(8,128)S(1)}, f32[1,128,4,128]{3,1,2,0:T(8,128)S(1)}, u32[]{:S(2)}, u32[]{:S(2)}) collective-permute-start(f32[1,128,4,128]{3,1,2,0:T(8,128)S(1)} %multiply_add_fusion.2), channel_id=1, source_target_pairs={{4,132},{12,140},{20,148},{28,156},{36,164},{44,172},{52,180},{60,... | collective-permute-start | bytes 786440 | tf_op jit(solution)/shard_map/ppermute | solution.py:20
  327.4 8.4 %collective-permute-done.43 = f32[1,4]{0,1:T(4,128)S(1)} collective-permute-done((f32[1,4]{0,1:T(4,128)S(1)}, f32[1,4]{0,1:T(4,128)S(1)}, u32[]{:S(2)}, u32[]{:S(2)}) %collective-permute-start.43) | collective-permute-done | bytes 48 | tf_op jit(solution)/shard_map/ppermute | solution.py:20
  335.9 6.8 %collective-permute-done.42 = f32[1,128,4,128]{3,1,2,0:T(8,128)S(1)} collective-permute-done((f32[1,128,4,128]{3,1,2,0:T(8,128)S(1)}, f32[1,128,4,128]{3,1,2,0:T(8,128)S(1)}, u32[]{:S(2)}, u32[]{:S(2)}) %collective-permute-start.42) | collective-permute-done | bytes 262176 | tf_op jit(solution)/shard_map/ppermute | solution.py:20
  346.0 8.5 %collective-permute-done.45 = f32[1,4]{0,1:T(4,128)S(1)} collective-permute-done((f32[1,4]{0,1:T(4,128)S(1)}, f32[1,4]{0,1:T(4,128)S(1)}, u32[]{:S(2)}, u32[]{:S(2)}) %collective-permute-start.45) | collective-permute-done | bytes 48 | tf_op jit(solution)/shard_map/ppermute | solution.py:20
  355.8 10.9 %collective-permute-done.47 = f32[1,4]{0,1:T(4,128)S(1)} collective-permute-done((f32[1,4]{0,1:T(4,128)S(1)}, f32[1,4]{0,1:T(4,128)S(1)}, u32[]{:S(2)}, u32[]{:S(2)}) %collective-permute-start.47) | collective-permute-done | bytes 48 | tf_op jit(solution)/shard_map/ppermute | solution.py:20
  369.5 19.0 %collective-permute-done.46 = f32[1,128,4,128]{3,1,2,0:T(8,128)S(1)} collective-permute-done((f32[1,128,4,128]{3,1,2,0:T(8,128)S(1)}, f32[1,128,4,128]{3,1,2,0:T(8,128)S(1)}, u32[]{:S(2)}, u32[]{:S(2)}) %collective-permute-start.46) | collective-permute-done | bytes 262176 | tf_op jit(solution)/shard_map/ppermute | solution.py:20
  (225 shorter events, 85.4 us)
Async XLA Ops:
  7.2 197.5 %reduce-scatter.4.cloned.1.call-start = ((), (), s32[]{:S(2)}) async-start(), calls=%async_computation.2 | async-start | bytes 2293760
  7.2 21.9 %collective-permute-start.2 = (bf16[256,128]{1,0:T(8,128)(2,1)}, bf16[256,128]{1,0:T(8,128)(2,1)S(1)}, u32[]{:S(2)}, u32[]{:S(2)}) collective-permute-start(bf16[256,128]{1,0:T(8,128)(2,1)} %bitcast.434), channel_id=1, source_target_pairs={{0,16},{8,24},{16,32},{24,40},{32,48},{40,56},{48,64},{56,72},{64,... | collective-permute-start | bytes 196616 | tf_op jit(solution)/shard_map/ppermute | solution.py:20
  7.9 22.3 %collective-permute-start = (bf16[256,128]{1,0:T(8,128)(2,1)}, bf16[256,128]{1,0:T(8,128)(2,1)S(1)}, u32[]{:S(2)}, u32[]{:S(2)}) collective-permute-start(bf16[256,128]{1,0:T(8,128)(2,1)} %bitcast.435), channel_id=1, source_target_pairs={{0,8},{8,16},{16,24},{24,32},{32,40},{40,48},{48,56},{56,64},{64,7... | collective-permute-start | bytes 196616 | tf_op jit(solution)/shard_map/ppermute | solution.py:20
  8.6 22.6 %collective-permute-start.28 = (bf16[256,128]{1,0:T(8,128)(2,1)}, bf16[256,128]{1,0:T(8,128)(2,1)S(1)}, u32[]{:S(2)}, u32[]{:S(2)}) collective-permute-start(bf16[256,128]{1,0:T(8,128)(2,1)} %bitcast.436), channel_id=1, source_target_pairs={{0,120},{8,128},{16,136},{24,144},{32,152},{40,160},{48,168},{56,1... | collective-permute-start | bytes 196616 | tf_op jit(solution)/shard_map/ppermute | solution.py:20
  9.2 23.0 %collective-permute-start.26 = (bf16[256,128]{1,0:T(8,128)(2,1)}, bf16[256,128]{1,0:T(8,128)(2,1)S(1)}, u32[]{:S(2)}, u32[]{:S(2)}) collective-permute-start(bf16[256,128]{1,0:T(8,128)(2,1)} %bitcast.437), channel_id=1, source_target_pairs={{0,112},{8,120},{16,128},{24,136},{32,144},{40,152},{48,160},{56,1... | collective-permute-start | bytes 196616 | tf_op jit(solution)/shard_map/ppermute | solution.py:20
  9.9 23.3 %collective-permute-start.24 = (bf16[256,128]{1,0:T(8,128)(2,1)}, bf16[256,128]{1,0:T(8,128)(2,1)S(1)}, u32[]{:S(2)}, u32[]{:S(2)}) collective-permute-start(bf16[256,128]{1,0:T(8,128)(2,1)} %bitcast.438), channel_id=1, source_target_pairs={{0,104},{8,112},{16,120},{24,128},{32,136},{40,144},{48,152},{56,1... | collective-permute-start | bytes 196616 | tf_op jit(solution)/shard_map/ppermute | solution.py:20
  40.3 9.0 %collective-permute-start.25 = (bf16[256,128]{0,1:T(8,128)(2,1)S(1)}, bf16[256,128]{0,1:T(8,128)(2,1)S(1)}, u32[]{:S(2)}, u32[]{:S(2)}) collective-permute-start(bf16[256,128]{0,1:T(8,128)(2,1)S(1)} %copy.209), channel_id=1, source_target_pairs={{0,104},{8,112},{16,120},{24,128},{32,136},{40,144},{48,152},{56,1... | collective-permute-start | bytes 196616 | tf_op jit(solution)/shard_map/ppermute | solution.py:20
  41.3 9.0 %collective-permute-start.23 = (bf16[256,128]{0,1:T(8,128)(2,1)S(1)}, bf16[256,128]{0,1:T(8,128)(2,1)S(1)}, u32[]{:S(2)}, u32[]{:S(2)}) collective-permute-start(bf16[256,128]{0,1:T(8,128)(2,1)S(1)} %copy.209), channel_id=1, source_target_pairs={{0,96},{8,104},{16,112},{24,120},{32,128},{40,136},{48,144},{56,15... | collective-permute-start | bytes 196616 | tf_op jit(solution)/shard_map/ppermute | solution.py:20
  42.3 9.2 %collective-permute-start.21 = (bf16[256,128]{0,1:T(8,128)(2,1)S(1)}, bf16[256,128]{0,1:T(8,128)(2,1)S(1)}, u32[]{:S(2)}, u32[]{:S(2)}) collective-permute-start(bf16[256,128]{0,1:T(8,128)(2,1)S(1)} %copy.209), channel_id=1, source_target_pairs={{0,88},{8,96},{16,104},{24,112},{32,120},{40,128},{48,136},{56,144... | collective-permute-start | bytes 196616 | tf_op jit(solution)/shard_map/ppermute | solution.py:20
  43.3 9.2 %collective-permute-start.19 = (bf16[256,128]{0,1:T(8,128)(2,1)S(1)}, bf16[256,128]{0,1:T(8,128)(2,1)S(1)}, u32[]{:S(2)}, u32[]{:S(2)}) collective-permute-start(bf16[256,128]{0,1:T(8,128)(2,1)S(1)} %copy.209), channel_id=1, source_target_pairs={{0,80},{8,88},{16,96},{24,104},{32,112},{40,120},{48,128},{56,136}... | collective-permute-start | bytes 196616 | tf_op jit(solution)/shard_map/ppermute | solution.py:20
  44.3 9.3 %collective-permute-start.17 = (bf16[256,128]{0,1:T(8,128)(2,1)S(1)}, bf16[256,128]{0,1:T(8,128)(2,1)S(1)}, u32[]{:S(2)}, u32[]{:S(2)}) collective-permute-start(bf16[256,128]{0,1:T(8,128)(2,1)S(1)} %copy.209), channel_id=1, source_target_pairs={{0,72},{8,80},{16,88},{24,96},{32,104},{40,112},{48,120},{56,128},... | collective-permute-start | bytes 196616 | tf_op jit(solution)/shard_map/ppermute | solution.py:20
  67.7 179.1 %all-gather.2.cloned.1.call-start = ((), (), s32[]{:S(2)}) async-start(), calls=%async_computation.1 | async-start | bytes 2293760 | tf_op jit(solution)/shard_map/all_gather | solution.py:99
  260.4 16.2 %collective-permute-start.34 = (f32[1,128,4,128]{3,1,2,0:T(8,128)S(1)}, f32[1,128,4,128]{3,1,2,0:T(8,128)S(1)}, u32[]{:S(2)}, u32[]{:S(2)}) collective-permute-start(f32[1,128,4,128]{3,1,2,0:T(8,128)S(1)} %collective-permute-done.33), channel_id=1, source_target_pairs={{4,12},{12,20},{20,28},{28,36},{36,44},{44,52},{52,60},{60,68},{68... | collective-permute-start | bytes 786440 | tf_op jit(solution)/shard_map/ppermute | solution.py:20
  276.7 10.2 %collective-permute-start.36 = (f32[1,128,4,128]{3,1,2,0:T(8,128)S(1)}, f32[1,128,4,128]{3,1,2,0:T(8,128)S(1)}, u32[]{:S(2)}, u32[]{:S(2)}) collective-permute-start(f32[1,128,4,128]{3,1,2,0:T(8,128)S(1)} %multiply_add_fusion.5), channel_id=1, source_target_pairs={{4,20},{12,28},{20,36},{28,44},{36,52},{44,60},{52,68},{60,76},{68... | collective-permute-start | bytes 786440 | tf_op jit(solution)/shard_map/ppermute | solution.py:20
  287.0 13.3 %collective-permute-start.38 = (f32[1,128,4,128]{3,1,2,0:T(8,128)S(1)}, f32[1,128,4,128]{3,1,2,0:T(8,128)S(1)}, u32[]{:S(2)}, u32[]{:S(2)}) collective-permute-start(f32[1,128,4,128]{3,1,2,0:T(8,128)S(1)} %multiply_add_fusion.4), channel_id=1, source_target_pairs={{4,36},{12,44},{20,52},{28,60},{36,68},{44,76},{52,84},{60,92},{68... | collective-permute-start | bytes 786440 | tf_op jit(solution)/shard_map/ppermute | solution.py:20
  290.4 7.4 %collective-permute-start.39 = (f32[1,4]{0,1:T(4,128)S(1)}, f32[1,4]{0,1:T(4,128)S(1)}, u32[]{:S(2)}, u32[]{:S(2)}) collective-permute-start(f32[1,4]{0,1:T(4,128)S(1)} %get-tuple-element.11), channel_id=1, source_target_pairs={{4,20},{12,28},{20,36},{28,44},{36,52},{44,60},{52,68},{60,76},{68... | collective-permute-start | bytes 56 | tf_op jit(solution)/shard_map/ppermute | solution.py:20
  300.4 15.9 %collective-permute-start.40 = (f32[1,128,4,128]{3,1,2,0:T(8,128)S(1)}, f32[1,128,4,128]{3,1,2,0:T(8,128)S(1)}, u32[]{:S(2)}, u32[]{:S(2)}) collective-permute-start(f32[1,128,4,128]{3,1,2,0:T(8,128)S(1)} %multiply_add_fusion.3), channel_id=1, source_target_pairs={{4,68},{12,76},{20,84},{28,92},{36,100},{44,108},{52,116},{60,124}... | collective-permute-start | bytes 786440 | tf_op jit(solution)/shard_map/ppermute | solution.py:20
  307.1 9.1 %collective-permute-start.41 = (f32[1,4]{0,1:T(4,128)S(1)}, f32[1,4]{0,1:T(4,128)S(1)}, u32[]{:S(2)}, u32[]{:S(2)}) collective-permute-start(f32[1,4]{0,1:T(4,128)S(1)} %get-tuple-element.9), channel_id=1, source_target_pairs={{4,36},{12,44},{20,52},{28,60},{36,68},{44,76},{52,84},{60,92},{68... | collective-permute-start | bytes 56 | tf_op jit(solution)/shard_map/ppermute | solution.py:20
  316.4 26.2 %collective-permute-start.42 = (f32[1,128,4,128]{3,1,2,0:T(8,128)S(1)}, f32[1,128,4,128]{3,1,2,0:T(8,128)S(1)}, u32[]{:S(2)}, u32[]{:S(2)}) collective-permute-start(f32[1,128,4,128]{3,1,2,0:T(8,128)S(1)} %multiply_add_fusion.2), channel_id=1, source_target_pairs={{4,132},{12,140},{20,148},{28,156},{36,164},{44,172},{52,180},{60,... | collective-permute-start | bytes 786440 | tf_op jit(solution)/shard_map/ppermute | solution.py:20
  325.5 10.3 %collective-permute-start.43 = (f32[1,4]{0,1:T(4,128)S(1)}, f32[1,4]{0,1:T(4,128)S(1)}, u32[]{:S(2)}, u32[]{:S(2)}) collective-permute-start(f32[1,4]{0,1:T(4,128)S(1)} %get-tuple-element.7), channel_id=1, source_target_pairs={{4,68},{12,76},{20,84},{28,92},{36,100},{44,108},{52,116},{60,124}... | collective-permute-start | bytes 56 | tf_op jit(solution)/shard_map/ppermute | solution.py:20
  342.8 24.1 %collective-permute-start.44 = (f32[1,128,4,128]{3,1,2,0:T(8,128)S(1)}, f32[1,128,4,128]{3,1,2,0:T(8,128)S(1)}, u32[]{:S(2)}, u32[]{:S(2)}) collective-permute-start(f32[1,128,4,128]{3,1,2,0:T(8,128)S(1)} %multiply_add_fusion.1), channel_id=1, source_target_pairs={{4,260},{12,268},{20,276},{28,284},{36,292},{44,300},{52,308},{60,... | collective-permute-start | bytes 786440 | tf_op jit(solution)/shard_map/ppermute | solution.py:20
  344.1 10.4 %collective-permute-start.45 = (f32[1,4]{0,1:T(4,128)S(1)}, f32[1,4]{0,1:T(4,128)S(1)}, u32[]{:S(2)}, u32[]{:S(2)}) collective-permute-start(f32[1,4]{0,1:T(4,128)S(1)} %get-tuple-element.5), channel_id=1, source_target_pairs={{4,132},{12,140},{20,148},{28,156},{36,164},{44,172},{52,180},{60,... | collective-permute-start | bytes 56 | tf_op jit(solution)/shard_map/ppermute | solution.py:20
  354.5 12.2 %collective-permute-start.47 = (f32[1,4]{0,1:T(4,128)S(1)}, f32[1,4]{0,1:T(4,128)S(1)}, u32[]{:S(2)}, u32[]{:S(2)}) collective-permute-start(f32[1,4]{0,1:T(4,128)S(1)} %add.529), channel_id=1, source_target_pairs={{4,260},{12,268},{20,276},{28,284},{36,292},{44,300},{52,308},{60,... | collective-permute-start | bytes 56 | tf_op jit(solution)/shard_map/ppermute | solution.py:20
  367.0 21.5 %collective-permute-start.46 = (f32[1,128,4,128]{3,1,2,0:T(8,128)S(1)}, f32[1,128,4,128]{3,1,2,0:T(8,128)S(1)}, u32[]{:S(2)}, u32[]{:S(2)}) collective-permute-start(f32[1,128,4,128]{3,1,2,0:T(8,128)S(1)} %multiply_add_fusion), channel_id=1, source_target_pairs={{4,516},{12,524},{20,532},{28,540},{36,548},{44,556},{52,564},{60,... | collective-permute-start | bytes 786440 | tf_op jit(solution)/shard_map/ppermute | solution.py:20
  (34 other events, 624.7 us)
Sparse Core Ops, SparseCore 0:
  67.8 136.7 reduce-scatter.3
  210.7 36.0 all-gather.1

commit v2 on v1

--- a/solution.py
+++ b/solution.py
@@ -49,6 +49,8 @@
 
     query_rows = queries[0].reshape(row_count, key_heads, group_size, head_size)
     base_distance = positions[:, None] - positions[None, :]
+    key_width = own_keys.shape[1]
+    packed = jnp.concatenate([own_keys, window_values], axis=1)
     running = jnp.zeros((key_heads, group_size, row_count, head_size), jnp.float32)
     totals = jnp.zeros((key_heads, group_size, row_count), jnp.float32)
     best = jnp.full((key_heads, group_size, row_count), -1e30, jnp.float32)
@@ -56,9 +58,8 @@
         if distance_blocks == 0:
             key_block, value_block = own_keys, window_values
         else:
-            key_block, value_block = passed_along(
-                (own_keys, window_values), distance_blocks, 0
-            )
+            joined = passed_along(packed, distance_blocks, 0)
+            key_block, value_block = joined[:, :key_width], joined[:, key_width:]
         source = shard_index - distance_blocks
         key_valid = (source >= 0) & (positions < lengths[jnp.maximum(source, 0)])
         scores = (
@@ -90,13 +91,35 @@
     attention = jnp.where(valid_rows[:, None], attention, 0.0).astype(jnp.bfloat16)
     projected = jnp.dot(attention, mixing[0], preferred_element_type=jnp.float32)
 
-    share = lax.psum_scatter(
-        projected.astype(jnp.bfloat16), "tp", scatter_dimension=1, tiled=True
+    members = lax.axis_size("tp")
+    member = lax.axis_index("tp")
+    width = feature_count // members
+    terms = projected.astype(jnp.bfloat16)
+    summed = residual.astype(jnp.float32) + lax.dynamic_slice_in_dim(
+        terms, member * width, width, 1
     ).astype(jnp.float32)
-    own_hidden = (share + residual.astype(jnp.float32)).astype(jnp.bfloat16)
-    moved_share = lax.ppermute(own_hidden, "section", [(0, 1)])
-    local_activations = jnp.where(section_index == 0, own_hidden, moved_share)
-    complete_hidden_matrix = lax.all_gather(local_activations, "tp", axis=1, tiled=True)
+    for step in range(1, members):
+        target = (member + step) % members
+        sent = lax.dynamic_slice_in_dim(terms, target * width, width, 1)
+        pairs = [(m, (m + step) % members) for m in range(members)]
+        summed = summed + lax.ppermute(sent, ("section", "tp"), pairs).astype(jnp.float32)
+    own_hidden = summed.astype(jnp.bfloat16)
+    arrived = jnp.stack(
+        [
+            lax.ppermute(
+                own_hidden,
+                ("section", "tp"),
+                [(m, members + (m + step) % members) for m in range(members)],
+            )
+            for step in range(members)
+        ],
+        0,
+    )
+    local_activations = jnp.where(section_index == 0, own_hidden, arrived[0])
+    order = (member - jnp.arange(members, dtype=jnp.int32)) % members
+    complete_hidden_matrix = (
+        jnp.take(arrived, order, axis=0).transpose(1, 0, 2).reshape(row_count, feature_count)
+    )
 
     masked_keys = jnp.where(valid_rows[:, None], own_keys, jnp.zeros_like(own_keys)).reshape(
         row_count, key_heads, head_size
@@ -124,17 +147,22 @@
     )
 
     def chain(previous_entry, latter):
-        return (
-            previous_entry[0] + latter[0],
-            previous_entry[1] * jnp.exp(latter[0])[:, None, :, None] + latter[1],
+        latter_total = latter[:, :1]
+        return jnp.concatenate(
+            [
+                previous_entry[:, :1] + latter_total,
+                previous_entry[:, 1:] * jnp.exp(latter_total) + latter[:, 1:],
+            ],
+            axis=1,
         )
 
-    entry = passed_along((cumulated[-1], fresh_state), 1, 1)
+    total_rows = jnp.broadcast_to(cumulated[-1][:, None, :, None], (key_heads, 1, group_size, head_size))
+    entry = passed_along(jnp.concatenate([total_rows, fresh_state], axis=1), 1, 1)
     reach = 1
     while reach < shards:
         entry = chain(passed_along(entry, reach, 1), entry)
         reach *= 2
-    incoming = entry[1]
+    incoming = entry[:, 1:]
 
     query_narrow = queries[0].reshape(row_count, key_heads, group_size, head_size)
     query_wide = query_narrow.astype(jnp.float32)

time: 399 us -> 301 us (0.75)
  the two profiles are of different devices: /device:TPU:113 before, /device:TPU:1 now
where the time goes in v2:
time: 301 us; the launch traced here: 299 us
  waiting for transfers between devices  148 us (49%)
  starting transfers between devices  89.1 us (30%)
  other arithmetic  29.9 us (10%)
  matrix products  17.9 us (6%)
  local copies, waits for them, and re-layouts  12.9 us (4%)
    ppermute x4, waiting for transfers between devices, body(): lax.ppermute(own_hidden, ('section', 'tp'), [(m, members + (m + step) % m...  102 us
    ppermute x24, starting transfers between devices, passed_along(): return lax.ppermute(x, ('ctx', 'section'), pairs)  79.6 us
    ppermute x24, waiting for transfers between devices, passed_along(): return lax.ppermute(x, ('ctx', 'section'), pairs)  45.8 us
    and x17, other arithmetic, body(): key_valid = (source >= 0) & (positions < lengths[jnp.maximum(source, 0)])  10.7 us
    dot_general x17, matrix products, body(): jnp.einsum('gjrk,kgd->gjrd', weights.astype(jnp.bfloat16), value_block.re...  6.19 us
  transfers between devices with their start and end apart: 31, of which 12 were waited for; matrix products, arithmetic and copies ran while one was open for 9% of the time, Pallas kernels for 0%

profile of v2, /device:TPU:1, one launch (start us, length us, event | category | flops | bytes accessed | tf_op | source)
XLA Modules:
  0.0 299.3 jit_solution(173746888840165902)
XLA Ops:
  5.0 2.1 fusion.372
  62.6 87.2 %collective-permute-done.19 = bf16[256,896]{1,0:T(8,128)(2,1)S(1)} collective-permute-done((bf16[256,896]{1,0:T(8,128)(2,1)S(1)}, bf16[256,896]{1,0:T(8,128)(2,1)S(1)}, u32[]{:S(2)}, u32[]{:S(2)}) %collective-permute-start.19) | collective-permute-done | bytes 458784 | tf_op jit(solution)/shard_map/ppermute | solution.py:109
  149.8 8.5 %collective-permute-done.20 = bf16[256,896]{1,0:T(8,128)(2,1)S(1)} collective-permute-done((bf16[256,896]{1,0:T(8,128)(2,1)S(1)}, bf16[256,896]{1,0:T(8,128)(2,1)S(1)}, u32[]{:S(2)}, u32[]{:S(2)}) %collective-permute-start.20) | collective-permute-done | bytes 458784 | tf_op jit(solution)/shard_map/ppermute | solution.py:109
  158.3 5.3 %collective-permute-done.21 = bf16[256,896]{1,0:T(8,128)(2,1)S(1)} collective-permute-done((bf16[256,896]{1,0:T(8,128)(2,1)S(1)}, bf16[256,896]{1,0:T(8,128)(2,1)S(1)}, u32[]{:S(2)}, u32[]{:S(2)}) %collective-permute-start.21) | collective-permute-done | bytes 458784 | tf_op jit(solution)/shard_map/ppermute | solution.py:109
  165.8 2.4 gather_fusion
  168.8 1.9 fusion.6
  170.7 2.7 copy.326
  173.5 3.2 %fusion.77 = bf16[256,512]{1,0:T(8,128)(2,1)S(1)} fusion(bf16[256,3584]{0,1:T(8,128)(2,1)S(1)} %bitcast.444, bf16[1,512,3584]{2,1,0:T(8,128)(2,1)} %param.14), kind=kOutput, calls=%fused_computation.105 | convolution fusion | flops 939655168 | bytes 5767168 | tf_op jit(solution)/shard_map/dot_general | solution.py:135
  177.6 2.4 collective-permute-start.23
  180.0 3.5 %collective-permute-done.23 = f32[1,129,4,128]{3,1,2,0:T(8,128)S(1)} collective-permute-done((f32[1,129,4,128]{3,1,2,0:T(8,128)S(1)}, f32[1,129,4,128]{3,1,2,0:T(8,128)S(1)}, u32[]{:S(2)}, u32[]{:S(2)}) %collective-permute-start.23) | collective-permute-done | bytes 264224 | tf_op jit(solution)/shard_map/ppermute | solution.py:20
  183.5 3.8 %collective-permute-start.24 = (f32[1,129,4,128]{3,1,2,0:T(8,128)S(1)}, f32[1,129,4,128]{3,1,2,0:T(8,128)S(1)}, u32[]{:S(2)}, u32[]{:S(2)}) collective-permute-start(f32[1,129,4,128]{3,1,2,0:T(8,128)S(1)} %collective-permute-done.23), channel_id=1, source_target_pairs={{4,12},{12,20},{20,28},{28,36},{36,44},{44,52},{52,60},{60,68},{68... | collective-permute-start | bytes 792584 | tf_op jit(solution)/shard_map/ppermute | solution.py:20
  187.3 3.5 %collective-permute-done.24 = f32[1,129,4,128]{3,1,2,0:T(8,128)S(1)} collective-permute-done((f32[1,129,4,128]{3,1,2,0:T(8,128)S(1)}, f32[1,129,4,128]{3,1,2,0:T(8,128)S(1)}, u32[]{:S(2)}, u32[]{:S(2)}) %collective-permute-start.24) | collective-permute-done | bytes 264224 | tf_op jit(solution)/shard_map/ppermute | solution.py:20
  190.9 5.8 %collective-permute-start.25 = (f32[1,129,4,128]{3,1,2,0:T(8,128)S(1)}, f32[1,129,4,128]{3,1,2,0:T(8,128)S(1)}, u32[]{:S(2)}, u32[]{:S(2)}) collective-permute-start(f32[1,129,4,128]{3,1,2,0:T(8,128)S(1)} %pad_maximum_fusion.2), channel_id=1, source_target_pairs={{4,20},{12,28},{20,36},{28,44},{36,52},{44,60},{52,68},{60,76},{68... | collective-permute-start | bytes 792584 | tf_op jit(solution)/shard_map/ppermute | solution.py:20
  196.7 3.5 %collective-permute-done.25 = f32[1,129,4,128]{3,1,2,0:T(8,128)S(1)} collective-permute-done((f32[1,129,4,128]{3,1,2,0:T(8,128)S(1)}, f32[1,129,4,128]{3,1,2,0:T(8,128)S(1)}, u32[]{:S(2)}, u32[]{:S(2)}) %collective-permute-start.25) | collective-permute-done | bytes 264224 | tf_op jit(solution)/shard_map/ppermute | solution.py:20
  200.3 12.6 %collective-permute-start.26 = (f32[1,129,4,128]{3,1,2,0:T(8,128)S(1)}, f32[1,129,4,128]{3,1,2,0:T(8,128)S(1)}, u32[]{:S(2)}, u32[]{:S(2)}) collective-permute-start(f32[1,129,4,128]{3,1,2,0:T(8,128)S(1)} %pad_maximum_fusion.3), channel_id=1, source_target_pairs={{4,36},{12,44},{20,52},{28,60},{36,68},{44,76},{52,84},{60,92},{68... | collective-permute-start | bytes 792584 | tf_op jit(solution)/shard_map/ppermute | solution.py:20
  212.9 11.6 %collective-permute-done.26 = f32[1,129,4,128]{3,1,2,0:T(8,128)S(1)} collective-permute-done((f32[1,129,4,128]{3,1,2,0:T(8,128)S(1)}, f32[1,129,4,128]{3,1,2,0:T(8,128)S(1)}, u32[]{:S(2)}, u32[]{:S(2)}) %collective-permute-start.26) | collective-permute-done | bytes 264224 | tf_op jit(solution)/shard_map/ppermute | solution.py:20
  224.7 6.9 %collective-permute-start.27 = (f32[1,129,4,128]{3,1,2,0:T(8,128)S(1)}, f32[1,129,4,128]{3,1,2,0:T(8,128)S(1)}, u32[]{:S(2)}, u32[]{:S(2)}) collective-permute-start(f32[1,129,4,128]{3,1,2,0:T(8,128)S(1)} %pad_maximum_fusion.4), channel_id=1, source_target_pairs={{4,68},{12,76},{20,84},{28,92},{36,100},{44,108},{52,116},{60,124}... | collective-permute-start | bytes 792584 | tf_op jit(solution)/shard_map/ppermute | solution.py:20
  231.6 4.3 %collective-permute-done.27 = f32[1,129,4,128]{3,1,2,0:T(8,128)S(1)} collective-permute-done((f32[1,129,4,128]{3,1,2,0:T(8,128)S(1)}, f32[1,129,4,128]{3,1,2,0:T(8,128)S(1)}, u32[]{:S(2)}, u32[]{:S(2)}) %collective-permute-start.27) | collective-permute-done | bytes 264224 | tf_op jit(solution)/shard_map/ppermute | solution.py:20
  236.0 12.6 %collective-permute-start.28 = (f32[1,129,4,128]{3,1,2,0:T(8,128)S(1)}, f32[1,129,4,128]{3,1,2,0:T(8,128)S(1)}, u32[]{:S(2)}, u32[]{:S(2)}) collective-permute-start(f32[1,129,4,128]{3,1,2,0:T(8,128)S(1)} %pad_maximum_fusion.5), channel_id=1, source_target_pairs={{4,132},{12,140},{20,148},{28,156},{36,164},{44,172},{52,180},{60,... | collective-permute-start | bytes 792584 | tf_op jit(solution)/shard_map/ppermute | solution.py:20
  248.6 8.5 %collective-permute-done.28 = f32[1,129,4,128]{3,1,2,0:T(8,128)S(1)} collective-permute-done((f32[1,129,4,128]{3,1,2,0:T(8,128)S(1)}, f32[1,129,4,128]{3,1,2,0:T(8,128)S(1)}, u32[]{:S(2)}, u32[]{:S(2)}) %collective-permute-start.28) | collective-permute-done | bytes 264224 | tf_op jit(solution)/shard_map/ppermute | solution.py:20
  257.9 10.2 %collective-permute-start.29 = (f32[1,129,4,128]{3,1,2,0:T(8,128)}, f32[1,129,4,128]{3,1,2,0:T(8,128)}, u32[]{:S(2)}, u32[]{:S(2)}) collective-permute-start(f32[1,129,4,128]{3,1,2,0:T(8,128)} %pad_maximum_fusion.6), channel_id=1, source_target_pairs={{4,260},{12,268},{20,276},{28,284},{36,292},{44,300},{52,308},{60,... | collective-permute-start | bytes 792584 | tf_op jit(solution)/shard_map/ppermute | solution.py:20
  268.8 2.4 collective-permute-done.29
  273.0 14.4 %collective-permute-start.30 = (f32[1,129,4,128]{3,1,2,0:T(8,128)S(1)}, f32[1,129,4,128]{3,1,2,0:T(8,128)S(1)}, u32[]{:S(2)}, u32[]{:S(2)}) collective-permute-start(f32[1,129,4,128]{3,1,2,0:T(8,128)S(1)} %pad_maximum_fusion.7), channel_id=1, source_target_pairs={{4,516},{12,524},{20,532},{28,540},{36,548},{44,556},{52,564},{60,... | collective-permute-start | bytes 792584 | tf_op jit(solution)/shard_map/ppermute | solution.py:20
  288.7 8.5 %collective-permute-done.30 = f32[1,129,4,128]{3,1,2,0:T(8,128)S(1)} collective-permute-done((f32[1,129,4,128]{3,1,2,0:T(8,128)S(1)}, f32[1,129,4,128]{3,1,2,0:T(8,128)S(1)}, u32[]{:S(2)}, u32[]{:S(2)}) %collective-permute-start.30) | collective-permute-done | bytes 264224 | tf_op jit(solution)/shard_map/ppermute | solution.py:20
  (211 shorter events, 69.5 us)
Async XLA Ops:
  1.6 20.9 %collective-permute-start.2 = (bf16[256,256]{1,0:T(8,128)(2,1)S(1)}, bf16[256,256]{1,0:T(8,128)(2,1)S(1)}, u32[]{:S(2)}, u32[]{:S(2)}) collective-permute-start(bf16[256,256]{1,0:T(8,128)(2,1)S(1)} %pad_maximum_fusion.8), channel_id=1, source_target_pairs={{0,24},{8,32},{16,40},{24,48},{32,56},{40,64},{48,72},{56,80},{64,... | collective-permute-start | bytes 393224 | tf_op jit(solution)/shard_map/ppermute | solution.py:20
  2.2 21.3 %collective-permute-start.1 = (bf16[256,256]{1,0:T(8,128)(2,1)S(1)}, bf16[256,256]{1,0:T(8,128)(2,1)S(1)}, u32[]{:S(2)}, u32[]{:S(2)}) collective-permute-start(bf16[256,256]{1,0:T(8,128)(2,1)S(1)} %pad_maximum_fusion.8), channel_id=1, source_target_pairs={{0,16},{8,24},{16,32},{24,40},{32,48},{40,56},{48,64},{56,72},{64,... | collective-permute-start | bytes 393224 | tf_op jit(solution)/shard_map/ppermute | solution.py:20
  2.9 21.6 %collective-permute-start = (bf16[256,256]{1,0:T(8,128)(2,1)S(1)}, bf16[256,256]{1,0:T(8,128)(2,1)S(1)}, u32[]{:S(2)}, u32[]{:S(2)}) collective-permute-start(bf16[256,256]{1,0:T(8,128)(2,1)S(1)} %pad_maximum_fusion.8), channel_id=1, source_target_pairs={{0,8},{8,16},{16,24},{24,32},{32,40},{40,48},{48,56},{56,64},{64,7... | collective-permute-start | bytes 393224 | tf_op jit(solution)/shard_map/ppermute | solution.py:20
  3.6 22.0 %collective-permute-start.14 = (bf16[256,256]{1,0:T(8,128)(2,1)S(1)}, bf16[256,256]{1,0:T(8,128)(2,1)S(1)}, u32[]{:S(2)}, u32[]{:S(2)}) collective-permute-start(bf16[256,256]{1,0:T(8,128)(2,1)S(1)} %pad_maximum_fusion.8), channel_id=1, source_target_pairs={{0,120},{8,128},{16,136},{24,144},{32,152},{40,160},{48,168},{56,1... | collective-permute-start | bytes 393224 | tf_op jit(solution)/shard_map/ppermute | solution.py:20
  4.3 22.3 %collective-permute-start.13 = (bf16[256,256]{1,0:T(8,128)(2,1)S(1)}, bf16[256,256]{1,0:T(8,128)(2,1)S(1)}, u32[]{:S(2)}, u32[]{:S(2)}) collective-permute-start(bf16[256,256]{1,0:T(8,128)(2,1)S(1)} %pad_maximum_fusion.8), channel_id=1, source_target_pairs={{0,112},{8,120},{16,128},{24,136},{32,144},{40,152},{48,160},{56,1... | collective-permute-start | bytes 393224 | tf_op jit(solution)/shard_map/ppermute | solution.py:20
  22.5 5.1 %collective-permute-start.12 = (bf16[256,256]{1,0:T(8,128)(2,1)S(1)}, bf16[256,256]{1,0:T(8,128)(2,1)S(1)}, u32[]{:S(2)}, u32[]{:S(2)}) collective-permute-start(bf16[256,256]{1,0:T(8,128)(2,1)S(1)} %pad_maximum_fusion.8), channel_id=1, source_target_pairs={{0,104},{8,112},{16,120},{24,128},{32,136},{40,144},{48,152},{56,1... | collective-permute-start | bytes 393224 | tf_op jit(solution)/shard_map/ppermute | solution.py:20
  24.6 5.1 %collective-permute-start.10 = (bf16[256,256]{1,0:T(8,128)(2,1)S(1)}, bf16[256,256]{1,0:T(8,128)(2,1)S(1)}, u32[]{:S(2)}, u32[]{:S(2)}) collective-permute-start(bf16[256,256]{1,0:T(8,128)(2,1)S(1)} %pad_maximum_fusion.8), channel_id=1, source_target_pairs={{0,88},{8,96},{16,104},{24,112},{32,120},{40,128},{48,136},{56,144... | collective-permute-start | bytes 393224 | tf_op jit(solution)/shard_map/ppermute | solution.py:20
  25.6 5.1 %collective-permute-start.9 = (bf16[256,256]{1,0:T(8,128)(2,1)S(1)}, bf16[256,256]{1,0:T(8,128)(2,1)S(1)}, u32[]{:S(2)}, u32[]{:S(2)}) collective-permute-start(bf16[256,256]{1,0:T(8,128)(2,1)S(1)} %pad_maximum_fusion.8), channel_id=1, source_target_pairs={{0,80},{8,88},{16,96},{24,104},{32,112},{40,120},{48,128},{56,136}... | collective-permute-start | bytes 393224 | tf_op jit(solution)/shard_map/ppermute | solution.py:20
  26.6 5.1 %collective-permute-start.8 = (bf16[256,256]{1,0:T(8,128)(2,1)S(1)}, bf16[256,256]{1,0:T(8,128)(2,1)S(1)}, u32[]{:S(2)}, u32[]{:S(2)}) collective-permute-start(bf16[256,256]{1,0:T(8,128)(2,1)S(1)} %pad_maximum_fusion.8), channel_id=1, source_target_pairs={{0,72},{8,80},{16,88},{24,96},{32,104},{40,112},{48,120},{56,128},... | collective-permute-start | bytes 393224 | tf_op jit(solution)/shard_map/ppermute | solution.py:20
  27.6 5.1 %collective-permute-start.7 = (bf16[256,256]{1,0:T(8,128)(2,1)S(1)}, bf16[256,256]{1,0:T(8,128)(2,1)S(1)}, u32[]{:S(2)}, u32[]{:S(2)}) collective-permute-start(bf16[256,256]{1,0:T(8,128)(2,1)S(1)} %pad_maximum_fusion.8), channel_id=1, source_target_pairs={{0,64},{8,72},{16,80},{24,88},{32,96},{40,104},{48,112},{56,120},{... | collective-permute-start | bytes 393224 | tf_op jit(solution)/shard_map/ppermute | solution.py:20
  28.6 5.3 %collective-permute-start.6 = (bf16[256,256]{1,0:T(8,128)(2,1)S(1)}, bf16[256,256]{1,0:T(8,128)(2,1)S(1)}, u32[]{:S(2)}, u32[]{:S(2)}) collective-permute-start(bf16[256,256]{1,0:T(8,128)(2,1)S(1)} %pad_maximum_fusion.8), channel_id=1, source_target_pairs={{0,56},{8,64},{16,72},{24,80},{32,88},{40,96},{48,104},{56,112},{6... | collective-permute-start | bytes 393224 | tf_op jit(solution)/shard_map/ppermute | solution.py:20
  48.7 6.2 %collective-permute-start.16 = (bf16[256,896]{1,0:T(8,128)(2,1)}, bf16[256,896]{1,0:T(8,128)(2,1)}, u32[]{:S(2)}, u32[]{:S(2)}) collective-permute-start(bf16[256,896]{1,0:T(8,128)(2,1)} %get-tuple-element.47), channel_id=1, source_target_pairs={{0,1},{1,2},{2,3},{3,0},{8,9},{9,10},{10,11},{11,8},{16,17},{17,18... | collective-permute-start | bytes 1376264 | tf_op jit(solution)/shard_map/ppermute | solution.py:105
  56.5 93.3 %collective-permute-start.19 = (bf16[256,896]{1,0:T(8,128)(2,1)S(1)}, bf16[256,896]{1,0:T(8,128)(2,1)S(1)}, u32[]{:S(2)}, u32[]{:S(2)}) collective-permute-start(bf16[256,896]{1,0:T(8,128)(2,1)S(1)} %add_convert_fusion), channel_id=1, source_target_pairs={{0,4},{1,5},{2,6},{3,7},{8,12},{9,13},{10,14},{11,15},{16,20},{17,... | collective-permute-start | bytes 1376264 | tf_op jit(solution)/shard_map/ppermute | solution.py:109
  57.8 100.5 %collective-permute-start.20 = (bf16[256,896]{1,0:T(8,128)(2,1)S(1)}, bf16[256,896]{1,0:T(8,128)(2,1)S(1)}, u32[]{:S(2)}, u32[]{:S(2)}) collective-permute-start(bf16[256,896]{1,0:T(8,128)(2,1)S(1)} %add_convert_fusion), channel_id=1, source_target_pairs={{0,5},{1,6},{2,7},{3,4},{8,13},{9,14},{10,15},{11,12},{16,21},{17,... | collective-permute-start | bytes 1376264 | tf_op jit(solution)/shard_map/ppermute | solution.py:109
  59.1 104.5 %collective-permute-start.21 = (bf16[256,896]{1,0:T(8,128)(2,1)S(1)}, bf16[256,896]{1,0:T(8,128)(2,1)S(1)}, u32[]{:S(2)}, u32[]{:S(2)}) collective-permute-start(bf16[256,896]{1,0:T(8,128)(2,1)S(1)} %add_convert_fusion), channel_id=1, source_target_pairs={{0,6},{1,7},{2,4},{3,5},{8,14},{9,15},{10,12},{11,13},{16,22},{17,... | collective-permute-start | bytes 1376264 | tf_op jit(solution)/shard_map/ppermute | solution.py:109
  60.4 103.9 %collective-permute-start.22 = (bf16[256,896]{1,0:T(8,128)(2,1)S(1)}, bf16[256,896]{1,0:T(8,128)(2,1)S(1)}, u32[]{:S(2)}, u32[]{:S(2)}) collective-permute-start(bf16[256,896]{1,0:T(8,128)(2,1)S(1)} %add_convert_fusion), channel_id=1, source_target_pairs={{0,7},{1,4},{2,5},{3,6},{8,15},{9,12},{10,13},{11,14},{16,23},{17,... | collective-permute-start | bytes 1376264 | tf_op jit(solution)/shard_map/ppermute | solution.py:109
  177.6 5.9 %collective-permute-start.23 = (f32[1,129,4,128]{3,1,2,0:T(8,128)S(1)}, f32[1,129,4,128]{3,1,2,0:T(8,128)S(1)}, u32[]{:S(2)}, u32[]{:S(2)}) collective-permute-start(f32[1,129,4,128]{3,1,2,0:T(8,128)S(1)} %pad_maximum_fusion.1), channel_id=1, source_target_pairs={{4,12},{12,20},{20,28},{28,36},{36,44},{44,52},{52,60},{60,68},{68... | collective-permute-start | bytes 792584 | tf_op jit(solution)/shard_map/ppermute | solution.py:20
  183.5 7.3 %collective-permute-start.24 = (f32[1,129,4,128]{3,1,2,0:T(8,128)S(1)}, f32[1,129,4,128]{3,1,2,0:T(8,128)S(1)}, u32[]{:S(2)}, u32[]{:S(2)}) collective-permute-start(f32[1,129,4,128]{3,1,2,0:T(8,128)S(1)} %collective-permute-done.23), channel_id=1, source_target_pairs={{4,12},{12,20},{20,28},{28,36},{36,44},{44,52},{52,60},{60,68},{68... | collective-permute-start | bytes 792584 | tf_op jit(solution)/shard_map/ppermute | solution.py:20
  190.9 9.3 %collective-permute-start.25 = (f32[1,129,4,128]{3,1,2,0:T(8,128)S(1)}, f32[1,129,4,128]{3,1,2,0:T(8,128)S(1)}, u32[]{:S(2)}, u32[]{:S(2)}) collective-permute-start(f32[1,129,4,128]{3,1,2,0:T(8,128)S(1)} %pad_maximum_fusion.2), channel_id=1, source_target_pairs={{4,20},{12,28},{20,36},{28,44},{36,52},{44,60},{52,68},{60,76},{68... | collective-permute-start | bytes 792584 | tf_op jit(solution)/shard_map/ppermute | solution.py:20
  200.3 24.3 %collective-permute-start.26 = (f32[1,129,4,128]{3,1,2,0:T(8,128)S(1)}, f32[1,129,4,128]{3,1,2,0:T(8,128)S(1)}, u32[]{:S(2)}, u32[]{:S(2)}) collective-permute-start(f32[1,129,4,128]{3,1,2,0:T(8,128)S(1)} %pad_maximum_fusion.3), channel_id=1, source_target_pairs={{4,36},{12,44},{20,52},{28,60},{36,68},{44,76},{52,84},{60,92},{68... | collective-permute-start | bytes 792584 | tf_op jit(solution)/shard_map/ppermute | solution.py:20
  224.7 11.2 %collective-permute-start.27 = (f32[1,129,4,128]{3,1,2,0:T(8,128)S(1)}, f32[1,129,4,128]{3,1,2,0:T(8,128)S(1)}, u32[]{:S(2)}, u32[]{:S(2)}) collective-permute-start(f32[1,129,4,128]{3,1,2,0:T(8,128)S(1)} %pad_maximum_fusion.4), channel_id=1, source_target_pairs={{4,68},{12,76},{20,84},{28,92},{36,100},{44,108},{52,116},{60,124}... | collective-permute-start | bytes 792584 | tf_op jit(solution)/shard_map/ppermute | solution.py:20
  236.0 21.1 %collective-permute-start.28 = (f32[1,129,4,128]{3,1,2,0:T(8,128)S(1)}, f32[1,129,4,128]{3,1,2,0:T(8,128)S(1)}, u32[]{:S(2)}, u32[]{:S(2)}) collective-permute-start(f32[1,129,4,128]{3,1,2,0:T(8,128)S(1)} %pad_maximum_fusion.5), channel_id=1, source_target_pairs={{4,132},{12,140},{20,148},{28,156},{36,164},{44,172},{52,180},{60,... | collective-permute-start | bytes 792584 | tf_op jit(solution)/shard_map/ppermute | solution.py:20
  257.9 13.3 %collective-permute-start.29 = (f32[1,129,4,128]{3,1,2,0:T(8,128)}, f32[1,129,4,128]{3,1,2,0:T(8,128)}, u32[]{:S(2)}, u32[]{:S(2)}) collective-permute-start(f32[1,129,4,128]{3,1,2,0:T(8,128)} %pad_maximum_fusion.6), channel_id=1, source_target_pairs={{4,260},{12,268},{20,276},{28,284},{36,292},{44,300},{52,308},{60,... | collective-permute-start | bytes 792584 | tf_op jit(solution)/shard_map/ppermute | solution.py:20
  273.0 24.3 %collective-permute-start.30 = (f32[1,129,4,128]{3,1,2,0:T(8,128)S(1)}, f32[1,129,4,128]{3,1,2,0:T(8,128)S(1)}, u32[]{:S(2)}, u32[]{:S(2)}) collective-permute-start(f32[1,129,4,128]{3,1,2,0:T(8,128)S(1)} %pad_maximum_fusion.7), channel_id=1, source_target_pairs={{4,516},{12,524},{20,532},{28,540},{36,548},{44,556},{52,564},{60,... | collective-permute-start | bytes 792584 | tf_op jit(solution)/shard_map/ppermute | solution.py:20
  (21 other events, 336.9 us)

commit v3 on v2

--- a/solution.py
+++ b/solution.py
@@ -156,11 +156,19 @@
             axis=1,
         )
 
+    def sent_along(entry, by):
+        total = entry[:, :1]
+        high = total.astype(jnp.bfloat16)
+        low = (total - high.astype(jnp.float32)).astype(jnp.bfloat16)
+        narrow = jnp.concatenate([high, low, entry[:, 1:].astype(jnp.bfloat16)], axis=1)
+        moved = passed_along(narrow, by, 1).astype(jnp.float32)
+        return jnp.concatenate([moved[:, :1] + moved[:, 1:2], moved[:, 2:]], axis=1)
+
     total_rows = jnp.broadcast_to(cumulated[-1][:, None, :, None], (key_heads, 1, group_size, head_size))
-    entry = passed_along(jnp.concatenate([total_rows, fresh_state], axis=1), 1, 1)
+    entry = sent_along(jnp.concatenate([total_rows, fresh_state], axis=1), 1)
     reach = 1
     while reach < shards:
-        entry = chain(passed_along(entry, reach, 1), entry)
+        entry = chain(sent_along(entry, reach), entry)
         reach *= 2
     incoming = entry[:, 1:]
 

time: 301 us -> 270 us (0.90)
  waiting for transfers between devices: 148 us -> 119 us
  starting transfers between devices: 89.1 us -> 85.7 us
    ppermute x24, waiting for transfers between devices: 45.8 us -> 19.9 us  [passed_along(): return lax.ppermute(x, ('ctx', 'section'), pairs)]
    ppermute x24, starting transfers between devices: 79.6 us -> 76.1 us  [passed_along(): return lax.ppermute(x, ('ctx', 'section'), pairs)]
  transfers between devices with their start and end apart: 31 -> 31, of which waited for: 12 -> 12; matrix products, arithmetic and copies ran while one was open for 9% -> 10% of each run, Pallas kernels for 0% -> 0%
where the time goes in v3:
time: 270 us; the launch traced here: 267 us
  waiting for transfers between devices  119 us (44%)
  starting transfers between devices  85.7 us (32%)
  other arithmetic  28.7 us (11%)
  matrix products  17.9 us (7%)
  local copies, waits for them, and re-layouts  13 us (5%)
    ppermute x4, waiting for transfers between devices, body(): lax.ppermute(own_hidden, ('section', 'tp'), [(m, members + (m + step) % m...  99.2 us
    ppermute x24, starting transfers between devices, passed_along(): return lax.ppermute(x, ('ctx', 'section'), pairs)  76.1 us
    ppermute x24, waiting for transfers between devices, passed_along(): return lax.ppermute(x, ('ctx', 'section'), pairs)  19.9 us
    and x17, other arithmetic, body(): key_valid = (source >= 0) & (positions < lengths[jnp.maximum(source, 0)])  10.7 us
    dot_general x17, matrix products, body(): jnp.einsum('gjrk,kgd->gjrd', weights.astype(jnp.bfloat16), value_block.re...  6.24 us
    dot_general x17, matrix products, body(): jnp.einsum('rgjd,kgd->gjrk', query_rows, key_block.reshape(row_count, key...  5.54 us
  transfers between devices with their start and end apart: 31, of which 12 were waited for; matrix products, arithmetic and copies ran while one was open for 10% of the time, Pallas kernels for 0%

profile of v3, /device:TPU:1, one launch (start us, length us, event | category | flops | bytes accessed | tf_op | source)
XLA Modules:
  0.0 266.7 jit_solution(380295316617190582)
XLA Ops:
  5.0 2.1 fusion.404
  50.2 1.6 collective-permute-start.16
  55.1 1.6 add_convert_fusion
  62.1 84.7 %collective-permute-done.19 = bf16[256,896]{1,0:T(8,128)(2,1)S(1)} collective-permute-done((bf16[256,896]{1,0:T(8,128)(2,1)S(1)}, bf16[256,896]{1,0:T(8,128)(2,1)S(1)}, u32[]{:S(2)}, u32[]{:S(2)}) %collective-permute-start.19) | collective-permute-done | bytes 458784 | tf_op jit(solution)/shard_map/ppermute | solution.py:109
  146.8 8.5 %collective-permute-done.20 = bf16[256,896]{1,0:T(8,128)(2,1)S(1)} collective-permute-done((bf16[256,896]{1,0:T(8,128)(2,1)S(1)}, bf16[256,896]{1,0:T(8,128)(2,1)S(1)}, u32[]{:S(2)}, u32[]{:S(2)}) %collective-permute-start.20) | collective-permute-done | bytes 458784 | tf_op jit(solution)/shard_map/ppermute | solution.py:109
  155.3 5.3 %collective-permute-done.21 = bf16[256,896]{1,0:T(8,128)(2,1)S(1)} collective-permute-done((bf16[256,896]{1,0:T(8,128)(2,1)S(1)}, bf16[256,896]{1,0:T(8,128)(2,1)S(1)}, u32[]{:S(2)}, u32[]{:S(2)}) %collective-permute-start.21) | collective-permute-done | bytes 458784 | tf_op jit(solution)/shard_map/ppermute | solution.py:109
  162.9 2.4 gather_fusion
  165.9 1.9 fusion.6
  167.8 2.7 %copy.326 = bf16[256,4,896]{0,2,1:T(8,128)(2,1)S(1)} copy(bf16[256,4,896]{2,0,1:T(8,128)(2,1)} %fusion.6) | data formatting | bytes 3670016 | tf_op jit(solution)/shard_map/mul | solution.py:131
  170.5 3.2 %fusion.77 = bf16[256,512]{1,0:T(8,128)(2,1)S(1)} fusion(bf16[256,3584]{0,1:T(8,128)(2,1)S(1)} %bitcast.444, bf16[1,512,3584]{2,1,0:T(8,128)(2,1)} %param.14), kind=kOutput, calls=%fused_computation.105 | convolution fusion | flops 939655168 | bytes 5767168 | tf_op jit(solution)/shard_map/dot_general | solution.py:135
  174.7 3.7 %collective-permute-start.23 = (bf16[1,130,4,128]{3,1,2,0:T(8,128)(2,1)S(1)}, bf16[1,130,4,128]{3,1,2,0:T(8,128)(2,1)S(1)}, u32[]{:S(2)}, u32[]{:S(2)}) collective-permute-start(bf16[1,130,4,128]{3,1,2,0:T(8,128)(2,1)S(1)} %pad_maximum_fusion.1), channel_id=1, source_target_pairs={{4,12},{12,20},{20,28},{28,36},{36,44},{44,52},{52,60},{60,68},{68... | collective-permute-start | bytes 399368 | tf_op jit(solution)/shard_map/ppermute | solution.py:20
  178.4 2.0 collective-permute-done.23
  180.6 3.8 %collective-permute-start.24 = (bf16[1,130,4,128]{3,1,2,0:T(8,128)(2,1)S(1)}, bf16[1,130,4,128]{3,1,2,0:T(8,128)(2,1)S(1)}, u32[]{:S(2)}, u32[]{:S(2)}) collective-permute-start(bf16[1,130,4,128]{3,1,2,0:T(8,128)(2,1)S(1)} %pad_maximum_fusion.2), channel_id=1, source_target_pairs={{4,12},{12,20},{20,28},{28,36},{36,44},{44,52},{52,60},{60,68},{68... | collective-permute-start | bytes 399368 | tf_op jit(solution)/shard_map/ppermute | solution.py:20
  184.4 2.0 collective-permute-done.24
  186.6 5.4 %collective-permute-start.25 = (bf16[1,130,4,128]{3,1,2,0:T(8,128)(2,1)S(1)}, bf16[1,130,4,128]{3,1,2,0:T(8,128)(2,1)S(1)}, u32[]{:S(2)}, u32[]{:S(2)}) collective-permute-start(bf16[1,130,4,128]{3,1,2,0:T(8,128)(2,1)S(1)} %pad_maximum_fusion.3), channel_id=1, source_target_pairs={{4,20},{12,28},{20,36},{28,44},{36,52},{44,60},{52,68},{60,76},{68... | collective-permute-start | bytes 399368 | tf_op jit(solution)/shard_map/ppermute | solution.py:20
  191.9 2.0 collective-permute-done.25
  194.1 10.7 %collective-permute-start.26 = (bf16[1,130,4,128]{3,1,2,0:T(8,128)(2,1)S(1)}, bf16[1,130,4,128]{3,1,2,0:T(8,128)(2,1)S(1)}, u32[]{:S(2)}, u32[]{:S(2)}) collective-permute-start(bf16[1,130,4,128]{3,1,2,0:T(8,128)(2,1)S(1)} %pad_maximum_fusion.4), channel_id=1, source_target_pairs={{4,36},{12,44},{20,52},{28,60},{36,68},{44,76},{52,84},{60,92},{68... | collective-permute-start | bytes 399368 | tf_op jit(solution)/shard_map/ppermute | solution.py:20
  204.8 6.5 %collective-permute-done.26 = bf16[1,130,4,128]{3,1,2,0:T(8,128)(2,1)S(1)} collective-permute-done((bf16[1,130,4,128]{3,1,2,0:T(8,128)(2,1)S(1)}, bf16[1,130,4,128]{3,1,2,0:T(8,128)(2,1)S(1)}, u32[]{:S(2)}, u32[]{:S(2)}) %collective-permute-start.26) | collective-permute-done | bytes 133152 | tf_op jit(solution)/shard_map/ppermute | solution.py:20
  211.5 6.8 %collective-permute-start.27 = (bf16[1,130,4,128]{3,1,2,0:T(8,128)(2,1)S(1)}, bf16[1,130,4,128]{3,1,2,0:T(8,128)(2,1)S(1)}, u32[]{:S(2)}, u32[]{:S(2)}) collective-permute-start(bf16[1,130,4,128]{3,1,2,0:T(8,128)(2,1)S(1)} %pad_maximum_fusion.5), channel_id=1, source_target_pairs={{4,68},{12,76},{20,84},{28,92},{36,100},{44,108},{52,116},{60,124}... | collective-permute-start | bytes 399368 | tf_op jit(solution)/shard_map/ppermute | solution.py:20
  218.3 2.0 collective-permute-done.27
  221.1 14.0 %collective-permute-start.28 = (bf16[1,130,4,128]{3,1,2,0:T(8,128)(2,1)}, bf16[1,130,4,128]{3,1,2,0:T(8,128)(2,1)S(1)}, u32[]{:S(2)}, u32[]{:S(2)}) collective-permute-start(bf16[1,130,4,128]{3,1,2,0:T(8,128)(2,1)} %pad_maximum_fusion.6), channel_id=1, source_target_pairs={{4,132},{12,140},{20,148},{28,156},{36,164},{44,172},{52,180},{60,... | collective-permute-start | bytes 399368 | tf_op jit(solution)/shard_map/ppermute | solution.py:20
  236.5 2.8 %collective-permute-done.28 = bf16[1,130,4,128]{3,1,2,0:T(8,128)(2,1)S(1)} collective-permute-done((bf16[1,130,4,128]{3,1,2,0:T(8,128)(2,1)}, bf16[1,130,4,128]{3,1,2,0:T(8,128)(2,1)S(1)}, u32[]{:S(2)}, u32[]{:S(2)}) %collective-permute-start.28) | collective-permute-done | bytes 133152 | tf_op jit(solution)/shard_map/ppermute | solution.py:20
  239.5 7.6 %collective-permute-start.29 = (bf16[1,130,4,128]{3,1,2,0:T(8,128)(2,1)S(1)}, bf16[1,130,4,128]{3,1,2,0:T(8,128)(2,1)S(1)}, u32[]{:S(2)}, u32[]{:S(2)}) collective-permute-start(bf16[1,130,4,128]{3,1,2,0:T(8,128)(2,1)S(1)} %pad_maximum_fusion.7), channel_id=1, source_target_pairs={{4,260},{12,268},{20,276},{28,284},{36,292},{44,300},{52,308},{60,... | collective-permute-start | bytes 399368 | tf_op jit(solution)/shard_map/ppermute | solution.py:20
  249.4 13.2 %collective-permute-start.30 = (bf16[1,130,4,128]{3,1,2,0:T(8,128)(2,1)S(1)}, bf16[1,130,4,128]{3,1,2,0:T(8,128)(2,1)S(1)}, u32[]{:S(2)}, u32[]{:S(2)}) collective-permute-start(bf16[1,130,4,128]{3,1,2,0:T(8,128)(2,1)S(1)} %pad_maximum_fusion.8), channel_id=1, source_target_pairs={{4,516},{12,524},{20,532},{28,540},{36,548},{44,556},{52,564},{60,... | collective-permute-start | bytes 399368 | tf_op jit(solution)/shard_map/ppermute | solution.py:20
  (234 shorter events, 68.2 us)
Async XLA Ops:
  1.6 22.5 %collective-permute-start.12 = (bf16[256,256]{1,0:T(8,128)(2,1)S(1)}, bf16[256,256]{1,0:T(8,128)(2,1)S(1)}, u32[]{:S(2)}, u32[]{:S(2)}) collective-permute-start(bf16[256,256]{1,0:T(8,128)(2,1)S(1)} %pad_maximum_fusion.9), channel_id=1, source_target_pairs={{0,104},{8,112},{16,120},{24,128},{32,136},{40,144},{48,152},{56,1... | collective-permute-start | bytes 393224 | tf_op jit(solution)/shard_map/ppermute | solution.py:20
  2.2 22.8 %collective-permute-start.11 = (bf16[256,256]{1,0:T(8,128)(2,1)S(1)}, bf16[256,256]{1,0:T(8,128)(2,1)S(1)}, u32[]{:S(2)}, u32[]{:S(2)}) collective-permute-start(bf16[256,256]{1,0:T(8,128)(2,1)S(1)} %pad_maximum_fusion.9), channel_id=1, source_target_pairs={{0,96},{8,104},{16,112},{24,120},{32,128},{40,136},{48,144},{56,15... | collective-permute-start | bytes 393224 | tf_op jit(solution)/shard_map/ppermute | solution.py:20
  2.9 23.1 %collective-permute-start.10 = (bf16[256,256]{1,0:T(8,128)(2,1)S(1)}, bf16[256,256]{1,0:T(8,128)(2,1)S(1)}, u32[]{:S(2)}, u32[]{:S(2)}) collective-permute-start(bf16[256,256]{1,0:T(8,128)(2,1)S(1)} %pad_maximum_fusion.9), channel_id=1, source_target_pairs={{0,88},{8,96},{16,104},{24,112},{32,120},{40,128},{48,136},{56,144... | collective-permute-start | bytes 393224 | tf_op jit(solution)/shard_map/ppermute | solution.py:20
  3.6 23.5 %collective-permute-start.9 = (bf16[256,256]{1,0:T(8,128)(2,1)S(1)}, bf16[256,256]{1,0:T(8,128)(2,1)S(1)}, u32[]{:S(2)}, u32[]{:S(2)}) collective-permute-start(bf16[256,256]{1,0:T(8,128)(2,1)S(1)} %pad_maximum_fusion.9), channel_id=1, source_target_pairs={{0,80},{8,88},{16,96},{24,104},{32,112},{40,120},{48,128},{56,136}... | collective-permute-start | bytes 393224 | tf_op jit(solution)/shard_map/ppermute | solution.py:20
  4.3 23.8 %collective-permute-start.8 = (bf16[256,256]{1,0:T(8,128)(2,1)S(1)}, bf16[256,256]{1,0:T(8,128)(2,1)S(1)}, u32[]{:S(2)}, u32[]{:S(2)}) collective-permute-start(bf16[256,256]{1,0:T(8,128)(2,1)S(1)} %pad_maximum_fusion.9), channel_id=1, source_target_pairs={{0,72},{8,80},{16,88},{24,96},{32,104},{40,112},{48,120},{56,128},... | collective-permute-start | bytes 393224 | tf_op jit(solution)/shard_map/ppermute | solution.py:20
  24.0 5.1 %collective-permute-start.7 = (bf16[256,256]{1,0:T(8,128)(2,1)S(1)}, bf16[256,256]{1,0:T(8,128)(2,1)S(1)}, u32[]{:S(2)}, u32[]{:S(2)}) collective-permute-start(bf16[256,256]{1,0:T(8,128)(2,1)S(1)} %pad_maximum_fusion.9), channel_id=1, source_target_pairs={{0,64},{8,72},{16,80},{24,88},{32,96},{40,104},{48,112},{56,120},{... | collective-permute-start | bytes 393224 | tf_op jit(solution)/shard_map/ppermute | solution.py:20
  25.1 5.1 %collective-permute-start.6 = (bf16[256,256]{1,0:T(8,128)(2,1)S(1)}, bf16[256,256]{1,0:T(8,128)(2,1)S(1)}, u32[]{:S(2)}, u32[]{:S(2)}) collective-permute-start(bf16[256,256]{1,0:T(8,128)(2,1)S(1)} %pad_maximum_fusion.9), channel_id=1, source_target_pairs={{0,56},{8,64},{16,72},{24,80},{32,88},{40,96},{48,104},{56,112},{6... | collective-permute-start | bytes 393224 | tf_op jit(solution)/shard_map/ppermute | solution.py:20
  26.1 5.1 %collective-permute-start.5 = (bf16[256,256]{1,0:T(8,128)(2,1)S(1)}, bf16[256,256]{1,0:T(8,128)(2,1)S(1)}, u32[]{:S(2)}, u32[]{:S(2)}) collective-permute-start(bf16[256,256]{1,0:T(8,128)(2,1)S(1)} %pad_maximum_fusion.9), channel_id=1, source_target_pairs={{0,48},{8,56},{16,64},{24,72},{32,80},{40,88},{48,96},{56,104},{64... | collective-permute-start | bytes 393224 | tf_op jit(solution)/shard_map/ppermute | solution.py:20
  27.1 5.1 %collective-permute-start.4 = (bf16[256,256]{1,0:T(8,128)(2,1)S(1)}, bf16[256,256]{1,0:T(8,128)(2,1)S(1)}, u32[]{:S(2)}, u32[]{:S(2)}) collective-permute-start(bf16[256,256]{1,0:T(8,128)(2,1)S(1)} %pad_maximum_fusion.9), channel_id=1, source_target_pairs={{0,40},{8,48},{16,56},{24,64},{32,72},{40,80},{48,88},{56,96},{64,... | collective-permute-start | bytes 393224 | tf_op jit(solution)/shard_map/ppermute | solution.py:20
  28.1 5.1 %collective-permute-start.3 = (bf16[256,256]{1,0:T(8,128)(2,1)S(1)}, bf16[256,256]{1,0:T(8,128)(2,1)S(1)}, u32[]{:S(2)}, u32[]{:S(2)}) collective-permute-start(bf16[256,256]{1,0:T(8,128)(2,1)S(1)} %pad_maximum_fusion.9), channel_id=1, source_target_pairs={{0,32},{8,40},{16,48},{24,56},{32,64},{40,72},{48,80},{56,88},{64,... | collective-permute-start | bytes 393224 | tf_op jit(solution)/shard_map/ppermute | solution.py:20
  29.1 5.1 %collective-permute-start.2 = (bf16[256,256]{1,0:T(8,128)(2,1)S(1)}, bf16[256,256]{1,0:T(8,128)(2,1)S(1)}, u32[]{:S(2)}, u32[]{:S(2)}) collective-permute-start(bf16[256,256]{1,0:T(8,128)(2,1)S(1)} %pad_maximum_fusion.9), channel_id=1, source_target_pairs={{0,24},{8,32},{16,40},{24,48},{32,56},{40,64},{48,72},{56,80},{64,... | collective-permute-start | bytes 393224 | tf_op jit(solution)/shard_map/ppermute | solution.py:20
  30.2 5.3 %collective-permute-start.1 = (bf16[256,256]{1,0:T(8,128)(2,1)S(1)}, bf16[256,256]{1,0:T(8,128)(2,1)S(1)}, u32[]{:S(2)}, u32[]{:S(2)}) collective-permute-start(bf16[256,256]{1,0:T(8,128)(2,1)S(1)} %pad_maximum_fusion.9), channel_id=1, source_target_pairs={{0,16},{8,24},{16,32},{24,40},{32,48},{40,56},{48,64},{56,72},{64,... | collective-permute-start | bytes 393224 | tf_op jit(solution)/shard_map/ppermute | solution.py:20
  56.7 90.2 %collective-permute-start.19 = (bf16[256,896]{1,0:T(8,128)(2,1)S(1)}, bf16[256,896]{1,0:T(8,128)(2,1)S(1)}, u32[]{:S(2)}, u32[]{:S(2)}) collective-permute-start(bf16[256,896]{1,0:T(8,128)(2,1)S(1)} %add_convert_fusion), channel_id=1, source_target_pairs={{0,4},{1,5},{2,6},{3,7},{8,12},{9,13},{10,14},{11,15},{16,20},{17,... | collective-permute-start | bytes 1376264 | tf_op jit(solution)/shard_map/ppermute | solution.py:109
  58.0 97.3 %collective-permute-start.20 = (bf16[256,896]{1,0:T(8,128)(2,1)S(1)}, bf16[256,896]{1,0:T(8,128)(2,1)S(1)}, u32[]{:S(2)}, u32[]{:S(2)}) collective-permute-start(bf16[256,896]{1,0:T(8,128)(2,1)S(1)} %add_convert_fusion), channel_id=1, source_target_pairs={{0,5},{1,6},{2,7},{3,4},{8,13},{9,14},{10,15},{11,12},{16,21},{17,... | collective-permute-start | bytes 1376264 | tf_op jit(solution)/shard_map/ppermute | solution.py:109
  59.3 101.4 %collective-permute-start.21 = (bf16[256,896]{1,0:T(8,128)(2,1)S(1)}, bf16[256,896]{1,0:T(8,128)(2,1)S(1)}, u32[]{:S(2)}, u32[]{:S(2)}) collective-permute-start(bf16[256,896]{1,0:T(8,128)(2,1)S(1)} %add_convert_fusion), channel_id=1, source_target_pairs={{0,6},{1,7},{2,4},{3,5},{8,14},{9,15},{10,12},{11,13},{16,22},{17,... | collective-permute-start | bytes 1376264 | tf_op jit(solution)/shard_map/ppermute | solution.py:109
  60.6 100.8 %collective-permute-start.22 = (bf16[256,896]{1,0:T(8,128)(2,1)S(1)}, bf16[256,896]{1,0:T(8,128)(2,1)S(1)}, u32[]{:S(2)}, u32[]{:S(2)}) collective-permute-start(bf16[256,896]{1,0:T(8,128)(2,1)S(1)} %add_convert_fusion), channel_id=1, source_target_pairs={{0,7},{1,4},{2,5},{3,6},{8,15},{9,12},{10,13},{11,14},{16,23},{17,... | collective-permute-start | bytes 1376264 | tf_op jit(solution)/shard_map/ppermute | solution.py:109
  174.7 5.7 %collective-permute-start.23 = (bf16[1,130,4,128]{3,1,2,0:T(8,128)(2,1)S(1)}, bf16[1,130,4,128]{3,1,2,0:T(8,128)(2,1)S(1)}, u32[]{:S(2)}, u32[]{:S(2)}) collective-permute-start(bf16[1,130,4,128]{3,1,2,0:T(8,128)(2,1)S(1)} %pad_maximum_fusion.1), channel_id=1, source_target_pairs={{4,12},{12,20},{20,28},{28,36},{36,44},{44,52},{52,60},{60,68},{68... | collective-permute-start | bytes 399368 | tf_op jit(solution)/shard_map/ppermute | solution.py:20
  180.6 5.8 %collective-permute-start.24 = (bf16[1,130,4,128]{3,1,2,0:T(8,128)(2,1)S(1)}, bf16[1,130,4,128]{3,1,2,0:T(8,128)(2,1)S(1)}, u32[]{:S(2)}, u32[]{:S(2)}) collective-permute-start(bf16[1,130,4,128]{3,1,2,0:T(8,128)(2,1)S(1)} %pad_maximum_fusion.2), channel_id=1, source_target_pairs={{4,12},{12,20},{20,28},{28,36},{36,44},{44,52},{52,60},{60,68},{68... | collective-permute-start | bytes 399368 | tf_op jit(solution)/shard_map/ppermute | solution.py:20
  186.6 7.4 %collective-permute-start.25 = (bf16[1,130,4,128]{3,1,2,0:T(8,128)(2,1)S(1)}, bf16[1,130,4,128]{3,1,2,0:T(8,128)(2,1)S(1)}, u32[]{:S(2)}, u32[]{:S(2)}) collective-permute-start(bf16[1,130,4,128]{3,1,2,0:T(8,128)(2,1)S(1)} %pad_maximum_fusion.3), channel_id=1, source_target_pairs={{4,20},{12,28},{20,36},{28,44},{36,52},{44,60},{52,68},{60,76},{68... | collective-permute-start | bytes 399368 | tf_op jit(solution)/shard_map/ppermute | solution.py:20
  194.1 17.1 %collective-permute-start.26 = (bf16[1,130,4,128]{3,1,2,0:T(8,128)(2,1)S(1)}, bf16[1,130,4,128]{3,1,2,0:T(8,128)(2,1)S(1)}, u32[]{:S(2)}, u32[]{:S(2)}) collective-permute-start(bf16[1,130,4,128]{3,1,2,0:T(8,128)(2,1)S(1)} %pad_maximum_fusion.4), channel_id=1, source_target_pairs={{4,36},{12,44},{20,52},{28,60},{36,68},{44,76},{52,84},{60,92},{68... | collective-permute-start | bytes 399368 | tf_op jit(solution)/shard_map/ppermute | solution.py:20
  211.5 8.8 %collective-permute-start.27 = (bf16[1,130,4,128]{3,1,2,0:T(8,128)(2,1)S(1)}, bf16[1,130,4,128]{3,1,2,0:T(8,128)(2,1)S(1)}, u32[]{:S(2)}, u32[]{:S(2)}) collective-permute-start(bf16[1,130,4,128]{3,1,2,0:T(8,128)(2,1)S(1)} %pad_maximum_fusion.5), channel_id=1, source_target_pairs={{4,68},{12,76},{20,84},{28,92},{36,100},{44,108},{52,116},{60,124}... | collective-permute-start | bytes 399368 | tf_op jit(solution)/shard_map/ppermute | solution.py:20
  221.1 18.2 %collective-permute-start.28 = (bf16[1,130,4,128]{3,1,2,0:T(8,128)(2,1)}, bf16[1,130,4,128]{3,1,2,0:T(8,128)(2,1)S(1)}, u32[]{:S(2)}, u32[]{:S(2)}) collective-permute-start(bf16[1,130,4,128]{3,1,2,0:T(8,128)(2,1)} %pad_maximum_fusion.6), channel_id=1, source_target_pairs={{4,132},{12,140},{20,148},{28,156},{36,164},{44,172},{52,180},{60,... | collective-permute-start | bytes 399368 | tf_op jit(solution)/shard_map/ppermute | solution.py:20
  239.5 9.7 %collective-permute-start.29 = (bf16[1,130,4,128]{3,1,2,0:T(8,128)(2,1)S(1)}, bf16[1,130,4,128]{3,1,2,0:T(8,128)(2,1)S(1)}, u32[]{:S(2)}, u32[]{:S(2)}) collective-permute-start(bf16[1,130,4,128]{3,1,2,0:T(8,128)(2,1)S(1)} %pad_maximum_fusion.7), channel_id=1, source_target_pairs={{4,260},{12,268},{20,276},{28,284},{36,292},{44,300},{52,308},{60,... | collective-permute-start | bytes 399368 | tf_op jit(solution)/shard_map/ppermute | solution.py:20
  249.4 15.2 %collective-permute-start.30 = (bf16[1,130,4,128]{3,1,2,0:T(8,128)(2,1)S(1)}, bf16[1,130,4,128]{3,1,2,0:T(8,128)(2,1)S(1)}, u32[]{:S(2)}, u32[]{:S(2)}) collective-permute-start(bf16[1,130,4,128]{3,1,2,0:T(8,128)(2,1)S(1)} %pad_maximum_fusion.8), channel_id=1, source_target_pairs={{4,516},{12,524},{20,532},{28,540},{36,548},{44,556},{52,564},{60,... | collective-permute-start | bytes 399368 | tf_op jit(solution)/shard_map/ppermute | solution.py:20
  (23 other events, 297.4 us)

commit v4 on v3

--- a/solution.py
+++ b/solution.py
@@ -165,8 +165,9 @@
         return jnp.concatenate([moved[:, :1] + moved[:, 1:2], moved[:, 2:]], axis=1)
 
     total_rows = jnp.broadcast_to(cumulated[-1][:, None, :, None], (key_heads, 1, group_size, head_size))
-    entry = sent_along(jnp.concatenate([total_rows, fresh_state], axis=1), 1)
-    reach = 1
+    own_entry = jnp.concatenate([total_rows, fresh_state], axis=1)
+    entry = chain(chain(sent_along(own_entry, 3), sent_along(own_entry, 2)), sent_along(own_entry, 1))
+    reach = 3
     while reach < shards:
         entry = chain(sent_along(entry, reach), entry)
         reach *= 2

time: 270 us -> 250 us (0.926)
  starting transfers between devices: 85.7 us -> 76.1 us
  waiting for transfers between devices: 119 us -> 110 us
    ppermute x24, starting transfers between devices: 76.1 us -> 66.5 us  [passed_along(): return lax.ppermute(x, ('ctx', 'section'), pairs)]
    ppermute x24, waiting for transfers between devices: 19.9 us -> 11 us  [passed_along(): return lax.ppermute(x, ('ctx', 'section'), pairs)]
  transfers between devices with their start and end apart: 31 -> 31, of which waited for: 12 -> 10; matrix products, arithmetic and copies ran while one was open for 10% -> 11% of each run, Pallas kernels for 0% -> 0%
where the time goes in v4:
time: 250 us; the launch traced here: 249 us
  waiting for transfers between devices  110 us (44%)
  starting transfers between devices  76.1 us (30%)
  other arithmetic  30 us (12%)
  matrix products  18 us (7%)
  local copies, waits for them, and re-layouts  13 us (5%)
    ppermute x4, waiting for transfers between devices, body(): lax.ppermute(own_hidden, ('section', 'tp'), [(m, members + (m + step) % m...  98.6 us
    ppermute x24, starting transfers between devices, passed_along(): return lax.ppermute(x, ('ctx', 'section'), pairs)  66.5 us
    ppermute x24, waiting for transfers between devices, passed_along(): return lax.ppermute(x, ('ctx', 'section'), pairs)  11 us
    and x17, other arithmetic, body(): key_valid = (source >= 0) & (positions < lengths[jnp.maximum(source, 0)])  10.7 us
    dot_general x17, matrix products, body(): jnp.einsum('gjrk,kgd->gjrd', weights.astype(jnp.bfloat16), value_block.re...  6.2 us
    dot_general x17, matrix products, body(): jnp.einsum('rgjd,kgd->gjrk', query_rows, key_block.reshape(row_count, key...  5.54 us
    ppermute x4, starting transfers between devices, body(): lax.ppermute(own_hidden, ('section', 'tp'), [(m, members + (m + step) % m...  5.17 us
  transfers between devices with their start and end apart: 31, of which 10 were waited for; matrix products, arithmetic and copies ran while one was open for 11% of the time, Pallas kernels for 0%

profile of v4, /device:TPU:1, one launch (start us, length us, event | category | flops | bytes accessed | tf_op | source)
XLA Modules:
  0.0 248.8 jit_solution(10971019745165029188)
XLA Ops:
  5.0 2.1 fusion.398
  50.2 1.6 collective-permute-start.16
  53.3 1.4 collective-permute-start.18
  55.1 1.6 add_convert_fusion
  63.3 84.0 %collective-permute-done.19 = bf16[256,896]{1,0:T(8,128)(2,1)S(1)} collective-permute-done((bf16[256,896]{1,0:T(8,128)(2,1)S(1)}, bf16[256,896]{1,0:T(8,128)(2,1)S(1)}, u32[]{:S(2)}, u32[]{:S(2)}) %collective-permute-start.19) | collective-permute-done | bytes 458784 | tf_op jit(solution)/shard_map/ppermute | solution.py:109
  147.3 8.5 %collective-permute-done.20 = bf16[256,896]{1,0:T(8,128)(2,1)S(1)} collective-permute-done((bf16[256,896]{1,0:T(8,128)(2,1)S(1)}, bf16[256,896]{1,0:T(8,128)(2,1)S(1)}, u32[]{:S(2)}, u32[]{:S(2)}) %collective-permute-start.20) | collective-permute-done | bytes 458784 | tf_op jit(solution)/shard_map/ppermute | solution.py:109
  155.8 5.4 %collective-permute-done.21 = bf16[256,896]{1,0:T(8,128)(2,1)S(1)} collective-permute-done((bf16[256,896]{1,0:T(8,128)(2,1)S(1)}, bf16[256,896]{1,0:T(8,128)(2,1)S(1)}, u32[]{:S(2)}, u32[]{:S(2)}) %collective-permute-start.21) | collective-permute-done | bytes 458784 | tf_op jit(solution)/shard_map/ppermute | solution.py:109
  161.9 1.5 pad_maximum_fusion
  163.4 2.4 gather_fusion
  166.4 1.9 fusion.6
  168.3 2.7 %copy.326 = bf16[256,4,896]{0,2,1:T(8,128)(2,1)S(1)} copy(bf16[256,4,896]{2,0,1:T(8,128)(2,1)} %fusion.6) | data formatting | bytes 3670016 | tf_op jit(solution)/shard_map/mul | solution.py:131
  171.1 3.3 %fusion.77 = bf16[256,512]{1,0:T(8,128)(2,1)S(1)} fusion(bf16[256,3584]{0,1:T(8,128)(2,1)S(1)} %bitcast.444, bf16[1,512,3584]{2,1,0:T(8,128)(2,1)} %param.14), kind=kOutput, calls=%fused_computation.105 | convolution fusion | flops 939655168 | bytes 5767168 | tf_op jit(solution)/shard_map/dot_general | solution.py:135
  175.4 2.8 %collective-permute-start.23 = (bf16[1,130,4,128]{3,1,2,0:T(8,128)(2,1)S(1)}, bf16[1,130,4,128]{3,1,2,0:T(8,128)(2,1)S(1)}, u32[]{:S(2)}, u32[]{:S(2)}) collective-permute-start(bf16[1,130,4,128]{3,1,2,0:T(8,128)(2,1)S(1)} %pad_maximum_fusion.1), channel_id=1, source_target_pairs={{4,28},{12,36},{20,44},{28,52},{36,60},{44,68},{52,76},{60,84},{68... | collective-permute-start | bytes 399368 | tf_op jit(solution)/shard_map/ppermute | solution.py:20
  178.2 6.7 %collective-permute-start.24 = (bf16[1,130,4,128]{3,1,2,0:T(8,128)(2,1)S(1)}, bf16[1,130,4,128]{3,1,2,0:T(8,128)(2,1)S(1)}, u32[]{:S(2)}, u32[]{:S(2)}) collective-permute-start(bf16[1,130,4,128]{3,1,2,0:T(8,128)(2,1)S(1)} %pad_maximum_fusion.1), channel_id=1, source_target_pairs={{4,20},{12,28},{20,36},{28,44},{36,52},{44,60},{52,68},{60,76},{68... | collective-permute-start | bytes 399368 | tf_op jit(solution)/shard_map/ppermute | solution.py:20
  184.9 2.9 %collective-permute-start.25 = (bf16[1,130,4,128]{3,1,2,0:T(8,128)(2,1)S(1)}, bf16[1,130,4,128]{3,1,2,0:T(8,128)(2,1)S(1)}, u32[]{:S(2)}, u32[]{:S(2)}) collective-permute-start(bf16[1,130,4,128]{3,1,2,0:T(8,128)(2,1)S(1)} %pad_maximum_fusion.1), channel_id=1, source_target_pairs={{4,12},{12,20},{20,28},{28,36},{36,44},{44,52},{52,60},{60,68},{68... | collective-permute-start | bytes 399368 | tf_op jit(solution)/shard_map/ppermute | solution.py:20
  187.9 3.4 %collective-permute-done.25 = bf16[1,130,4,128]{3,1,2,0:T(8,128)(2,1)S(1)} collective-permute-done((bf16[1,130,4,128]{3,1,2,0:T(8,128)(2,1)S(1)}, bf16[1,130,4,128]{3,1,2,0:T(8,128)(2,1)S(1)}, u32[]{:S(2)}, u32[]{:S(2)}) %collective-permute-start.25) | collective-permute-done | bytes 133152 | tf_op jit(solution)/shard_map/ppermute | solution.py:20
  191.5 3.5 %collective-permute-start.26 = (bf16[1,130,4,128]{3,1,2,0:T(8,128)(2,1)S(1)}, bf16[1,130,4,128]{3,1,2,0:T(8,128)(2,1)S(1)}, u32[]{:S(2)}, u32[]{:S(2)}) collective-permute-start(bf16[1,130,4,128]{3,1,2,0:T(8,128)(2,1)S(1)} %pad_maximum_fusion.2), channel_id=1, source_target_pairs={{4,28},{12,36},{20,44},{28,52},{36,60},{44,68},{52,76},{60,84},{68... | collective-permute-start | bytes 399368 | tf_op jit(solution)/shard_map/ppermute | solution.py:20
  195.0 2.0 collective-permute-done.26
  197.2 9.3 %collective-permute-start.27 = (bf16[1,130,4,128]{3,1,2,0:T(8,128)(2,1)S(1)}, bf16[1,130,4,128]{3,1,2,0:T(8,128)(2,1)S(1)}, u32[]{:S(2)}, u32[]{:S(2)}) collective-permute-start(bf16[1,130,4,128]{3,1,2,0:T(8,128)(2,1)S(1)} %pad_maximum_fusion.3), channel_id=1, source_target_pairs={{4,52},{12,60},{20,68},{28,76},{36,84},{44,92},{52,100},{60,108},{... | collective-permute-start | bytes 399368 | tf_op jit(solution)/shard_map/ppermute | solution.py:20
  206.5 2.0 collective-permute-done.27
  209.3 16.2 %collective-permute-start.28 = (bf16[1,130,4,128]{3,1,2,0:T(8,128)(2,1)}, bf16[1,130,4,128]{3,1,2,0:T(8,128)(2,1)}, u32[]{:S(2)}, u32[]{:S(2)}) collective-permute-start(bf16[1,130,4,128]{3,1,2,0:T(8,128)(2,1)} %pad_maximum_fusion.4), channel_id=1, source_target_pairs={{4,100},{12,108},{20,116},{28,124},{36,132},{44,140},{52,148},{60,... | collective-permute-start | bytes 399368 | tf_op jit(solution)/shard_map/ppermute | solution.py:20
  228.3 6.4 %collective-permute-start.29 = (bf16[1,130,4,128]{3,1,2,0:T(8,128)(2,1)S(1)}, bf16[1,130,4,128]{3,1,2,0:T(8,128)(2,1)S(1)}, u32[]{:S(2)}, u32[]{:S(2)}) collective-permute-start(bf16[1,130,4,128]{3,1,2,0:T(8,128)(2,1)S(1)} %pad_maximum_fusion.5), channel_id=1, source_target_pairs={{4,196},{12,204},{20,212},{28,220},{36,228},{44,236},{52,244},{60,... | collective-permute-start | bytes 399368 | tf_op jit(solution)/shard_map/ppermute | solution.py:20
  236.9 7.8 %collective-permute-start.30 = (bf16[1,130,4,128]{3,1,2,0:T(8,128)(2,1)S(1)}, bf16[1,130,4,128]{3,1,2,0:T(8,128)(2,1)S(1)}, u32[]{:S(2)}, u32[]{:S(2)}) collective-permute-start(bf16[1,130,4,128]{3,1,2,0:T(8,128)(2,1)S(1)} %pad_maximum_fusion.6), channel_id=1, source_target_pairs={{4,388},{12,396},{20,404},{28,412},{36,420},{44,428},{52,436},{60,... | collective-permute-start | bytes 399368 | tf_op jit(solution)/shard_map/ppermute | solution.py:20
  245.3 1.5 collective-permute-done.30
  (220 shorter events, 65.9 us)
Async XLA Ops:
  1.6 22.5 %collective-permute-start.10 = (bf16[256,256]{1,0:T(8,128)(2,1)S(1)}, bf16[256,256]{1,0:T(8,128)(2,1)S(1)}, u32[]{:S(2)}, u32[]{:S(2)}) collective-permute-start(bf16[256,256]{1,0:T(8,128)(2,1)S(1)} %pad_maximum_fusion.7), channel_id=1, source_target_pairs={{0,88},{8,96},{16,104},{24,112},{32,120},{40,128},{48,136},{56,144... | collective-permute-start | bytes 393224 | tf_op jit(solution)/shard_map/ppermute | solution.py:20
  2.2 22.8 %collective-permute-start.9 = (bf16[256,256]{1,0:T(8,128)(2,1)S(1)}, bf16[256,256]{1,0:T(8,128)(2,1)S(1)}, u32[]{:S(2)}, u32[]{:S(2)}) collective-permute-start(bf16[256,256]{1,0:T(8,128)(2,1)S(1)} %pad_maximum_fusion.7), channel_id=1, source_target_pairs={{0,80},{8,88},{16,96},{24,104},{32,112},{40,120},{48,128},{56,136}... | collective-permute-start | bytes 393224 | tf_op jit(solution)/shard_map/ppermute | solution.py:20
  2.9 23.1 %collective-permute-start.8 = (bf16[256,256]{1,0:T(8,128)(2,1)S(1)}, bf16[256,256]{1,0:T(8,128)(2,1)S(1)}, u32[]{:S(2)}, u32[]{:S(2)}) collective-permute-start(bf16[256,256]{1,0:T(8,128)(2,1)S(1)} %pad_maximum_fusion.7), channel_id=1, source_target_pairs={{0,72},{8,80},{16,88},{24,96},{32,104},{40,112},{48,120},{56,128},... | collective-permute-start | bytes 393224 | tf_op jit(solution)/shard_map/ppermute | solution.py:20
  3.6 23.5 %collective-permute-start.7 = (bf16[256,256]{1,0:T(8,128)(2,1)S(1)}, bf16[256,256]{1,0:T(8,128)(2,1)S(1)}, u32[]{:S(2)}, u32[]{:S(2)}) collective-permute-start(bf16[256,256]{1,0:T(8,128)(2,1)S(1)} %pad_maximum_fusion.7), channel_id=1, source_target_pairs={{0,64},{8,72},{16,80},{24,88},{32,96},{40,104},{48,112},{56,120},{... | collective-permute-start | bytes 393224 | tf_op jit(solution)/shard_map/ppermute | solution.py:20
  4.3 23.8 %collective-permute-start.6 = (bf16[256,256]{1,0:T(8,128)(2,1)S(1)}, bf16[256,256]{1,0:T(8,128)(2,1)S(1)}, u32[]{:S(2)}, u32[]{:S(2)}) collective-permute-start(bf16[256,256]{1,0:T(8,128)(2,1)S(1)} %pad_maximum_fusion.7), channel_id=1, source_target_pairs={{0,56},{8,64},{16,72},{24,80},{32,88},{40,96},{48,104},{56,112},{6... | collective-permute-start | bytes 393224 | tf_op jit(solution)/shard_map/ppermute | solution.py:20
  24.0 5.1 %collective-permute-start.5 = (bf16[256,256]{1,0:T(8,128)(2,1)S(1)}, bf16[256,256]{1,0:T(8,128)(2,1)S(1)}, u32[]{:S(2)}, u32[]{:S(2)}) collective-permute-start(bf16[256,256]{1,0:T(8,128)(2,1)S(1)} %pad_maximum_fusion.7), channel_id=1, source_target_pairs={{0,48},{8,56},{16,64},{24,72},{32,80},{40,88},{48,96},{56,104},{64... | collective-permute-start | bytes 393224 | tf_op jit(solution)/shard_map/ppermute | solution.py:20
  25.1 5.1 %collective-permute-start.4 = (bf16[256,256]{1,0:T(8,128)(2,1)S(1)}, bf16[256,256]{1,0:T(8,128)(2,1)S(1)}, u32[]{:S(2)}, u32[]{:S(2)}) collective-permute-start(bf16[256,256]{1,0:T(8,128)(2,1)S(1)} %pad_maximum_fusion.7), channel_id=1, source_target_pairs={{0,40},{8,48},{16,56},{24,64},{32,72},{40,80},{48,88},{56,96},{64,... | collective-permute-start | bytes 393224 | tf_op jit(solution)/shard_map/ppermute | solution.py:20
  26.1 5.1 %collective-permute-start.3 = (bf16[256,256]{1,0:T(8,128)(2,1)S(1)}, bf16[256,256]{1,0:T(8,128)(2,1)S(1)}, u32[]{:S(2)}, u32[]{:S(2)}) collective-permute-start(bf16[256,256]{1,0:T(8,128)(2,1)S(1)} %pad_maximum_fusion.7), channel_id=1, source_target_pairs={{0,32},{8,40},{16,48},{24,56},{32,64},{40,72},{48,80},{56,88},{64,... | collective-permute-start | bytes 393224 | tf_op jit(solution)/shard_map/ppermute | solution.py:20
  27.1 5.1 %collective-permute-start.2 = (bf16[256,256]{1,0:T(8,128)(2,1)S(1)}, bf16[256,256]{1,0:T(8,128)(2,1)S(1)}, u32[]{:S(2)}, u32[]{:S(2)}) collective-permute-start(bf16[256,256]{1,0:T(8,128)(2,1)S(1)} %pad_maximum_fusion.7), channel_id=1, source_target_pairs={{0,24},{8,32},{16,40},{24,48},{32,56},{40,64},{48,72},{56,80},{64,... | collective-permute-start | bytes 393224 | tf_op jit(solution)/shard_map/ppermute | solution.py:20
  28.1 5.1 %collective-permute-start.1 = (bf16[256,256]{1,0:T(8,128)(2,1)S(1)}, bf16[256,256]{1,0:T(8,128)(2,1)S(1)}, u32[]{:S(2)}, u32[]{:S(2)}) collective-permute-start(bf16[256,256]{1,0:T(8,128)(2,1)S(1)} %pad_maximum_fusion.7), channel_id=1, source_target_pairs={{0,16},{8,24},{16,32},{24,40},{32,48},{40,56},{48,64},{56,72},{64,... | collective-permute-start | bytes 393224 | tf_op jit(solution)/shard_map/ppermute | solution.py:20
  29.1 5.1 %collective-permute-start = (bf16[256,256]{1,0:T(8,128)(2,1)S(1)}, bf16[256,256]{1,0:T(8,128)(2,1)S(1)}, u32[]{:S(2)}, u32[]{:S(2)}) collective-permute-start(bf16[256,256]{1,0:T(8,128)(2,1)S(1)} %pad_maximum_fusion.7), channel_id=1, source_target_pairs={{0,8},{8,16},{16,24},{24,32},{32,40},{40,48},{48,56},{56,64},{64,7... | collective-permute-start | bytes 393224 | tf_op jit(solution)/shard_map/ppermute | solution.py:20
  30.2 5.3 %collective-permute-start.14 = (bf16[256,256]{1,0:T(8,128)(2,1)S(1)}, bf16[256,256]{1,0:T(8,128)(2,1)S(1)}, u32[]{:S(2)}, u32[]{:S(2)}) collective-permute-start(bf16[256,256]{1,0:T(8,128)(2,1)S(1)} %pad_maximum_fusion.7), channel_id=1, source_target_pairs={{0,120},{8,128},{16,136},{24,144},{32,152},{40,160},{48,168},{56,1... | collective-permute-start | bytes 393224 | tf_op jit(solution)/shard_map/ppermute | solution.py:20
  56.7 90.6 %collective-permute-start.19 = (bf16[256,896]{1,0:T(8,128)(2,1)S(1)}, bf16[256,896]{1,0:T(8,128)(2,1)S(1)}, u32[]{:S(2)}, u32[]{:S(2)}) collective-permute-start(bf16[256,896]{1,0:T(8,128)(2,1)S(1)} %add_convert_fusion), channel_id=1, source_target_pairs={{0,4},{1,5},{2,6},{3,7},{8,12},{9,13},{10,14},{11,15},{16,20},{17,... | collective-permute-start | bytes 1376264 | tf_op jit(solution)/shard_map/ppermute | solution.py:109
  58.0 97.8 %collective-permute-start.20 = (bf16[256,896]{1,0:T(8,128)(2,1)S(1)}, bf16[256,896]{1,0:T(8,128)(2,1)S(1)}, u32[]{:S(2)}, u32[]{:S(2)}) collective-permute-start(bf16[256,896]{1,0:T(8,128)(2,1)S(1)} %add_convert_fusion), channel_id=1, source_target_pairs={{0,5},{1,6},{2,7},{3,4},{8,13},{9,14},{10,15},{11,12},{16,21},{17,... | collective-permute-start | bytes 1376264 | tf_op jit(solution)/shard_map/ppermute | solution.py:109
  59.3 101.9 %collective-permute-start.21 = (bf16[256,896]{1,0:T(8,128)(2,1)S(1)}, bf16[256,896]{1,0:T(8,128)(2,1)S(1)}, u32[]{:S(2)}, u32[]{:S(2)}) collective-permute-start(bf16[256,896]{1,0:T(8,128)(2,1)S(1)} %add_convert_fusion), channel_id=1, source_target_pairs={{0,6},{1,7},{2,4},{3,5},{8,14},{9,15},{10,12},{11,13},{16,22},{17,... | collective-permute-start | bytes 1376264 | tf_op jit(solution)/shard_map/ppermute | solution.py:109
  60.6 101.3 %collective-permute-start.22 = (bf16[256,896]{1,0:T(8,128)(2,1)S(1)}, bf16[256,896]{1,0:T(8,128)(2,1)S(1)}, u32[]{:S(2)}, u32[]{:S(2)}) collective-permute-start(bf16[256,896]{1,0:T(8,128)(2,1)S(1)} %add_convert_fusion), channel_id=1, source_target_pairs={{0,7},{1,4},{2,5},{3,6},{8,15},{9,12},{10,13},{11,14},{16,23},{17,... | collective-permute-start | bytes 1376264 | tf_op jit(solution)/shard_map/ppermute | solution.py:109
  175.4 12.4 %collective-permute-start.23 = (bf16[1,130,4,128]{3,1,2,0:T(8,128)(2,1)S(1)}, bf16[1,130,4,128]{3,1,2,0:T(8,128)(2,1)S(1)}, u32[]{:S(2)}, u32[]{:S(2)}) collective-permute-start(bf16[1,130,4,128]{3,1,2,0:T(8,128)(2,1)S(1)} %pad_maximum_fusion.1), channel_id=1, source_target_pairs={{4,28},{12,36},{20,44},{28,52},{36,60},{44,68},{52,76},{60,84},{68... | collective-permute-start | bytes 399368 | tf_op jit(solution)/shard_map/ppermute | solution.py:20
  178.2 9.6 %collective-permute-start.24 = (bf16[1,130,4,128]{3,1,2,0:T(8,128)(2,1)S(1)}, bf16[1,130,4,128]{3,1,2,0:T(8,128)(2,1)S(1)}, u32[]{:S(2)}, u32[]{:S(2)}) collective-permute-start(bf16[1,130,4,128]{3,1,2,0:T(8,128)(2,1)S(1)} %pad_maximum_fusion.1), channel_id=1, source_target_pairs={{4,20},{12,28},{20,36},{28,44},{36,52},{44,60},{52,68},{60,76},{68... | collective-permute-start | bytes 399368 | tf_op jit(solution)/shard_map/ppermute | solution.py:20
  184.9 6.4 %collective-permute-start.25 = (bf16[1,130,4,128]{3,1,2,0:T(8,128)(2,1)S(1)}, bf16[1,130,4,128]{3,1,2,0:T(8,128)(2,1)S(1)}, u32[]{:S(2)}, u32[]{:S(2)}) collective-permute-start(bf16[1,130,4,128]{3,1,2,0:T(8,128)(2,1)S(1)} %pad_maximum_fusion.1), channel_id=1, source_target_pairs={{4,12},{12,20},{20,28},{28,36},{36,44},{44,52},{52,60},{60,68},{68... | collective-permute-start | bytes 399368 | tf_op jit(solution)/shard_map/ppermute | solution.py:20
  191.5 5.5 %collective-permute-start.26 = (bf16[1,130,4,128]{3,1,2,0:T(8,128)(2,1)S(1)}, bf16[1,130,4,128]{3,1,2,0:T(8,128)(2,1)S(1)}, u32[]{:S(2)}, u32[]{:S(2)}) collective-permute-start(bf16[1,130,4,128]{3,1,2,0:T(8,128)(2,1)S(1)} %pad_maximum_fusion.2), channel_id=1, source_target_pairs={{4,28},{12,36},{20,44},{28,52},{36,60},{44,68},{52,76},{60,84},{68... | collective-permute-start | bytes 399368 | tf_op jit(solution)/shard_map/ppermute | solution.py:20
  197.2 11.3 %collective-permute-start.27 = (bf16[1,130,4,128]{3,1,2,0:T(8,128)(2,1)S(1)}, bf16[1,130,4,128]{3,1,2,0:T(8,128)(2,1)S(1)}, u32[]{:S(2)}, u32[]{:S(2)}) collective-permute-start(bf16[1,130,4,128]{3,1,2,0:T(8,128)(2,1)S(1)} %pad_maximum_fusion.3), channel_id=1, source_target_pairs={{4,52},{12,60},{20,68},{28,76},{36,84},{44,92},{52,100},{60,108},{... | collective-permute-start | bytes 399368 | tf_op jit(solution)/shard_map/ppermute | solution.py:20
  209.3 17.9 %collective-permute-start.28 = (bf16[1,130,4,128]{3,1,2,0:T(8,128)(2,1)}, bf16[1,130,4,128]{3,1,2,0:T(8,128)(2,1)}, u32[]{:S(2)}, u32[]{:S(2)}) collective-permute-start(bf16[1,130,4,128]{3,1,2,0:T(8,128)(2,1)} %pad_maximum_fusion.4), channel_id=1, source_target_pairs={{4,100},{12,108},{20,116},{28,124},{36,132},{44,140},{52,148},{60,... | collective-permute-start | bytes 399368 | tf_op jit(solution)/shard_map/ppermute | solution.py:20
  228.3 8.4 %collective-permute-start.29 = (bf16[1,130,4,128]{3,1,2,0:T(8,128)(2,1)S(1)}, bf16[1,130,4,128]{3,1,2,0:T(8,128)(2,1)S(1)}, u32[]{:S(2)}, u32[]{:S(2)}) collective-permute-start(bf16[1,130,4,128]{3,1,2,0:T(8,128)(2,1)S(1)} %pad_maximum_fusion.5), channel_id=1, source_target_pairs={{4,196},{12,204},{20,212},{28,220},{36,228},{44,236},{52,244},{60,... | collective-permute-start | bytes 399368 | tf_op jit(solution)/shard_map/ppermute | solution.py:20
  236.9 9.8 %collective-permute-start.30 = (bf16[1,130,4,128]{3,1,2,0:T(8,128)(2,1)S(1)}, bf16[1,130,4,128]{3,1,2,0:T(8,128)(2,1)S(1)}, u32[]{:S(2)}, u32[]{:S(2)}) collective-permute-start(bf16[1,130,4,128]{3,1,2,0:T(8,128)(2,1)S(1)} %pad_maximum_fusion.6), channel_id=1, source_target_pairs={{4,388},{12,396},{20,404},{28,412},{36,420},{44,428},{52,436},{60,... | collective-permute-start | bytes 399368 | tf_op jit(solution)/shard_map/ppermute | solution.py:20
  (20 other events, 141.1 us)

commit v5 on v4

--- a/solution.py
+++ b/solution.py
@@ -47,19 +47,40 @@
     valid_rows = positions < lengths[shard_index]
     own_keys = keys[0]
 
-    query_rows = queries[0].reshape(row_count, key_heads, group_size, head_size)
+    key_width = own_keys.shape[1]
+    query_width = queries.shape[2]
+    mate_copy = lax.ppermute(
+        jnp.concatenate([queries[0], own_keys], axis=1), "section", [(0, 1)]
+    )
+    first_queries = jnp.where(section_index == 0, queries[0], mate_copy[:, :query_width])
+    first_keys = jnp.where(section_index == 0, own_keys, mate_copy[:, query_width:])
+    query_rows = first_queries.reshape(row_count, key_heads, group_size, head_size)
     base_distance = positions[:, None] - positions[None, :]
-    key_width = own_keys.shape[1]
-    packed = jnp.concatenate([own_keys, window_values], axis=1)
+    packed = jnp.concatenate([first_keys, window_values], axis=1)
+    sections = lax.axis_size("section")
+    plan = [(0, 1)] + [(2 * j, 2 * j + 1) for j in range(1, span_blocks // 2)]
+    plan += [(2 * j, None) for j in range(span_blocks // 2, span_blocks // 2 + 1)]
     running = jnp.zeros((key_heads, group_size, row_count, head_size), jnp.float32)
     totals = jnp.zeros((key_heads, group_size, row_count), jnp.float32)
     best = jnp.full((key_heads, group_size, row_count), -1e30, jnp.float32)
-    for distance_blocks in range(span_blocks + 1):
-        if distance_blocks == 0:
-            key_block, value_block = own_keys, window_values
-        else:
-            joined = passed_along(packed, distance_blocks, 0)
-            key_block, value_block = joined[:, :key_width], joined[:, key_width:]
+    for first_distance, second_distance in plan:
+        pairs = []
+        for taken, owner in ((first_distance, 0), (second_distance, 1)):
+            if taken:
+                pairs += [
+                    (i * sections + owner, (i + taken) * sections + owner)
+                    for i in range(shards)
+                    if i + taken < shards
+                ]
+        joined = lax.ppermute(packed, ("ctx", "section"), pairs)
+        if first_distance == 0:
+            joined = jnp.where(section_index == 0, packed, joined)
+        key_block, value_block = joined[:, :key_width], joined[:, key_width:]
+        distance_blocks = jnp.where(
+            section_index == 0,
+            first_distance,
+            span_blocks + 1 if second_distance is None else second_distance,
+        )
         source = shard_index - distance_blocks
         key_valid = (source >= 0) & (positions < lengths[jnp.maximum(source, 0)])
         scores = (
@@ -86,6 +107,17 @@
         running = running * factor[..., None] + blended
         totals = totals * factor + jnp.sum(weights, axis=-1)
         best = new_best
+    partial = lax.ppermute(
+        jnp.concatenate([running, totals[..., None], best[..., None]], axis=-1),
+        "section",
+        [(1, 0)],
+    )
+    other_best = partial[..., head_size + 1]
+    merged_best = jnp.maximum(best, other_best)
+    own_factor = jnp.exp(best - merged_best)
+    other_factor = jnp.exp(other_best - merged_best)
+    running = running * own_factor[..., None] + partial[..., :head_size] * other_factor[..., None]
+    totals = totals * own_factor + partial[..., head_size] * other_factor
     attention = running / jnp.maximum(totals, 1.0)[..., None]
     attention = attention.transpose(2, 0, 1, 3).reshape(row_count, query_head_rows * head_size)
     attention = jnp.where(valid_rows[:, None], attention, 0.0).astype(jnp.bfloat16)

time: 250 us -> 247 us (0.988)
  starting transfers between devices: 76.1 us -> 145 us
  waiting for transfers between devices: 110 us -> 49.9 us
  other arithmetic: 30 us -> 24.1 us
  matrix products: 18 us -> 14.3 us
    ppermute x4, waiting for transfers between devices: 98.6 us -> 22.2 us  [body(): lax.ppermute(own_hidden, ('section', 'tp'), [(m, members + (m + step) % m...]
    ppermute x0 -> x11, starting transfers between devices: none -> 67.5 us  [the longest x9 57.5 us: body(): joined = lax.ppermute(packed, ('ctx', 'section'), pairs)]
    ppermute x0 -> x11, waiting for transfers between devices: none -> 16.5 us  [the longest x9 13.6 us: body(): joined = lax.ppermute(packed, ('ctx', 'section'), pairs)]
    and x17 -> x9, other arithmetic: 10.7 us -> 5.72 us  [body(): key_valid = (source >= 0) & (positions < lengths[jnp.maximum(source, 0)])]
    dot_general x17 -> x9, matrix products: 6.2 us -> 3.12 us  [body(): jnp.einsum('gjrk,kgd->gjrd', weights.astype(jnp.bfloat16), value_block.re...]
    dot_general x17 -> x9, matrix products: 5.54 us -> 2.91 us  [body(): jnp.einsum('rgjd,kgd->gjrk', query_rows, key_block.reshape(row_count, key...]
    ppermute x24 -> x8, starting transfers between devices: 66.5 us -> 67.8 us  [passed_along(): return lax.ppermute(x, ('ctx', 'section'), pairs)]
    ppermute x24 -> x8, waiting for transfers between devices: 11 us -> 11.1 us  [passed_along(): return lax.ppermute(x, ('ctx', 'section'), pairs)]
  transfers between devices with their start and end apart: 31 -> 26, of which waited for: 10 -> 15; matrix products, arithmetic and copies ran while one was open for 11% -> 8% of each run, Pallas kernels for 0% -> 0%
where the time goes in v5:
time: 247 us; the launch traced here: 246 us
  starting transfers between devices  145 us (59%)
  waiting for transfers between devices  49.9 us (20%)
  other arithmetic  24.1 us (10%)
  matrix products  14.3 us (6%)
  local copies, waits for them, and re-layouts  11 us (4%)
    ppermute x8, starting transfers between devices, passed_along(): return lax.ppermute(x, ('ctx', 'section'), pairs)  67.8 us
    ppermute x9, starting transfers between devices, body(): joined = lax.ppermute(packed, ('ctx', 'section'), pairs)  57.5 us
    ppermute x4, waiting for transfers between devices, body(): lax.ppermute(own_hidden, ('section', 'tp'), [(m, members + (m + step) % m...  22.2 us
    ppermute x9, waiting for transfers between devices, body(): joined = lax.ppermute(packed, ('ctx', 'section'), pairs)  13.6 us
    ppermute x8, waiting for transfers between devices, passed_along(): return lax.ppermute(x, ('ctx', 'section'), pairs)  11.1 us
    ppermute x1, starting transfers between devices, body(): lax.ppermute(jnp.concatenate([running, totals[..., None], best[..., None]...  8.62 us
    and x9, other arithmetic, body(): key_valid = (source >= 0) & (positions < lengths[jnp.maximum(source, 0)])  5.72 us
    ppermute x4, starting transfers between devices, body(): lax.ppermute(own_hidden, ('section', 'tp'), [(m, members + (m + step) % m...  5.17 us
  transfers between devices with their start and end apart: 26, of which 15 were waited for; matrix products, arithmetic and copies ran while one was open for 8% of the time, Pallas kernels for 0%

profile of v5, /device:TPU:1, one launch (start us, length us, event | category | flops | bytes accessed | tf_op | source)
XLA Modules:
  0.0 245.9 jit_solution(2844823781821484270)
XLA Ops:
  11.7 3.0 %collective-permute-done = bf16[256,640]{1,0:T(8,128)(2,1)S(1)} collective-permute-done((bf16[256,640]{1,0:T(8,128)(2,1)S(1)}, bf16[256,640]{1,0:T(8,128)(2,1)S(1)}, u32[]{:S(2)}, u32[]{:S(2)}) %collective-permute-start) | collective-permute-done | bytes 327712 | tf_op jit(solution)/shard_map/ppermute | solution.py:52
  16.3 6.5 %collective-permute-start.8 = (bf16[256,256]{1,0:T(8,128)(2,1)S(1)}, bf16[256,256]{1,0:T(8,128)(2,1)S(1)}, u32[]{:S(2)}, u32[]{:S(2)}) collective-permute-start(bf16[256,256]{1,0:T(8,128)(2,1)S(1)} %pad_maximum_fusion.9), channel_id=1, source_target_pairs={{0,112},{8,120},{16,128},{24,136},{32,144},{40,152},{48,160},{56,1... | collective-permute-start | bytes 393224 | tf_op jit(solution)/shard_map/ppermute | solution.py:75
  22.9 6.2 %collective-permute-start.7 = (bf16[256,256]{1,0:T(8,128)(2,1)S(1)}, bf16[256,256]{1,0:T(8,128)(2,1)S(1)}, u32[]{:S(2)}, u32[]{:S(2)}) collective-permute-start(bf16[256,256]{1,0:T(8,128)(2,1)S(1)} %pad_maximum_fusion.9), channel_id=1, source_target_pairs={{0,96},{8,104},{16,112},{24,120},{32,128},{40,136},{48,144},{56,15... | collective-permute-start | bytes 393224 | tf_op jit(solution)/shard_map/ppermute | solution.py:75
  29.1 2.3 collective-permute-start.6
  31.4 8.2 %collective-permute-start.5 = (bf16[256,256]{1,0:T(8,128)(2,1)S(1)}, bf16[256,256]{1,0:T(8,128)(2,1)S(1)}, u32[]{:S(2)}, u32[]{:S(2)}) collective-permute-start(bf16[256,256]{1,0:T(8,128)(2,1)S(1)} %pad_maximum_fusion.9), channel_id=1, source_target_pairs={{0,64},{8,72},{16,80},{24,88},{32,96},{40,104},{48,112},{56,120},{... | collective-permute-start | bytes 393224 | tf_op jit(solution)/shard_map/ppermute | solution.py:75
  42.8 5.0 %collective-permute-start.2 = (bf16[256,256]{1,0:T(8,128)(2,1)S(1)}, bf16[256,256]{1,0:T(8,128)(2,1)S(1)}, u32[]{:S(2)}, u32[]{:S(2)}) collective-permute-start(bf16[256,256]{1,0:T(8,128)(2,1)S(1)} %pad_maximum_fusion.9), channel_id=1, source_target_pairs={{0,16},{8,24},{16,32},{24,40},{32,48},{40,56},{48,64},{56,72},{64,... | collective-permute-start | bytes 393224 | tf_op jit(solution)/shard_map/ppermute | solution.py:75
  48.2 2.5 %collective-permute-done.2 = bf16[256,256]{1,0:T(8,128)(2,1)S(1)} collective-permute-done((bf16[256,256]{1,0:T(8,128)(2,1)S(1)}, bf16[256,256]{1,0:T(8,128)(2,1)S(1)}, u32[]{:S(2)}, u32[]{:S(2)}) %collective-permute-start.2) | collective-permute-done | bytes 131104 | tf_op jit(solution)/shard_map/ppermute | solution.py:75
  50.7 12.9 %collective-permute-start.3 = (bf16[256,256]{1,0:T(8,128)(2,1)S(1)}, bf16[256,256]{1,0:T(8,128)(2,1)S(1)}, u32[]{:S(2)}, u32[]{:S(2)}) collective-permute-start(bf16[256,256]{1,0:T(8,128)(2,1)S(1)} %pad_maximum_fusion.9), channel_id=1, source_target_pairs={{0,32},{8,40},{16,48},{24,56},{32,64},{40,72},{48,80},{56,88},{64,... | collective-permute-start | bytes 393224 | tf_op jit(solution)/shard_map/ppermute | solution.py:75
  65.6 14.5 %collective-permute-start.4 = (bf16[256,256]{1,0:T(8,128)(2,1)S(1)}, bf16[256,256]{1,0:T(8,128)(2,1)S(1)}, u32[]{:S(2)}, u32[]{:S(2)}) collective-permute-start(bf16[256,256]{1,0:T(8,128)(2,1)S(1)} %pad_maximum_fusion.9), channel_id=1, source_target_pairs={{0,48},{8,56},{16,64},{24,72},{32,80},{40,88},{48,96},{56,104},{64... | collective-permute-start | bytes 393224 | tf_op jit(solution)/shard_map/ppermute | solution.py:75
  80.4 7.6 %collective-permute-done.4 = bf16[256,256]{1,0:T(8,128)(2,1)S(1)} collective-permute-done((bf16[256,256]{1,0:T(8,128)(2,1)S(1)}, bf16[256,256]{1,0:T(8,128)(2,1)S(1)}, u32[]{:S(2)}, u32[]{:S(2)}) %collective-permute-start.4) | collective-permute-done | bytes 131104 | tf_op jit(solution)/shard_map/ppermute | solution.py:75
  96.2 8.6 %collective-permute-start.10 = (f32[1,4,256,130]{2,1,3,0:T(4,128)S(1)}, f32[1,4,256,130]{2,1,3,0:T(4,128)S(1)}, u32[]{:S(2)}, u32[]{:S(2)}) collective-permute-start(f32[1,4,256,130]{2,1,3,0:T(4,128)S(1)} %copy.226), channel_id=1, source_target_pairs={{4,0},{5,1},{6,2},{7,3},{12,8},{13,9},{14,10},{15,11},{20,16},{21,... | collective-permute-start | bytes 1597448 | tf_op jit(solution)/shard_map/ppermute | solution.py:110
  107.8 3.2 %convolution_convert_fusion = bf16[256,3584]{1,0:T(8,128)(2,1)S(1)} fusion(bf16[256,512]{0,1:T(8,128)(2,1)S(1)} %bitcast.500, bf16[1,512,3584]{2,1,0:T(8,128)(2,1)} %param.14), kind=kOutput, calls=%fused_computation.1 | convolution fusion | flops 940441600 | bytes 5767168 | tf_op jit(solution)/shard_map/dot_general | solution.py:124
  125.0 16.3 %collective-permute-done.17 = bf16[256,896]{1,0:T(8,128)(2,1)S(1)} collective-permute-done((bf16[256,896]{1,0:T(8,128)(2,1)S(1)}, bf16[256,896]{1,0:T(8,128)(2,1)S(1)}, u32[]{:S(2)}, u32[]{:S(2)}) %collective-permute-start.17) | collective-permute-done | bytes 458784 | tf_op jit(solution)/shard_map/ppermute | solution.py:141
  142.4 4.8 %collective-permute-done.15 = bf16[256,896]{1,0:T(8,128)(2,1)S(1)} collective-permute-done((bf16[256,896]{1,0:T(8,128)(2,1)S(1)}, bf16[256,896]{1,0:T(8,128)(2,1)S(1)}, u32[]{:S(2)}, u32[]{:S(2)}) %collective-permute-start.15) | collective-permute-done | bytes 458784 | tf_op jit(solution)/shard_map/ppermute | solution.py:141
  148.8 2.4 gather_fusion
  153.6 2.7 %copy.231 = bf16[256,4,896]{0,2,1:T(8,128)(2,1)S(1)} copy(bf16[256,4,896]{2,0,1:T(8,128)(2,1)} %fusion.6) | data formatting | bytes 3670016 | tf_op jit(solution)/shard_map/mul | solution.py:163
  156.4 3.3 %fusion.44 = bf16[256,512]{1,0:T(8,128)(2,1)S(1)} fusion(bf16[256,3584]{0,1:T(8,128)(2,1)S(1)} %bitcast.497, bf16[1,512,3584]{2,1,0:T(8,128)(2,1)} %param.14), kind=kOutput, calls=%fused_computation.64 | convolution fusion | flops 939655168 | bytes 5767168 | tf_op jit(solution)/shard_map/dot_general | solution.py:167
  160.7 8.4 %collective-permute-start.20 = (bf16[1,130,4,128]{3,1,2,0:T(8,128)(2,1)S(1)}, bf16[1,130,4,128]{3,1,2,0:T(8,128)(2,1)S(1)}, u32[]{:S(2)}, u32[]{:S(2)}) collective-permute-start(bf16[1,130,4,128]{3,1,2,0:T(8,128)(2,1)S(1)} %pad_maximum_fusion.3), channel_id=1, source_target_pairs={{4,12},{12,20},{20,28},{28,36},{36,44},{44,52},{52,60},{60,68},{68... | collective-permute-start | bytes 399368 | tf_op jit(solution)/shard_map/ppermute | solution.py:20
  174.4 9.8 %collective-permute-start.21 = (bf16[1,130,4,128]{3,1,2,0:T(8,128)(2,1)S(1)}, bf16[1,130,4,128]{3,1,2,0:T(8,128)(2,1)S(1)}, u32[]{:S(2)}, u32[]{:S(2)}) collective-permute-start(bf16[1,130,4,128]{3,1,2,0:T(8,128)(2,1)S(1)} %pad_maximum_fusion.4), channel_id=1, source_target_pairs={{4,28},{12,36},{20,44},{28,52},{36,60},{44,68},{52,76},{60,84},{68... | collective-permute-start | bytes 399368 | tf_op jit(solution)/shard_map/ppermute | solution.py:20
  186.6 14.6 %collective-permute-start.22 = (bf16[1,130,4,128]{3,1,2,0:T(8,128)(2,1)S(1)}, bf16[1,130,4,128]{3,1,2,0:T(8,128)(2,1)S(1)}, u32[]{:S(2)}, u32[]{:S(2)}) collective-permute-start(bf16[1,130,4,128]{3,1,2,0:T(8,128)(2,1)S(1)} %pad_maximum_fusion.5), channel_id=1, source_target_pairs={{4,52},{12,60},{20,68},{28,76},{36,84},{44,92},{52,100},{60,108},{... | collective-permute-start | bytes 399368 | tf_op jit(solution)/shard_map/ppermute | solution.py:20
  201.3 3.3 %collective-permute-done.22 = bf16[1,130,4,128]{3,1,2,0:T(8,128)(2,1)S(1)} collective-permute-done((bf16[1,130,4,128]{3,1,2,0:T(8,128)(2,1)S(1)}, bf16[1,130,4,128]{3,1,2,0:T(8,128)(2,1)S(1)}, u32[]{:S(2)}, u32[]{:S(2)}) %collective-permute-start.22) | collective-permute-done | bytes 133152 | tf_op jit(solution)/shard_map/ppermute | solution.py:20
  204.9 8.9 %collective-permute-start.23 = (bf16[1,130,4,128]{3,1,2,0:T(8,128)(2,1)S(1)}, bf16[1,130,4,128]{3,1,2,0:T(8,128)(2,1)}, u32[]{:S(2)}, u32[]{:S(2)}) collective-permute-start(bf16[1,130,4,128]{3,1,2,0:T(8,128)(2,1)S(1)} %pad_maximum_fusion.6), channel_id=1, source_target_pairs={{4,100},{12,108},{20,116},{28,124},{36,132},{44,140},{52,148},{60,... | collective-permute-start | bytes 399368 | tf_op jit(solution)/shard_map/ppermute | solution.py:20
  216.2 7.1 %collective-permute-start.24 = (bf16[1,130,4,128]{3,1,2,0:T(8,128)(2,1)S(1)}, bf16[1,130,4,128]{3,1,2,0:T(8,128)(2,1)S(1)}, u32[]{:S(2)}, u32[]{:S(2)}) collective-permute-start(bf16[1,130,4,128]{3,1,2,0:T(8,128)(2,1)S(1)} %pad_maximum_fusion.7), channel_id=1, source_target_pairs={{4,196},{12,204},{20,212},{28,220},{36,228},{44,236},{52,244},{60,... | collective-permute-start | bytes 399368 | tf_op jit(solution)/shard_map/ppermute | solution.py:20
  225.6 16.2 %collective-permute-start.25 = (bf16[1,130,4,128]{3,1,2,0:T(8,128)(2,1)S(1)}, bf16[1,130,4,128]{3,1,2,0:T(8,128)(2,1)S(1)}, u32[]{:S(2)}, u32[]{:S(2)}) collective-permute-start(bf16[1,130,4,128]{3,1,2,0:T(8,128)(2,1)S(1)} %pad_maximum_fusion.8), channel_id=1, source_target_pairs={{4,388},{12,396},{20,404},{28,412},{36,420},{44,428},{52,436},{60,... | collective-permute-start | bytes 399368 | tf_op jit(solution)/shard_map/ppermute | solution.py:20
  (195 shorter events, 65.7 us)
Async XLA Ops:
  1.7 12.9 %collective-permute-start = (bf16[256,640]{1,0:T(8,128)(2,1)S(1)}, bf16[256,640]{1,0:T(8,128)(2,1)S(1)}, u32[]{:S(2)}, u32[]{:S(2)}) collective-permute-start(bf16[256,640]{1,0:T(8,128)(2,1)S(1)} %pad_maximum_fusion.2), channel_id=1, source_target_pairs={{0,4},{1,5},{2,6},{3,7},{8,12},{9,13},{10,14},{11,15},{16,20},{17,... | collective-permute-start | bytes 983048 | tf_op jit(solution)/shard_map/ppermute | solution.py:52
  16.3 74.5 %collective-permute-start.8 = (bf16[256,256]{1,0:T(8,128)(2,1)S(1)}, bf16[256,256]{1,0:T(8,128)(2,1)S(1)}, u32[]{:S(2)}, u32[]{:S(2)}) collective-permute-start(bf16[256,256]{1,0:T(8,128)(2,1)S(1)} %pad_maximum_fusion.9), channel_id=1, source_target_pairs={{0,112},{8,120},{16,128},{24,136},{32,144},{40,152},{48,160},{56,1... | collective-permute-start | bytes 393224 | tf_op jit(solution)/shard_map/ppermute | solution.py:75
  22.9 67.5 %collective-permute-start.7 = (bf16[256,256]{1,0:T(8,128)(2,1)S(1)}, bf16[256,256]{1,0:T(8,128)(2,1)S(1)}, u32[]{:S(2)}, u32[]{:S(2)}) collective-permute-start(bf16[256,256]{1,0:T(8,128)(2,1)S(1)} %pad_maximum_fusion.9), channel_id=1, source_target_pairs={{0,96},{8,104},{16,112},{24,120},{32,128},{40,136},{48,144},{56,15... | collective-permute-start | bytes 393224 | tf_op jit(solution)/shard_map/ppermute | solution.py:75
  29.1 60.7 %collective-permute-start.6 = (bf16[256,256]{1,0:T(8,128)(2,1)S(1)}, bf16[256,256]{1,0:T(8,128)(2,1)S(1)}, u32[]{:S(2)}, u32[]{:S(2)}) collective-permute-start(bf16[256,256]{1,0:T(8,128)(2,1)S(1)} %pad_maximum_fusion.9), channel_id=1, source_target_pairs={{0,80},{8,88},{16,96},{24,104},{32,112},{40,120},{48,128},{56,136}... | collective-permute-start | bytes 393224 | tf_op jit(solution)/shard_map/ppermute | solution.py:75
  31.4 57.8 %collective-permute-start.5 = (bf16[256,256]{1,0:T(8,128)(2,1)S(1)}, bf16[256,256]{1,0:T(8,128)(2,1)S(1)}, u32[]{:S(2)}, u32[]{:S(2)}) collective-permute-start(bf16[256,256]{1,0:T(8,128)(2,1)S(1)} %pad_maximum_fusion.9), channel_id=1, source_target_pairs={{0,64},{8,72},{16,80},{24,88},{32,96},{40,104},{48,112},{56,120},{... | collective-permute-start | bytes 393224 | tf_op jit(solution)/shard_map/ppermute | solution.py:75
  39.6 3.2 %collective-permute-start.1 = (bf16[256,256]{1,0:T(8,128)(2,1)S(1)}, bf16[256,256]{1,0:T(8,128)(2,1)S(1)}, u32[]{:S(2)}, u32[]{:S(2)}) collective-permute-start(bf16[256,256]{1,0:T(8,128)(2,1)S(1)} %pad_maximum_fusion.9), channel_id=1, source_target_pairs={{4,12},{12,20},{20,28},{28,36},{36,44},{44,52},{52,60},{60,68},{68... | collective-permute-start | bytes 393224 | tf_op jit(solution)/shard_map/ppermute | solution.py:75
  42.8 7.9 %collective-permute-start.2 = (bf16[256,256]{1,0:T(8,128)(2,1)S(1)}, bf16[256,256]{1,0:T(8,128)(2,1)S(1)}, u32[]{:S(2)}, u32[]{:S(2)}) collective-permute-start(bf16[256,256]{1,0:T(8,128)(2,1)S(1)} %pad_maximum_fusion.9), channel_id=1, source_target_pairs={{0,16},{8,24},{16,32},{24,40},{32,48},{40,56},{48,64},{56,72},{64,... | collective-permute-start | bytes 393224 | tf_op jit(solution)/shard_map/ppermute | solution.py:75
  50.7 14.8 %collective-permute-start.3 = (bf16[256,256]{1,0:T(8,128)(2,1)S(1)}, bf16[256,256]{1,0:T(8,128)(2,1)S(1)}, u32[]{:S(2)}, u32[]{:S(2)}) collective-permute-start(bf16[256,256]{1,0:T(8,128)(2,1)S(1)} %pad_maximum_fusion.9), channel_id=1, source_target_pairs={{0,32},{8,40},{16,48},{24,56},{32,64},{40,72},{48,80},{56,88},{64,... | collective-permute-start | bytes 393224 | tf_op jit(solution)/shard_map/ppermute | solution.py:75
  65.6 22.4 %collective-permute-start.4 = (bf16[256,256]{1,0:T(8,128)(2,1)S(1)}, bf16[256,256]{1,0:T(8,128)(2,1)S(1)}, u32[]{:S(2)}, u32[]{:S(2)}) collective-permute-start(bf16[256,256]{1,0:T(8,128)(2,1)S(1)} %pad_maximum_fusion.9), channel_id=1, source_target_pairs={{0,48},{8,56},{16,64},{24,72},{32,80},{40,88},{48,96},{56,104},{64... | collective-permute-start | bytes 393224 | tf_op jit(solution)/shard_map/ppermute | solution.py:75
  88.0 3.5 %collective-permute-start.9 = (bf16[256,256]{1,0:T(8,128)(2,1)S(1)}, bf16[256,256]{1,0:T(8,128)(2,1)S(1)}, u32[]{:S(2)}, u32[]{:S(2)}) collective-permute-start(bf16[256,256]{1,0:T(8,128)(2,1)S(1)} %pad_maximum_fusion.9), channel_id=1, source_target_pairs={{0,128},{8,136},{16,144},{24,152},{32,160},{40,168},{48,176},{56,1... | collective-permute-start | bytes 393224 | tf_op jit(solution)/shard_map/ppermute | solution.py:75
  96.2 11.4 %collective-permute-start.10 = (f32[1,4,256,130]{2,1,3,0:T(4,128)S(1)}, f32[1,4,256,130]{2,1,3,0:T(4,128)S(1)}, u32[]{:S(2)}, u32[]{:S(2)}) collective-permute-start(f32[1,4,256,130]{2,1,3,0:T(4,128)S(1)} %copy.226), channel_id=1, source_target_pairs={{4,0},{5,1},{6,2},{7,3},{12,8},{13,9},{14,10},{15,11},{20,16},{21,... | collective-permute-start | bytes 1597448 | tf_op jit(solution)/shard_map/ppermute | solution.py:110
  112.0 4.8 %collective-permute-start.11 = (bf16[256,896]{1,0:T(8,128)(2,1)}, bf16[256,896]{1,0:T(8,128)(2,1)}, u32[]{:S(2)}, u32[]{:S(2)}) collective-permute-start(bf16[256,896]{1,0:T(8,128)(2,1)} %get-tuple-element.37), channel_id=1, source_target_pairs={{0,1},{1,2},{2,3},{3,0},{8,9},{9,10},{10,11},{11,8},{16,17},{17,18... | collective-permute-start | bytes 1376264 | tf_op jit(solution)/shard_map/ppermute | solution.py:137
  118.4 22.8 %collective-permute-start.17 = (bf16[256,896]{1,0:T(8,128)(2,1)S(1)}, bf16[256,896]{1,0:T(8,128)(2,1)S(1)}, u32[]{:S(2)}, u32[]{:S(2)}) collective-permute-start(bf16[256,896]{1,0:T(8,128)(2,1)S(1)} %add_convert_fusion), channel_id=1, source_target_pairs={{0,7},{1,4},{2,5},{3,6},{8,15},{9,12},{10,13},{11,14},{16,23},{17,... | collective-permute-start | bytes 1376264 | tf_op jit(solution)/shard_map/ppermute | solution.py:141
  119.7 22.7 %collective-permute-start.16 = (bf16[256,896]{1,0:T(8,128)(2,1)S(1)}, bf16[256,896]{1,0:T(8,128)(2,1)S(1)}, u32[]{:S(2)}, u32[]{:S(2)}) collective-permute-start(bf16[256,896]{1,0:T(8,128)(2,1)S(1)} %add_convert_fusion), channel_id=1, source_target_pairs={{0,6},{1,7},{2,4},{3,5},{8,14},{9,15},{10,12},{11,13},{16,22},{17,... | collective-permute-start | bytes 1376264 | tf_op jit(solution)/shard_map/ppermute | solution.py:141
  121.0 26.2 %collective-permute-start.15 = (bf16[256,896]{1,0:T(8,128)(2,1)S(1)}, bf16[256,896]{1,0:T(8,128)(2,1)S(1)}, u32[]{:S(2)}, u32[]{:S(2)}) collective-permute-start(bf16[256,896]{1,0:T(8,128)(2,1)S(1)} %add_convert_fusion), channel_id=1, source_target_pairs={{0,5},{1,6},{2,7},{3,4},{8,13},{9,14},{10,15},{11,12},{16,21},{17,... | collective-permute-start | bytes 1376264 | tf_op jit(solution)/shard_map/ppermute | solution.py:141
  122.3 24.9 %collective-permute-start.14 = (bf16[256,896]{1,0:T(8,128)(2,1)S(1)}, bf16[256,896]{1,0:T(8,128)(2,1)S(1)}, u32[]{:S(2)}, u32[]{:S(2)}) collective-permute-start(bf16[256,896]{1,0:T(8,128)(2,1)S(1)} %add_convert_fusion), channel_id=1, source_target_pairs={{0,4},{1,5},{2,6},{3,7},{8,12},{9,13},{10,14},{11,15},{16,20},{17,... | collective-permute-start | bytes 1376264 | tf_op jit(solution)/shard_map/ppermute | solution.py:141
  160.7 11.2 %collective-permute-start.20 = (bf16[1,130,4,128]{3,1,2,0:T(8,128)(2,1)S(1)}, bf16[1,130,4,128]{3,1,2,0:T(8,128)(2,1)S(1)}, u32[]{:S(2)}, u32[]{:S(2)}) collective-permute-start(bf16[1,130,4,128]{3,1,2,0:T(8,128)(2,1)S(1)} %pad_maximum_fusion.3), channel_id=1, source_target_pairs={{4,12},{12,20},{20,28},{28,36},{36,44},{44,52},{52,60},{60,68},{68... | collective-permute-start | bytes 399368 | tf_op jit(solution)/shard_map/ppermute | solution.py:20
  169.1 3.5 %collective-permute-start.19 = (bf16[1,130,4,128]{3,1,2,0:T(8,128)(2,1)S(1)}, bf16[1,130,4,128]{3,1,2,0:T(8,128)(2,1)S(1)}, u32[]{:S(2)}, u32[]{:S(2)}) collective-permute-start(bf16[1,130,4,128]{3,1,2,0:T(8,128)(2,1)S(1)} %pad_maximum_fusion.3), channel_id=1, source_target_pairs={{4,20},{12,28},{20,36},{28,44},{36,52},{44,60},{52,68},{60,76},{68... | collective-permute-start | bytes 399368 | tf_op jit(solution)/shard_map/ppermute | solution.py:20
  170.4 3.7 %collective-permute-start.18 = (bf16[1,130,4,128]{3,1,2,0:T(8,128)(2,1)S(1)}, bf16[1,130,4,128]{3,1,2,0:T(8,128)(2,1)S(1)}, u32[]{:S(2)}, u32[]{:S(2)}) collective-permute-start(bf16[1,130,4,128]{3,1,2,0:T(8,128)(2,1)S(1)} %pad_maximum_fusion.3), channel_id=1, source_target_pairs={{4,28},{12,36},{20,44},{28,52},{36,60},{44,68},{52,76},{60,84},{68... | collective-permute-start | bytes 399368 | tf_op jit(solution)/shard_map/ppermute | solution.py:20
  174.4 12.1 %collective-permute-start.21 = (bf16[1,130,4,128]{3,1,2,0:T(8,128)(2,1)S(1)}, bf16[1,130,4,128]{3,1,2,0:T(8,128)(2,1)S(1)}, u32[]{:S(2)}, u32[]{:S(2)}) collective-permute-start(bf16[1,130,4,128]{3,1,2,0:T(8,128)(2,1)S(1)} %pad_maximum_fusion.4), channel_id=1, source_target_pairs={{4,28},{12,36},{20,44},{28,52},{36,60},{44,68},{52,76},{60,84},{68... | collective-permute-start | bytes 399368 | tf_op jit(solution)/shard_map/ppermute | solution.py:20
  186.6 18.0 %collective-permute-start.22 = (bf16[1,130,4,128]{3,1,2,0:T(8,128)(2,1)S(1)}, bf16[1,130,4,128]{3,1,2,0:T(8,128)(2,1)S(1)}, u32[]{:S(2)}, u32[]{:S(2)}) collective-permute-start(bf16[1,130,4,128]{3,1,2,0:T(8,128)(2,1)S(1)} %pad_maximum_fusion.5), channel_id=1, source_target_pairs={{4,52},{12,60},{20,68},{28,76},{36,84},{44,92},{52,100},{60,108},{... | collective-permute-start | bytes 399368 | tf_op jit(solution)/shard_map/ppermute | solution.py:20
  204.9 10.3 %collective-permute-start.23 = (bf16[1,130,4,128]{3,1,2,0:T(8,128)(2,1)S(1)}, bf16[1,130,4,128]{3,1,2,0:T(8,128)(2,1)}, u32[]{:S(2)}, u32[]{:S(2)}) collective-permute-start(bf16[1,130,4,128]{3,1,2,0:T(8,128)(2,1)S(1)} %pad_maximum_fusion.6), channel_id=1, source_target_pairs={{4,100},{12,108},{20,116},{28,124},{36,132},{44,140},{52,148},{60,... | collective-permute-start | bytes 399368 | tf_op jit(solution)/shard_map/ppermute | solution.py:20
  216.2 9.1 %collective-permute-start.24 = (bf16[1,130,4,128]{3,1,2,0:T(8,128)(2,1)S(1)}, bf16[1,130,4,128]{3,1,2,0:T(8,128)(2,1)S(1)}, u32[]{:S(2)}, u32[]{:S(2)}) collective-permute-start(bf16[1,130,4,128]{3,1,2,0:T(8,128)(2,1)S(1)} %pad_maximum_fusion.7), channel_id=1, source_target_pairs={{4,196},{12,204},{20,212},{28,220},{36,228},{44,236},{52,244},{60,... | collective-permute-start | bytes 399368 | tf_op jit(solution)/shard_map/ppermute | solution.py:20
  225.6 18.2 %collective-permute-start.25 = (bf16[1,130,4,128]{3,1,2,0:T(8,128)(2,1)S(1)}, bf16[1,130,4,128]{3,1,2,0:T(8,128)(2,1)S(1)}, u32[]{:S(2)}, u32[]{:S(2)}) collective-permute-start(bf16[1,130,4,128]{3,1,2,0:T(8,128)(2,1)S(1)} %pad_maximum_fusion.8), channel_id=1, source_target_pairs={{4,388},{12,396},{20,404},{28,412},{36,420},{44,428},{52,436},{60,... | collective-permute-start | bytes 399368 | tf_op jit(solution)/shard_map/ppermute | solution.py:20
  (15 other events, 207.8 us)

commit v6 on v5

--- a/solution.py
+++ b/solution.py
@@ -198,11 +198,17 @@
 
     total_rows = jnp.broadcast_to(cumulated[-1][:, None, :, None], (key_heads, 1, group_size, head_size))
     own_entry = jnp.concatenate([total_rows, fresh_state], axis=1)
-    entry = chain(chain(sent_along(own_entry, 3), sent_along(own_entry, 2)), sent_along(own_entry, 1))
-    reach = 3
+    entry = sent_along(own_entry, 1)
+    for times in range(2, 5):
+        entry = chain(sent_along(own_entry, times), entry)
+    reach = 4
     while reach < shards:
-        entry = chain(sent_along(entry, reach), entry)
-        reach *= 2
+        spread = 4 if reach < 16 else -(-shards // reach)
+        joined = entry
+        for times in range(1, spread):
+            joined = chain(sent_along(entry, times * reach), joined)
+        entry = joined
+        reach *= spread
     incoming = entry[:, 1:]
 
     query_narrow = queries[0].reshape(row_count, key_heads, group_size, head_size)

time: 247 us -> 244 us (0.988)
  waiting for transfers between devices: 49.9 us -> 41.5 us
  other arithmetic: 24.1 us -> 28.6 us
    ppermute x8 -> x12, waiting for transfers between devices: 11.1 us -> 5.46 us  [passed_along(): return lax.ppermute(x, ('ctx', 'section'), pairs)]
    convert_element_type x7 -> x11, other arithmetic: 1.05 us -> 3.85 us  [sent_along(): moved = passed_along(narrow, by, 1).astype(jnp.float32)]
    ppermute x4, waiting for transfers between devices: 22.2 us -> 19.5 us  [body(): lax.ppermute(own_hidden, ('section', 'tp'), [(m, members + (m + step) % m...]
    ppermute x8 -> x12, starting transfers between devices: 67.8 us -> 66.8 us  [passed_along(): return lax.ppermute(x, ('ctx', 'section'), pairs)]
  transfers between devices with their start and end apart: 26 -> 30, of which waited for: 15 -> 11; matrix products, arithmetic and copies ran while one was open for 8% -> 10% of each run, Pallas kernels for 0% -> 0%
where the time goes in v6:
time: 244 us; the launch traced here: 242 us
  starting transfers between devices  144 us (59%)
  waiting for transfers between devices  41.5 us (17%)
  other arithmetic  28.6 us (12%)
  matrix products  14.4 us (6%)
  local copies, waits for them, and re-layouts  11.7 us (5%)
    ppermute x12, starting transfers between devices, passed_along(): return lax.ppermute(x, ('ctx', 'section'), pairs)  66.8 us
    ppermute x9, starting transfers between devices, body(): joined = lax.ppermute(packed, ('ctx', 'section'), pairs)  57.5 us
    ppermute x4, waiting for transfers between devices, body(): lax.ppermute(own_hidden, ('section', 'tp'), [(m, members + (m + step) % m...  19.5 us
    ppermute x9, waiting for transfers between devices, body(): joined = lax.ppermute(packed, ('ctx', 'section'), pairs)  13.6 us
    ppermute x1, starting transfers between devices, body(): lax.ppermute(jnp.concatenate([running, totals[..., None], best[..., None]...  8.62 us
    and x9, other arithmetic, body(): key_valid = (source >= 0) & (positions < lengths[jnp.maximum(source, 0)])  5.72 us
    ppermute x12, waiting for transfers between devices, passed_along(): return lax.ppermute(x, ('ctx', 'section'), pairs)  5.46 us
    ppermute x4, starting transfers between devices, body(): lax.ppermute(own_hidden, ('section', 'tp'), [(m, members + (m + step) % m...  5.17 us
  transfers between devices with their start and end apart: 30, of which 11 were waited for; matrix products, arithmetic and copies ran while one was open for 10% of the time, Pallas kernels for 0%

profile of v6, /device:TPU:1, one launch (start us, length us, event | category | flops | bytes accessed | tf_op | source)
XLA Modules:
  0.0 241.7 jit_solution(2238212052070794969)
XLA Ops:
  11.7 3.0 %collective-permute-done = bf16[256,640]{1,0:T(8,128)(2,1)S(1)} collective-permute-done((bf16[256,640]{1,0:T(8,128)(2,1)S(1)}, bf16[256,640]{1,0:T(8,128)(2,1)S(1)}, u32[]{:S(2)}, u32[]{:S(2)}) %collective-permute-start) | collective-permute-done | bytes 327712 | tf_op jit(solution)/shard_map/ppermute | solution.py:52
  16.3 6.5 %collective-permute-start.8 = (bf16[256,256]{1,0:T(8,128)(2,1)S(1)}, bf16[256,256]{1,0:T(8,128)(2,1)S(1)}, u32[]{:S(2)}, u32[]{:S(2)}) collective-permute-start(bf16[256,256]{1,0:T(8,128)(2,1)S(1)} %pad_maximum_fusion.6), channel_id=1, source_target_pairs={{0,112},{8,120},{16,128},{24,136},{32,144},{40,152},{48,160},{56,1... | collective-permute-start | bytes 393224 | tf_op jit(solution)/shard_map/ppermute | solution.py:75
  22.9 6.2 %collective-permute-start.7 = (bf16[256,256]{1,0:T(8,128)(2,1)S(1)}, bf16[256,256]{1,0:T(8,128)(2,1)S(1)}, u32[]{:S(2)}, u32[]{:S(2)}) collective-permute-start(bf16[256,256]{1,0:T(8,128)(2,1)S(1)} %pad_maximum_fusion.6), channel_id=1, source_target_pairs={{0,96},{8,104},{16,112},{24,120},{32,128},{40,136},{48,144},{56,15... | collective-permute-start | bytes 393224 | tf_op jit(solution)/shard_map/ppermute | solution.py:75
  31.4 8.2 %collective-permute-start.5 = (bf16[256,256]{1,0:T(8,128)(2,1)S(1)}, bf16[256,256]{1,0:T(8,128)(2,1)S(1)}, u32[]{:S(2)}, u32[]{:S(2)}) collective-permute-start(bf16[256,256]{1,0:T(8,128)(2,1)S(1)} %pad_maximum_fusion.6), channel_id=1, source_target_pairs={{0,64},{8,72},{16,80},{24,88},{32,96},{40,104},{48,112},{56,120},{... | collective-permute-start | bytes 393224 | tf_op jit(solution)/shard_map/ppermute | solution.py:75
  42.8 5.0 %collective-permute-start.2 = (bf16[256,256]{1,0:T(8,128)(2,1)S(1)}, bf16[256,256]{1,0:T(8,128)(2,1)S(1)}, u32[]{:S(2)}, u32[]{:S(2)}) collective-permute-start(bf16[256,256]{1,0:T(8,128)(2,1)S(1)} %pad_maximum_fusion.6), channel_id=1, source_target_pairs={{0,16},{8,24},{16,32},{24,40},{32,48},{40,56},{48,64},{56,72},{64,... | collective-permute-start | bytes 393224 | tf_op jit(solution)/shard_map/ppermute | solution.py:75
  48.2 2.5 %collective-permute-done.2 = bf16[256,256]{1,0:T(8,128)(2,1)S(1)} collective-permute-done((bf16[256,256]{1,0:T(8,128)(2,1)S(1)}, bf16[256,256]{1,0:T(8,128)(2,1)S(1)}, u32[]{:S(2)}, u32[]{:S(2)}) %collective-permute-start.2) | collective-permute-done | bytes 131104 | tf_op jit(solution)/shard_map/ppermute | solution.py:75
  50.7 12.9 %collective-permute-start.3 = (bf16[256,256]{1,0:T(8,128)(2,1)S(1)}, bf16[256,256]{1,0:T(8,128)(2,1)S(1)}, u32[]{:S(2)}, u32[]{:S(2)}) collective-permute-start(bf16[256,256]{1,0:T(8,128)(2,1)S(1)} %pad_maximum_fusion.6), channel_id=1, source_target_pairs={{0,32},{8,40},{16,48},{24,56},{32,64},{40,72},{48,80},{56,88},{64,... | collective-permute-start | bytes 393224 | tf_op jit(solution)/shard_map/ppermute | solution.py:75
  65.6 14.5 %collective-permute-start.4 = (bf16[256,256]{1,0:T(8,128)(2,1)S(1)}, bf16[256,256]{1,0:T(8,128)(2,1)S(1)}, u32[]{:S(2)}, u32[]{:S(2)}) collective-permute-start(bf16[256,256]{1,0:T(8,128)(2,1)S(1)} %pad_maximum_fusion.6), channel_id=1, source_target_pairs={{0,48},{8,56},{16,64},{24,72},{32,80},{40,88},{48,96},{56,104},{64... | collective-permute-start | bytes 393224 | tf_op jit(solution)/shard_map/ppermute | solution.py:75
  80.4 7.6 %collective-permute-done.4 = bf16[256,256]{1,0:T(8,128)(2,1)S(1)} collective-permute-done((bf16[256,256]{1,0:T(8,128)(2,1)S(1)}, bf16[256,256]{1,0:T(8,128)(2,1)S(1)}, u32[]{:S(2)}, u32[]{:S(2)}) %collective-permute-start.4) | collective-permute-done | bytes 131104 | tf_op jit(solution)/shard_map/ppermute | solution.py:75
  96.2 8.6 %collective-permute-start.10 = (f32[1,4,256,130]{2,1,3,0:T(4,128)S(1)}, f32[1,4,256,130]{2,1,3,0:T(4,128)S(1)}, u32[]{:S(2)}, u32[]{:S(2)}) collective-permute-start(f32[1,4,256,130]{2,1,3,0:T(4,128)S(1)} %copy.226), channel_id=1, source_target_pairs={{4,0},{5,1},{6,2},{7,3},{12,8},{13,9},{14,10},{15,11},{20,16},{21,... | collective-permute-start | bytes 1597448 | tf_op jit(solution)/shard_map/ppermute | solution.py:110
  107.8 3.2 %convolution_convert_fusion = bf16[256,3584]{1,0:T(8,128)(2,1)S(1)} fusion(bf16[256,512]{0,1:T(8,128)(2,1)S(1)} %bitcast.504, bf16[1,512,3584]{2,1,0:T(8,128)(2,1)} %param.14), kind=kOutput, calls=%fused_computation.1 | convolution fusion | flops 940441600 | bytes 5767168 | tf_op jit(solution)/shard_map/dot_general | solution.py:124
  127.6 13.5 %collective-permute-done.17 = bf16[256,896]{1,0:T(8,128)(2,1)S(1)} collective-permute-done((bf16[256,896]{1,0:T(8,128)(2,1)S(1)}, bf16[256,896]{1,0:T(8,128)(2,1)S(1)}, u32[]{:S(2)}, u32[]{:S(2)}) %collective-permute-start.17) | collective-permute-done | bytes 458784 | tf_op jit(solution)/shard_map/ppermute | solution.py:141
  142.3 4.8 %collective-permute-done.15 = bf16[256,896]{1,0:T(8,128)(2,1)S(1)} collective-permute-done((bf16[256,896]{1,0:T(8,128)(2,1)S(1)}, bf16[256,896]{1,0:T(8,128)(2,1)S(1)}, u32[]{:S(2)}, u32[]{:S(2)}) %collective-permute-start.15) | collective-permute-done | bytes 458784 | tf_op jit(solution)/shard_map/ppermute | solution.py:141
  148.6 2.4 gather_fusion
  153.5 2.7 %copy.231 = bf16[256,4,896]{0,2,1:T(8,128)(2,1)S(1)} copy(bf16[256,4,896]{2,0,1:T(8,128)(2,1)} %fusion.6) | data formatting | bytes 3670016 | tf_op jit(solution)/shard_map/mul | solution.py:163
  156.3 3.3 %fusion.44 = bf16[256,512]{1,0:T(8,128)(2,1)S(1)} fusion(bf16[256,3584]{0,1:T(8,128)(2,1)S(1)} %bitcast.501, bf16[1,512,3584]{2,1,0:T(8,128)(2,1)} %param.14), kind=kOutput, calls=%fused_computation.64 | convolution fusion | flops 939655168 | bytes 5767168 | tf_op jit(solution)/shard_map/dot_general | solution.py:167
  160.6 9.1 %collective-permute-start.21 = (bf16[1,130,4,128]{3,1,2,0:T(8,128)(2,1)S(1)}, bf16[1,130,4,128]{3,1,2,0:T(8,128)(2,1)}, u32[]{:S(2)}, u32[]{:S(2)}) collective-permute-start(bf16[1,130,4,128]{3,1,2,0:T(8,128)(2,1)S(1)} %pad_maximum_fusion.3), channel_id=1, source_target_pairs={{4,12},{12,20},{20,28},{28,36},{36,44},{44,52},{52,60},{60,68},{68... | collective-permute-start | bytes 399368 | tf_op jit(solution)/shard_map/ppermute | solution.py:20
  173.6 7.1 %collective-permute-start.18 = (bf16[1,130,4,128]{3,1,2,0:T(8,128)(2,1)S(1)}, bf16[1,130,4,128]{3,1,2,0:T(8,128)(2,1)}, u32[]{:S(2)}, u32[]{:S(2)}) collective-permute-start(bf16[1,130,4,128]{3,1,2,0:T(8,128)(2,1)S(1)} %pad_maximum_fusion.3), channel_id=1, source_target_pairs={{4,36},{12,44},{20,52},{28,60},{36,68},{44,76},{52,84},{60,92},{68... | collective-permute-start | bytes 399368 | tf_op jit(solution)/shard_map/ppermute | solution.py:20
  185.4 6.3 %collective-permute-start.24 = (bf16[1,130,4,128]{3,1,2,0:T(8,128)(2,1)S(1)}, bf16[1,130,4,128]{3,1,2,0:T(8,128)(2,1)S(1)}, u32[]{:S(2)}, u32[]{:S(2)}) collective-permute-start(bf16[1,130,4,128]{3,1,2,0:T(8,128)(2,1)S(1)} %pad_maximum_fusion.4), channel_id=1, source_target_pairs={{4,36},{12,44},{20,52},{28,60},{36,68},{44,76},{52,84},{60,92},{68... | collective-permute-start | bytes 399368 | tf_op jit(solution)/shard_map/ppermute | solution.py:20
  191.7 9.9 %collective-permute-start.23 = (bf16[1,130,4,128]{3,1,2,0:T(8,128)(2,1)S(1)}, bf16[1,130,4,128]{3,1,2,0:T(8,128)(2,1)S(1)}, u32[]{:S(2)}, u32[]{:S(2)}) collective-permute-start(bf16[1,130,4,128]{3,1,2,0:T(8,128)(2,1)S(1)} %pad_maximum_fusion.4), channel_id=1, source_target_pairs={{4,68},{12,76},{20,84},{28,92},{36,100},{44,108},{52,116},{60,124}... | collective-permute-start | bytes 399368 | tf_op jit(solution)/shard_map/ppermute | solution.py:20
  201.7 7.4 %collective-permute-start.22 = (bf16[1,130,4,128]{3,1,2,0:T(8,128)(2,1)S(1)}, bf16[1,130,4,128]{3,1,2,0:T(8,128)(2,1)S(1)}, u32[]{:S(2)}, u32[]{:S(2)}) collective-permute-start(bf16[1,130,4,128]{3,1,2,0:T(8,128)(2,1)S(1)} %pad_maximum_fusion.4), channel_id=1, source_target_pairs={{4,100},{12,108},{20,116},{28,124},{36,132},{44,140},{52,148},{60,... | collective-permute-start | bytes 399368 | tf_op jit(solution)/shard_map/ppermute | solution.py:20
  211.4 6.3 %collective-permute-start.29 = (bf16[1,130,4,128]{3,1,2,0:T(8,128)(2,1)S(1)}, bf16[1,130,4,128]{3,1,2,0:T(8,128)(2,1)S(1)}, u32[]{:S(2)}, u32[]{:S(2)}) collective-permute-start(bf16[1,130,4,128]{3,1,2,0:T(8,128)(2,1)S(1)} %pad_maximum_fusion.5), channel_id=1, source_target_pairs={{4,132},{12,140},{20,148},{28,156},{36,164},{44,172},{52,180},{60,... | collective-permute-start | bytes 399368 | tf_op jit(solution)/shard_map/ppermute | solution.py:20
  217.6 12.9 %collective-permute-start.28 = (bf16[1,130,4,128]{3,1,2,0:T(8,128)(2,1)S(1)}, bf16[1,130,4,128]{3,1,2,0:T(8,128)(2,1)S(1)}, u32[]{:S(2)}, u32[]{:S(2)}) collective-permute-start(bf16[1,130,4,128]{3,1,2,0:T(8,128)(2,1)S(1)} %pad_maximum_fusion.5), channel_id=1, source_target_pairs={{4,260},{12,268},{20,276},{28,284},{36,292},{44,300},{52,308},{60,... | collective-permute-start | bytes 399368 | tf_op jit(solution)/shard_map/ppermute | solution.py:20
  235.0 2.4 collective-permute-done.28
  (203 shorter events, 73.6 us)
Async XLA Ops:
  1.7 12.9 %collective-permute-start = (bf16[256,640]{1,0:T(8,128)(2,1)S(1)}, bf16[256,640]{1,0:T(8,128)(2,1)S(1)}, u32[]{:S(2)}, u32[]{:S(2)}) collective-permute-start(bf16[256,640]{1,0:T(8,128)(2,1)S(1)} %pad_maximum_fusion.2), channel_id=1, source_target_pairs={{0,4},{1,5},{2,6},{3,7},{8,12},{9,13},{10,14},{11,15},{16,20},{17,... | collective-permute-start | bytes 983048 | tf_op jit(solution)/shard_map/ppermute | solution.py:52
  16.3 74.5 %collective-permute-start.8 = (bf16[256,256]{1,0:T(8,128)(2,1)S(1)}, bf16[256,256]{1,0:T(8,128)(2,1)S(1)}, u32[]{:S(2)}, u32[]{:S(2)}) collective-permute-start(bf16[256,256]{1,0:T(8,128)(2,1)S(1)} %pad_maximum_fusion.6), channel_id=1, source_target_pairs={{0,112},{8,120},{16,128},{24,136},{32,144},{40,152},{48,160},{56,1... | collective-permute-start | bytes 393224 | tf_op jit(solution)/shard_map/ppermute | solution.py:75
  22.9 67.5 %collective-permute-start.7 = (bf16[256,256]{1,0:T(8,128)(2,1)S(1)}, bf16[256,256]{1,0:T(8,128)(2,1)S(1)}, u32[]{:S(2)}, u32[]{:S(2)}) collective-permute-start(bf16[256,256]{1,0:T(8,128)(2,1)S(1)} %pad_maximum_fusion.6), channel_id=1, source_target_pairs={{0,96},{8,104},{16,112},{24,120},{32,128},{40,136},{48,144},{56,15... | collective-permute-start | bytes 393224 | tf_op jit(solution)/shard_map/ppermute | solution.py:75
  29.1 60.7 %collective-permute-start.6 = (bf16[256,256]{1,0:T(8,128)(2,1)S(1)}, bf16[256,256]{1,0:T(8,128)(2,1)S(1)}, u32[]{:S(2)}, u32[]{:S(2)}) collective-permute-start(bf16[256,256]{1,0:T(8,128)(2,1)S(1)} %pad_maximum_fusion.6), channel_id=1, source_target_pairs={{0,80},{8,88},{16,96},{24,104},{32,112},{40,120},{48,128},{56,136}... | collective-permute-start | bytes 393224 | tf_op jit(solution)/shard_map/ppermute | solution.py:75
  31.4 57.8 %collective-permute-start.5 = (bf16[256,256]{1,0:T(8,128)(2,1)S(1)}, bf16[256,256]{1,0:T(8,128)(2,1)S(1)}, u32[]{:S(2)}, u32[]{:S(2)}) collective-permute-start(bf16[256,256]{1,0:T(8,128)(2,1)S(1)} %pad_maximum_fusion.6), channel_id=1, source_target_pairs={{0,64},{8,72},{16,80},{24,88},{32,96},{40,104},{48,112},{56,120},{... | collective-permute-start | bytes 393224 | tf_op jit(solution)/shard_map/ppermute | solution.py:75
  42.8 7.9 %collective-permute-start.2 = (bf16[256,256]{1,0:T(8,128)(2,1)S(1)}, bf16[256,256]{1,0:T(8,128)(2,1)S(1)}, u32[]{:S(2)}, u32[]{:S(2)}) collective-permute-start(bf16[256,256]{1,0:T(8,128)(2,1)S(1)} %pad_maximum_fusion.6), channel_id=1, source_target_pairs={{0,16},{8,24},{16,32},{24,40},{32,48},{40,56},{48,64},{56,72},{64,... | collective-permute-start | bytes 393224 | tf_op jit(solution)/shard_map/ppermute | solution.py:75
  50.7 14.8 %collective-permute-start.3 = (bf16[256,256]{1,0:T(8,128)(2,1)S(1)}, bf16[256,256]{1,0:T(8,128)(2,1)S(1)}, u32[]{:S(2)}, u32[]{:S(2)}) collective-permute-start(bf16[256,256]{1,0:T(8,128)(2,1)S(1)} %pad_maximum_fusion.6), channel_id=1, source_target_pairs={{0,32},{8,40},{16,48},{24,56},{32,64},{40,72},{48,80},{56,88},{64,... | collective-permute-start | bytes 393224 | tf_op jit(solution)/shard_map/ppermute | solution.py:75
  65.6 22.4 %collective-permute-start.4 = (bf16[256,256]{1,0:T(8,128)(2,1)S(1)}, bf16[256,256]{1,0:T(8,128)(2,1)S(1)}, u32[]{:S(2)}, u32[]{:S(2)}) collective-permute-start(bf16[256,256]{1,0:T(8,128)(2,1)S(1)} %pad_maximum_fusion.6), channel_id=1, source_target_pairs={{0,48},{8,56},{16,64},{24,72},{32,80},{40,88},{48,96},{56,104},{64... | collective-permute-start | bytes 393224 | tf_op jit(solution)/shard_map/ppermute | solution.py:75
  96.2 11.4 %collective-permute-start.10 = (f32[1,4,256,130]{2,1,3,0:T(4,128)S(1)}, f32[1,4,256,130]{2,1,3,0:T(4,128)S(1)}, u32[]{:S(2)}, u32[]{:S(2)}) collective-permute-start(f32[1,4,256,130]{2,1,3,0:T(4,128)S(1)} %copy.226), channel_id=1, source_target_pairs={{4,0},{5,1},{6,2},{7,3},{12,8},{13,9},{14,10},{15,11},{20,16},{21,... | collective-permute-start | bytes 1597448 | tf_op jit(solution)/shard_map/ppermute | solution.py:110
  118.8 22.3 %collective-permute-start.17 = (bf16[256,896]{1,0:T(8,128)(2,1)S(1)}, bf16[256,896]{1,0:T(8,128)(2,1)S(1)}, u32[]{:S(2)}, u32[]{:S(2)}) collective-permute-start(bf16[256,896]{1,0:T(8,128)(2,1)S(1)} %add_convert_fusion), channel_id=1, source_target_pairs={{0,7},{1,4},{2,5},{3,6},{8,15},{9,12},{10,13},{11,14},{16,23},{17,... | collective-permute-start | bytes 1376264 | tf_op jit(solution)/shard_map/ppermute | solution.py:141
  120.1 22.2 %collective-permute-start.16 = (bf16[256,896]{1,0:T(8,128)(2,1)S(1)}, bf16[256,896]{1,0:T(8,128)(2,1)S(1)}, u32[]{:S(2)}, u32[]{:S(2)}) collective-permute-start(bf16[256,896]{1,0:T(8,128)(2,1)S(1)} %add_convert_fusion), channel_id=1, source_target_pairs={{0,6},{1,7},{2,4},{3,5},{8,14},{9,15},{10,12},{11,13},{16,22},{17,... | collective-permute-start | bytes 1376264 | tf_op jit(solution)/shard_map/ppermute | solution.py:141
  121.4 25.7 %collective-permute-start.15 = (bf16[256,896]{1,0:T(8,128)(2,1)S(1)}, bf16[256,896]{1,0:T(8,128)(2,1)S(1)}, u32[]{:S(2)}, u32[]{:S(2)}) collective-permute-start(bf16[256,896]{1,0:T(8,128)(2,1)S(1)} %add_convert_fusion), channel_id=1, source_target_pairs={{0,5},{1,6},{2,7},{3,4},{8,13},{9,14},{10,15},{11,12},{16,21},{17,... | collective-permute-start | bytes 1376264 | tf_op jit(solution)/shard_map/ppermute | solution.py:141
  122.7 24.4 %collective-permute-start.14 = (bf16[256,896]{1,0:T(8,128)(2,1)S(1)}, bf16[256,896]{1,0:T(8,128)(2,1)S(1)}, u32[]{:S(2)}, u32[]{:S(2)}) collective-permute-start(bf16[256,896]{1,0:T(8,128)(2,1)S(1)} %add_convert_fusion), channel_id=1, source_target_pairs={{0,4},{1,5},{2,6},{3,7},{8,12},{9,13},{10,14},{11,15},{16,20},{17,... | collective-permute-start | bytes 1376264 | tf_op jit(solution)/shard_map/ppermute | solution.py:141
  160.6 20.8 %collective-permute-start.21 = (bf16[1,130,4,128]{3,1,2,0:T(8,128)(2,1)S(1)}, bf16[1,130,4,128]{3,1,2,0:T(8,128)(2,1)}, u32[]{:S(2)}, u32[]{:S(2)}) collective-permute-start(bf16[1,130,4,128]{3,1,2,0:T(8,128)(2,1)S(1)} %pad_maximum_fusion.3), channel_id=1, source_target_pairs={{4,12},{12,20},{20,28},{28,36},{36,44},{44,52},{52,60},{60,68},{68... | collective-permute-start | bytes 399368 | tf_op jit(solution)/shard_map/ppermute | solution.py:20
  169.7 12.6 %collective-permute-start.20 = (bf16[1,130,4,128]{3,1,2,0:T(8,128)(2,1)S(1)}, bf16[1,130,4,128]{3,1,2,0:T(8,128)(2,1)}, u32[]{:S(2)}, u32[]{:S(2)}) collective-permute-start(bf16[1,130,4,128]{3,1,2,0:T(8,128)(2,1)S(1)} %pad_maximum_fusion.3), channel_id=1, source_target_pairs={{4,20},{12,28},{20,36},{28,44},{36,52},{44,60},{52,68},{60,76},{68... | collective-permute-start | bytes 399368 | tf_op jit(solution)/shard_map/ppermute | solution.py:20
  171.6 11.6 %collective-permute-start.19 = (bf16[1,130,4,128]{3,1,2,0:T(8,128)(2,1)S(1)}, bf16[1,130,4,128]{3,1,2,0:T(8,128)(2,1)}, u32[]{:S(2)}, u32[]{:S(2)}) collective-permute-start(bf16[1,130,4,128]{3,1,2,0:T(8,128)(2,1)S(1)} %pad_maximum_fusion.3), channel_id=1, source_target_pairs={{4,28},{12,36},{20,44},{28,52},{36,60},{44,68},{52,76},{60,84},{68... | collective-permute-start | bytes 399368 | tf_op jit(solution)/shard_map/ppermute | solution.py:20
  173.6 10.6 %collective-permute-start.18 = (bf16[1,130,4,128]{3,1,2,0:T(8,128)(2,1)S(1)}, bf16[1,130,4,128]{3,1,2,0:T(8,128)(2,1)}, u32[]{:S(2)}, u32[]{:S(2)}) collective-permute-start(bf16[1,130,4,128]{3,1,2,0:T(8,128)(2,1)S(1)} %pad_maximum_fusion.3), channel_id=1, source_target_pairs={{4,36},{12,44},{20,52},{28,60},{36,68},{44,76},{52,84},{60,92},{68... | collective-permute-start | bytes 399368 | tf_op jit(solution)/shard_map/ppermute | solution.py:20
  185.4 24.5 %collective-permute-start.24 = (bf16[1,130,4,128]{3,1,2,0:T(8,128)(2,1)S(1)}, bf16[1,130,4,128]{3,1,2,0:T(8,128)(2,1)S(1)}, u32[]{:S(2)}, u32[]{:S(2)}) collective-permute-start(bf16[1,130,4,128]{3,1,2,0:T(8,128)(2,1)S(1)} %pad_maximum_fusion.4), channel_id=1, source_target_pairs={{4,36},{12,44},{20,52},{28,60},{36,68},{44,76},{52,84},{60,92},{68... | collective-permute-start | bytes 399368 | tf_op jit(solution)/shard_map/ppermute | solution.py:20
  191.7 18.2 %collective-permute-start.23 = (bf16[1,130,4,128]{3,1,2,0:T(8,128)(2,1)S(1)}, bf16[1,130,4,128]{3,1,2,0:T(8,128)(2,1)S(1)}, u32[]{:S(2)}, u32[]{:S(2)}) collective-permute-start(bf16[1,130,4,128]{3,1,2,0:T(8,128)(2,1)S(1)} %pad_maximum_fusion.4), channel_id=1, source_target_pairs={{4,68},{12,76},{20,84},{28,92},{36,100},{44,108},{52,116},{60,124}... | collective-permute-start | bytes 399368 | tf_op jit(solution)/shard_map/ppermute | solution.py:20
  201.7 9.4 %collective-permute-start.22 = (bf16[1,130,4,128]{3,1,2,0:T(8,128)(2,1)S(1)}, bf16[1,130,4,128]{3,1,2,0:T(8,128)(2,1)S(1)}, u32[]{:S(2)}, u32[]{:S(2)}) collective-permute-start(bf16[1,130,4,128]{3,1,2,0:T(8,128)(2,1)S(1)} %pad_maximum_fusion.4), channel_id=1, source_target_pairs={{4,100},{12,108},{20,116},{28,124},{36,132},{44,140},{52,148},{60,... | collective-permute-start | bytes 399368 | tf_op jit(solution)/shard_map/ppermute | solution.py:20
  211.4 23.6 %collective-permute-start.29 = (bf16[1,130,4,128]{3,1,2,0:T(8,128)(2,1)S(1)}, bf16[1,130,4,128]{3,1,2,0:T(8,128)(2,1)S(1)}, u32[]{:S(2)}, u32[]{:S(2)}) collective-permute-start(bf16[1,130,4,128]{3,1,2,0:T(8,128)(2,1)S(1)} %pad_maximum_fusion.5), channel_id=1, source_target_pairs={{4,132},{12,140},{20,148},{28,156},{36,164},{44,172},{52,180},{60,... | collective-permute-start | bytes 399368 | tf_op jit(solution)/shard_map/ppermute | solution.py:20
  217.6 19.8 %collective-permute-start.28 = (bf16[1,130,4,128]{3,1,2,0:T(8,128)(2,1)S(1)}, bf16[1,130,4,128]{3,1,2,0:T(8,128)(2,1)S(1)}, u32[]{:S(2)}, u32[]{:S(2)}) collective-permute-start(bf16[1,130,4,128]{3,1,2,0:T(8,128)(2,1)S(1)} %pad_maximum_fusion.5), channel_id=1, source_target_pairs={{4,260},{12,268},{20,276},{28,284},{36,292},{44,300},{52,308},{60,... | collective-permute-start | bytes 399368 | tf_op jit(solution)/shard_map/ppermute | solution.py:20
  230.5 6.9 %collective-permute-start.27 = (bf16[1,130,4,128]{3,1,2,0:T(8,128)(2,1)S(1)}, bf16[1,130,4,128]{3,1,2,0:T(8,128)(2,1)S(1)}, u32[]{:S(2)}, u32[]{:S(2)}) collective-permute-start(bf16[1,130,4,128]{3,1,2,0:T(8,128)(2,1)S(1)} %pad_maximum_fusion.5), channel_id=1, source_target_pairs={{4,388},{12,396},{20,404},{28,412},{36,420},{44,428},{52,436},{60,... | collective-permute-start | bytes 399368 | tf_op jit(solution)/shard_map/ppermute | solution.py:20
  233.7 5.8 %collective-permute-start.25 = (bf16[1,130,4,128]{3,1,2,0:T(8,128)(2,1)S(1)}, bf16[1,130,4,128]{3,1,2,0:T(8,128)(2,1)S(1)}, u32[]{:S(2)}, u32[]{:S(2)}) collective-permute-start(bf16[1,130,4,128]{3,1,2,0:T(8,128)(2,1)S(1)} %pad_maximum_fusion.5), channel_id=1, source_target_pairs={{4,644},{12,652},{20,660},{28,668},{36,676},{44,684},{52,692},{60,... | collective-permute-start | bytes 399368 | tf_op jit(solution)/shard_map/ppermute | solution.py:20
  (19 other events, 175.0 us)

commit v7 on v6

--- a/solution.py
+++ b/solution.py
@@ -148,25 +148,28 @@
         0,
     )
     local_activations = jnp.where(section_index == 0, own_hidden, arrived[0])
-    order = (member - jnp.arange(members, dtype=jnp.int32)) % members
-    complete_hidden_matrix = (
-        jnp.take(arrived, order, axis=0).transpose(1, 0, 2).reshape(row_count, feature_count)
-    )
 
     masked_keys = jnp.where(valid_rows[:, None], own_keys, jnp.zeros_like(own_keys)).reshape(
         row_count, key_heads, head_size
     )
     wide_keys = masked_keys.astype(jnp.float32)
     decays = log_decay * valid_rows[:, None].astype(jnp.float32)
-    wide = complete_hidden_matrix.astype(jnp.float32)
-    normed = (
-        wide
-        * lax.rsqrt(jnp.mean(wide * wide, axis=-1, keepdims=True) + 1e-05)
-        * norm_gain.astype(jnp.float32)
-    ).astype(jnp.bfloat16)
-    payload_vectors = lax.dot_general(
-        normed, mixing[0], (((1,), (1,)), ((), ())), preferred_element_type=jnp.float32
-    ).astype(jnp.bfloat16)
+    wide = arrived.astype(jnp.float32)
+    inverse_scale = lax.rsqrt(
+        jnp.sum(wide * wide, axis=(0, 2))[:, None] / feature_count + 1e-05
+    )
+    payload_sum = jnp.zeros((row_count, mixing.shape[1]), jnp.float32)
+    for step in range(members):
+        owner = (member - step) % members
+        gain = lax.dynamic_slice_in_dim(norm_gain, owner * width, width, 0).astype(jnp.float32)
+        normed = (wide[step] * inverse_scale * gain).astype(jnp.bfloat16)
+        payload_sum = payload_sum + lax.dot_general(
+            normed,
+            lax.dynamic_slice_in_dim(mixing[0], owner * width, width, 1),
+            (((1,), (1,)), ((), ())),
+            preferred_element_type=jnp.float32,
+        )
+    payload_vectors = payload_sum.astype(jnp.bfloat16)
     cumulated = jnp.cumsum(decays, axis=0).reshape(row_count, key_heads, group_size)
     value_rows = payload_vectors.astype(jnp.float32).reshape(
         row_count, key_heads, group_size, head_size
@@ -199,11 +202,11 @@
     total_rows = jnp.broadcast_to(cumulated[-1][:, None, :, None], (key_heads, 1, group_size, head_size))
     own_entry = jnp.concatenate([total_rows, fresh_state], axis=1)
     entry = sent_along(own_entry, 1)
-    for times in range(2, 5):
+    for times in range(2, 4):
         entry = chain(sent_along(own_entry, times), entry)
-    reach = 4
+    reach = 3
     while reach < shards:
-        spread = 4 if reach < 16 else -(-shards // reach)
+        spread = 4 if reach < 12 else -(-shards // reach)
         joined = entry
         for times in range(1, spread):
             joined = chain(sent_along(entry, times * reach), joined)

time: 244 us -> 237 us (0.971)
  local copies, waits for them, and re-layouts: 11.7 us -> 7.05 us
  other arithmetic: 28.6 us -> 25.1 us
    ppermute x9, waiting for transfers between devices: 13.6 us -> 5.98 us  [body(): joined = lax.ppermute(packed, ('ctx', 'section'), pairs)]
    ppermute x12 -> x13, waiting for transfers between devices: 5.46 us -> 10 us  [passed_along(): return lax.ppermute(x, ('ctx', 'section'), pairs)]
    ppermute x1, starting transfers between devices: 8.62 us -> 12.3 us  [body(): lax.ppermute(jnp.concatenate([running, totals[..., None], best[..., None]...]
    ppermute x4, waiting for transfers between devices: 19.5 us -> 23 us  [body(): lax.ppermute(own_hidden, ('section', 'tp'), [(m, members + (m + step) % m...]
    mul x2 -> x0, local copies, waits for them, and re-layouts: 3.45 us -> none  [body(): wide * lax.rsqrt(jnp.mean(wide * wide, axis=-1, keepdims=True) + 1e-05)]
    ppermute x12 -> x13, starting transfers between devices: 66.8 us -> 65.1 us  [passed_along(): return lax.ppermute(x, ('ctx', 'section'), pairs)]
  transfers between devices with their start and end apart: 30 -> 31, of which waited for: 11 -> 14; matrix products, arithmetic and copies ran while one was open for 10% -> 10% of each run, Pallas kernels for 0% -> 0%
where the time goes in v7:
time: 237 us; the launch traced here: 236 us
  starting transfers between devices  146 us (62%)
  waiting for transfers between devices  42.2 us (18%)
  other arithmetic  25.1 us (11%)
  matrix products  13.9 us (6%)
  local copies, waits for them, and re-layouts  7.05 us (3%)
    ppermute x13, starting transfers between devices, passed_along(): return lax.ppermute(x, ('ctx', 'section'), pairs)  65.1 us
    ppermute x9, starting transfers between devices, body(): joined = lax.ppermute(packed, ('ctx', 'section'), pairs)  58.4 us
    ppermute x4, waiting for transfers between devices, body(): lax.ppermute(own_hidden, ('section', 'tp'), [(m, members + (m + step) % m...  23 us
    ppermute x1, starting transfers between devices, body(): lax.ppermute(jnp.concatenate([running, totals[..., None], best[..., None]...  12.3 us
    ppermute x13, waiting for transfers between devices, passed_along(): return lax.ppermute(x, ('ctx', 'section'), pairs)  10 us
    ppermute x9, waiting for transfers between devices, body(): joined = lax.ppermute(packed, ('ctx', 'section'), pairs)  5.98 us
    and x9, other arithmetic, body(): key_valid = (source >= 0) & (positions < lengths[jnp.maximum(source, 0)])  5.59 us
    ppermute x4, starting transfers between devices, body(): lax.ppermute(own_hidden, ('section', 'tp'), [(m, members + (m + step) % m...  5.17 us
  transfers between devices with their start and end apart: 31, of which 14 were waited for; matrix products, arithmetic and copies ran while one was open for 10% of the time, Pallas kernels for 0%

profile of v7, /device:TPU:1, one launch (start us, length us, event | category | flops | bytes accessed | tf_op | source)
XLA Modules:
  0.0 236.1 jit_solution(14645110624560943446)
XLA Ops:
  3.0 1.7 fusion.315
  11.5 3.1 %collective-permute-done = bf16[256,640]{1,0:T(8,128)(2,1)S(1)} collective-permute-done((bf16[256,640]{1,0:T(8,128)(2,1)S(1)}, bf16[256,640]{1,0:T(8,128)(2,1)S(1)}, u32[]{:S(2)}, u32[]{:S(2)}) %collective-permute-start) | collective-permute-done | bytes 327712 | tf_op jit(solution)/shard_map/ppermute | solution.py:52
  16.3 6.4 %collective-permute-start.8 = (bf16[256,256]{1,0:T(8,128)(2,1)S(1)}, bf16[256,256]{1,0:T(8,128)(2,1)S(1)}, u32[]{:S(2)}, u32[]{:S(2)}) collective-permute-start(bf16[256,256]{1,0:T(8,128)(2,1)S(1)} %pad_maximum_fusion.5), channel_id=1, source_target_pairs={{0,112},{8,120},{16,128},{24,136},{32,144},{40,152},{48,160},{56,1... | collective-permute-start | bytes 393224 | tf_op jit(solution)/shard_map/ppermute | solution.py:75
  22.7 6.2 %collective-permute-start.7 = (bf16[256,256]{1,0:T(8,128)(2,1)S(1)}, bf16[256,256]{1,0:T(8,128)(2,1)S(1)}, u32[]{:S(2)}, u32[]{:S(2)}) collective-permute-start(bf16[256,256]{1,0:T(8,128)(2,1)S(1)} %pad_maximum_fusion.5), channel_id=1, source_target_pairs={{0,96},{8,104},{16,112},{24,120},{32,128},{40,136},{48,144},{56,15... | collective-permute-start | bytes 393224 | tf_op jit(solution)/shard_map/ppermute | solution.py:75
  28.9 2.3 collective-permute-start.6
  31.2 8.2 %collective-permute-start.5 = (bf16[256,256]{1,0:T(8,128)(2,1)S(1)}, bf16[256,256]{1,0:T(8,128)(2,1)S(1)}, u32[]{:S(2)}, u32[]{:S(2)}) collective-permute-start(bf16[256,256]{1,0:T(8,128)(2,1)S(1)} %pad_maximum_fusion.5), channel_id=1, source_target_pairs={{0,64},{8,72},{16,80},{24,88},{32,96},{40,104},{48,112},{56,120},{... | collective-permute-start | bytes 393224 | tf_op jit(solution)/shard_map/ppermute | solution.py:75
  42.6 5.0 %collective-permute-start.2 = (bf16[256,256]{1,0:T(8,128)(2,1)S(1)}, bf16[256,256]{1,0:T(8,128)(2,1)S(1)}, u32[]{:S(2)}, u32[]{:S(2)}) collective-permute-start(bf16[256,256]{1,0:T(8,128)(2,1)S(1)} %pad_maximum_fusion.5), channel_id=1, source_target_pairs={{0,16},{8,24},{16,32},{24,40},{32,48},{40,56},{48,64},{56,72},{64,... | collective-permute-start | bytes 393224 | tf_op jit(solution)/shard_map/ppermute | solution.py:75
  48.9 1.7 collective-permute-done.2
  50.5 13.3 %collective-permute-start.3 = (bf16[256,256]{1,0:T(8,128)(2,1)S(1)}, bf16[256,256]{1,0:T(8,128)(2,1)S(1)}, u32[]{:S(2)}, u32[]{:S(2)}) collective-permute-start(bf16[256,256]{1,0:T(8,128)(2,1)S(1)} %pad_maximum_fusion.5), channel_id=1, source_target_pairs={{0,32},{8,40},{16,48},{24,56},{32,64},{40,72},{48,80},{56,88},{64,... | collective-permute-start | bytes 393224 | tf_op jit(solution)/shard_map/ppermute | solution.py:75
  65.7 15.1 %collective-permute-start.4 = (bf16[256,256]{1,0:T(8,128)(2,1)S(1)}, bf16[256,256]{1,0:T(8,128)(2,1)S(1)}, u32[]{:S(2)}, u32[]{:S(2)}) collective-permute-start(bf16[256,256]{1,0:T(8,128)(2,1)S(1)} %pad_maximum_fusion.5), channel_id=1, source_target_pairs={{0,48},{8,56},{16,64},{24,72},{32,80},{40,88},{48,96},{56,104},{64... | collective-permute-start | bytes 393224 | tf_op jit(solution)/shard_map/ppermute | solution.py:75
  81.2 1.8 collective-permute-done.4
  91.1 12.3 %collective-permute-start.10 = (f32[1,4,256,130]{2,1,3,0:T(4,128)S(1)}, f32[1,4,256,130]{2,1,3,0:T(4,128)S(1)}, u32[]{:S(2)}, u32[]{:S(2)}) collective-permute-start(f32[1,4,256,130]{2,1,3,0:T(4,128)S(1)} %copy.179), channel_id=1, source_target_pairs={{4,0},{5,1},{6,2},{7,3},{12,8},{13,9},{14,10},{15,11},{20,16},{21,... | collective-permute-start | bytes 1597448 | tf_op jit(solution)/shard_map/ppermute | solution.py:110
  105.2 3.2 %convolution_convert_fusion = bf16[256,3584]{1,0:T(8,128)(2,1)S(1)} fusion(bf16[256,512]{0,1:T(8,128)(2,1)S(1)} %bitcast.525, bf16[1,512,3584]{2,1,0:T(8,128)(2,1)} %param.14), kind=kOutput, calls=%fused_computation | convolution fusion | flops 940441600 | bytes 5767168 | tf_op jit(solution)/shard_map/dot_general | solution.py:124
  122.4 17.0 %collective-permute-done.17 = bf16[256,896]{1,0:T(8,128)(2,1)S(1)} collective-permute-done((bf16[256,896]{1,0:T(8,128)(2,1)S(1)}, bf16[256,896]{1,0:T(8,128)(2,1)S(1)}, u32[]{:S(2)}, u32[]{:S(2)}) %collective-permute-start.17) | collective-permute-done | bytes 458784 | tf_op jit(solution)/shard_map/ppermute | solution.py:141
  140.6 4.8 %collective-permute-done.15 = bf16[256,896]{1,0:T(8,128)(2,1)S(1)} collective-permute-done((bf16[256,896]{1,0:T(8,128)(2,1)S(1)}, bf16[256,896]{1,0:T(8,128)(2,1)S(1)}, u32[]{:S(2)}, u32[]{:S(2)}) %collective-permute-start.15) | collective-permute-done | bytes 458784 | tf_op jit(solution)/shard_map/ppermute | solution.py:141
  150.5 9.7 %collective-permute-start.20 = (bf16[1,130,4,128]{3,1,2,0:T(8,128)(2,1)S(1)}, bf16[1,130,4,128]{3,1,2,0:T(8,128)(2,1)S(1)}, u32[]{:S(2)}, u32[]{:S(2)}) collective-permute-start(bf16[1,130,4,128]{3,1,2,0:T(8,128)(2,1)S(1)} %pad_maximum_fusion.2), channel_id=1, source_target_pairs={{4,12},{12,20},{20,28},{28,36},{36,44},{44,52},{52,60},{60,68},{68... | collective-permute-start | bytes 399368 | tf_op jit(solution)/shard_map/ppermute | solution.py:20
  160.2 4.9 %collective-permute-start.19 = (bf16[1,130,4,128]{3,1,2,0:T(8,128)(2,1)S(1)}, bf16[1,130,4,128]{3,1,2,0:T(8,128)(2,1)S(1)}, u32[]{:S(2)}, u32[]{:S(2)}) collective-permute-start(bf16[1,130,4,128]{3,1,2,0:T(8,128)(2,1)S(1)} %pad_maximum_fusion.2), channel_id=1, source_target_pairs={{4,20},{12,28},{20,36},{28,44},{36,52},{44,60},{52,68},{60,76},{68... | collective-permute-start | bytes 399368 | tf_op jit(solution)/shard_map/ppermute | solution.py:20
  171.4 10.0 %collective-permute-start.23 = (bf16[1,130,4,128]{3,1,2,0:T(8,128)(2,1)S(1)}, bf16[1,130,4,128]{3,1,2,0:T(8,128)(2,1)}, u32[]{:S(2)}, u32[]{:S(2)}) collective-permute-start(bf16[1,130,4,128]{3,1,2,0:T(8,128)(2,1)S(1)} %pad_maximum_fusion.3), channel_id=1, source_target_pairs={{4,28},{12,36},{20,44},{28,52},{36,60},{44,68},{52,76},{60,84},{68... | collective-permute-start | bytes 399368 | tf_op jit(solution)/shard_map/ppermute | solution.py:20
  181.4 8.2 %collective-permute-start.22 = (bf16[1,130,4,128]{3,1,2,0:T(8,128)(2,1)S(1)}, bf16[1,130,4,128]{3,1,2,0:T(8,128)(2,1)}, u32[]{:S(2)}, u32[]{:S(2)}) collective-permute-start(bf16[1,130,4,128]{3,1,2,0:T(8,128)(2,1)S(1)} %pad_maximum_fusion.3), channel_id=1, source_target_pairs={{4,52},{12,60},{20,68},{28,76},{36,84},{44,92},{52,100},{60,108},{... | collective-permute-start | bytes 399368 | tf_op jit(solution)/shard_map/ppermute | solution.py:20
  189.6 3.1 %collective-permute-start.21 = (bf16[1,130,4,128]{3,1,2,0:T(8,128)(2,1)S(1)}, bf16[1,130,4,128]{3,1,2,0:T(8,128)(2,1)S(1)}, u32[]{:S(2)}, u32[]{:S(2)}) collective-permute-start(bf16[1,130,4,128]{3,1,2,0:T(8,128)(2,1)S(1)} %pad_maximum_fusion.3), channel_id=1, source_target_pairs={{4,76},{12,84},{20,92},{28,100},{36,108},{44,116},{52,124},{60,132... | collective-permute-start | bytes 399368 | tf_op jit(solution)/shard_map/ppermute | solution.py:20
  197.6 10.1 %collective-permute-start.30 = (bf16[1,130,4,128]{3,1,2,0:T(8,128)(2,1)S(1)}, bf16[1,130,4,128]{3,1,2,0:T(8,128)(2,1)S(1)}, u32[]{:S(2)}, u32[]{:S(2)}) collective-permute-start(bf16[1,130,4,128]{3,1,2,0:T(8,128)(2,1)S(1)} %pad_maximum_fusion.4), channel_id=1, source_target_pairs={{4,100},{12,108},{20,116},{28,124},{36,132},{44,140},{52,148},{60,... | collective-permute-start | bytes 399368 | tf_op jit(solution)/shard_map/ppermute | solution.py:20
  208.5 5.5 %collective-permute-start.29 = (bf16[1,130,4,128]{3,1,2,0:T(8,128)(2,1)S(1)}, bf16[1,130,4,128]{3,1,2,0:T(8,128)(2,1)S(1)}, u32[]{:S(2)}, u32[]{:S(2)}) collective-permute-start(bf16[1,130,4,128]{3,1,2,0:T(8,128)(2,1)S(1)} %pad_maximum_fusion.4), channel_id=1, source_target_pairs={{4,196},{12,204},{20,212},{28,220},{36,228},{44,236},{52,244},{60,... | collective-permute-start | bytes 399368 | tf_op jit(solution)/shard_map/ppermute | solution.py:20
  214.0 6.3 %collective-permute-start.28 = (bf16[1,130,4,128]{3,1,2,0:T(8,128)(2,1)S(1)}, bf16[1,130,4,128]{3,1,2,0:T(8,128)(2,1)S(1)}, u32[]{:S(2)}, u32[]{:S(2)}) collective-permute-start(bf16[1,130,4,128]{3,1,2,0:T(8,128)(2,1)S(1)} %pad_maximum_fusion.4), channel_id=1, source_target_pairs={{4,292},{12,300},{20,308},{28,316},{36,324},{44,332},{52,340},{60,... | collective-permute-start | bytes 399368 | tf_op jit(solution)/shard_map/ppermute | solution.py:20
  226.7 4.0 %collective-permute-done.26 = bf16[1,130,4,128]{3,1,2,0:T(8,128)(2,1)S(1)} collective-permute-done((bf16[1,130,4,128]{3,1,2,0:T(8,128)(2,1)S(1)}, bf16[1,130,4,128]{3,1,2,0:T(8,128)(2,1)S(1)}, u32[]{:S(2)}, u32[]{:S(2)}) %collective-permute-start.26) | collective-permute-done | bytes 133152 | tf_op jit(solution)/shard_map/ppermute | solution.py:20
  (206 shorter events, 70.2 us)
Async XLA Ops:
  1.7 12.9 %collective-permute-start = (bf16[256,640]{1,0:T(8,128)(2,1)S(1)}, bf16[256,640]{1,0:T(8,128)(2,1)S(1)}, u32[]{:S(2)}, u32[]{:S(2)}) collective-permute-start(bf16[256,640]{1,0:T(8,128)(2,1)S(1)} %pad_maximum_fusion.1), channel_id=1, source_target_pairs={{0,4},{1,5},{2,6},{3,7},{8,12},{9,13},{10,14},{11,15},{16,20},{17,... | collective-permute-start | bytes 983048 | tf_op jit(solution)/shard_map/ppermute | solution.py:52
  16.3 69.6 %collective-permute-start.8 = (bf16[256,256]{1,0:T(8,128)(2,1)S(1)}, bf16[256,256]{1,0:T(8,128)(2,1)S(1)}, u32[]{:S(2)}, u32[]{:S(2)}) collective-permute-start(bf16[256,256]{1,0:T(8,128)(2,1)S(1)} %pad_maximum_fusion.5), channel_id=1, source_target_pairs={{0,112},{8,120},{16,128},{24,136},{32,144},{40,152},{48,160},{56,1... | collective-permute-start | bytes 393224 | tf_op jit(solution)/shard_map/ppermute | solution.py:75
  22.7 62.7 %collective-permute-start.7 = (bf16[256,256]{1,0:T(8,128)(2,1)S(1)}, bf16[256,256]{1,0:T(8,128)(2,1)S(1)}, u32[]{:S(2)}, u32[]{:S(2)}) collective-permute-start(bf16[256,256]{1,0:T(8,128)(2,1)S(1)} %pad_maximum_fusion.5), channel_id=1, source_target_pairs={{0,96},{8,104},{16,112},{24,120},{32,128},{40,136},{48,144},{56,15... | collective-permute-start | bytes 393224 | tf_op jit(solution)/shard_map/ppermute | solution.py:75
  28.9 55.9 %collective-permute-start.6 = (bf16[256,256]{1,0:T(8,128)(2,1)S(1)}, bf16[256,256]{1,0:T(8,128)(2,1)S(1)}, u32[]{:S(2)}, u32[]{:S(2)}) collective-permute-start(bf16[256,256]{1,0:T(8,128)(2,1)S(1)} %pad_maximum_fusion.5), channel_id=1, source_target_pairs={{0,80},{8,88},{16,96},{24,104},{32,112},{40,120},{48,128},{56,136}... | collective-permute-start | bytes 393224 | tf_op jit(solution)/shard_map/ppermute | solution.py:75
  31.2 53.0 %collective-permute-start.5 = (bf16[256,256]{1,0:T(8,128)(2,1)S(1)}, bf16[256,256]{1,0:T(8,128)(2,1)S(1)}, u32[]{:S(2)}, u32[]{:S(2)}) collective-permute-start(bf16[256,256]{1,0:T(8,128)(2,1)S(1)} %pad_maximum_fusion.5), channel_id=1, source_target_pairs={{0,64},{8,72},{16,80},{24,88},{32,96},{40,104},{48,112},{56,120},{... | collective-permute-start | bytes 393224 | tf_op jit(solution)/shard_map/ppermute | solution.py:75
  42.6 7.9 %collective-permute-start.2 = (bf16[256,256]{1,0:T(8,128)(2,1)S(1)}, bf16[256,256]{1,0:T(8,128)(2,1)S(1)}, u32[]{:S(2)}, u32[]{:S(2)}) collective-permute-start(bf16[256,256]{1,0:T(8,128)(2,1)S(1)} %pad_maximum_fusion.5), channel_id=1, source_target_pairs={{0,16},{8,24},{16,32},{24,40},{32,48},{40,56},{48,64},{56,72},{64,... | collective-permute-start | bytes 393224 | tf_op jit(solution)/shard_map/ppermute | solution.py:75
  50.5 15.2 %collective-permute-start.3 = (bf16[256,256]{1,0:T(8,128)(2,1)S(1)}, bf16[256,256]{1,0:T(8,128)(2,1)S(1)}, u32[]{:S(2)}, u32[]{:S(2)}) collective-permute-start(bf16[256,256]{1,0:T(8,128)(2,1)S(1)} %pad_maximum_fusion.5), channel_id=1, source_target_pairs={{0,32},{8,40},{16,48},{24,56},{32,64},{40,72},{48,80},{56,88},{64,... | collective-permute-start | bytes 393224 | tf_op jit(solution)/shard_map/ppermute | solution.py:75
  65.7 17.3 %collective-permute-start.4 = (bf16[256,256]{1,0:T(8,128)(2,1)S(1)}, bf16[256,256]{1,0:T(8,128)(2,1)S(1)}, u32[]{:S(2)}, u32[]{:S(2)}) collective-permute-start(bf16[256,256]{1,0:T(8,128)(2,1)S(1)} %pad_maximum_fusion.5), channel_id=1, source_target_pairs={{0,48},{8,56},{16,64},{24,72},{32,80},{40,88},{48,96},{56,104},{64... | collective-permute-start | bytes 393224 | tf_op jit(solution)/shard_map/ppermute | solution.py:75
  91.1 13.8 %collective-permute-start.10 = (f32[1,4,256,130]{2,1,3,0:T(4,128)S(1)}, f32[1,4,256,130]{2,1,3,0:T(4,128)S(1)}, u32[]{:S(2)}, u32[]{:S(2)}) collective-permute-start(f32[1,4,256,130]{2,1,3,0:T(4,128)S(1)} %copy.179), channel_id=1, source_target_pairs={{4,0},{5,1},{6,2},{7,3},{12,8},{13,9},{14,10},{15,11},{20,16},{21,... | collective-permute-start | bytes 1597448 | tf_op jit(solution)/shard_map/ppermute | solution.py:110
  116.3 23.1 %collective-permute-start.17 = (bf16[256,896]{1,0:T(8,128)(2,1)S(1)}, bf16[256,896]{1,0:T(8,128)(2,1)S(1)}, u32[]{:S(2)}, u32[]{:S(2)}) collective-permute-start(bf16[256,896]{1,0:T(8,128)(2,1)S(1)} %add_convert_fusion), channel_id=1, source_target_pairs={{0,7},{1,4},{2,5},{3,6},{8,15},{9,12},{10,13},{11,14},{16,23},{17,... | collective-permute-start | bytes 1376264 | tf_op jit(solution)/shard_map/ppermute | solution.py:141
  117.6 23.0 %collective-permute-start.16 = (bf16[256,896]{1,0:T(8,128)(2,1)S(1)}, bf16[256,896]{1,0:T(8,128)(2,1)S(1)}, u32[]{:S(2)}, u32[]{:S(2)}) collective-permute-start(bf16[256,896]{1,0:T(8,128)(2,1)S(1)} %add_convert_fusion), channel_id=1, source_target_pairs={{0,6},{1,7},{2,4},{3,5},{8,14},{9,15},{10,12},{11,13},{16,22},{17,... | collective-permute-start | bytes 1376264 | tf_op jit(solution)/shard_map/ppermute | solution.py:141
  118.9 26.5 %collective-permute-start.15 = (bf16[256,896]{1,0:T(8,128)(2,1)S(1)}, bf16[256,896]{1,0:T(8,128)(2,1)S(1)}, u32[]{:S(2)}, u32[]{:S(2)}) collective-permute-start(bf16[256,896]{1,0:T(8,128)(2,1)S(1)} %add_convert_fusion), channel_id=1, source_target_pairs={{0,5},{1,6},{2,7},{3,4},{8,13},{9,14},{10,15},{11,12},{16,21},{17,... | collective-permute-start | bytes 1376264 | tf_op jit(solution)/shard_map/ppermute | solution.py:141
  120.2 25.2 %collective-permute-start.14 = (bf16[256,896]{1,0:T(8,128)(2,1)S(1)}, bf16[256,896]{1,0:T(8,128)(2,1)S(1)}, u32[]{:S(2)}, u32[]{:S(2)}) collective-permute-start(bf16[256,896]{1,0:T(8,128)(2,1)S(1)} %add_convert_fusion), channel_id=1, source_target_pairs={{0,4},{1,5},{2,6},{3,7},{8,12},{9,13},{10,14},{11,15},{16,20},{17,... | collective-permute-start | bytes 1376264 | tf_op jit(solution)/shard_map/ppermute | solution.py:141
  150.5 16.4 %collective-permute-start.20 = (bf16[1,130,4,128]{3,1,2,0:T(8,128)(2,1)S(1)}, bf16[1,130,4,128]{3,1,2,0:T(8,128)(2,1)S(1)}, u32[]{:S(2)}, u32[]{:S(2)}) collective-permute-start(bf16[1,130,4,128]{3,1,2,0:T(8,128)(2,1)S(1)} %pad_maximum_fusion.2), channel_id=1, source_target_pairs={{4,12},{12,20},{20,28},{28,36},{36,44},{44,52},{52,60},{60,68},{68... | collective-permute-start | bytes 399368 | tf_op jit(solution)/shard_map/ppermute | solution.py:20
  160.2 8.4 %collective-permute-start.19 = (bf16[1,130,4,128]{3,1,2,0:T(8,128)(2,1)S(1)}, bf16[1,130,4,128]{3,1,2,0:T(8,128)(2,1)S(1)}, u32[]{:S(2)}, u32[]{:S(2)}) collective-permute-start(bf16[1,130,4,128]{3,1,2,0:T(8,128)(2,1)S(1)} %pad_maximum_fusion.2), channel_id=1, source_target_pairs={{4,20},{12,28},{20,36},{28,44},{36,52},{44,60},{52,68},{60,76},{68... | collective-permute-start | bytes 399368 | tf_op jit(solution)/shard_map/ppermute | solution.py:20
  171.4 22.6 %collective-permute-start.23 = (bf16[1,130,4,128]{3,1,2,0:T(8,128)(2,1)S(1)}, bf16[1,130,4,128]{3,1,2,0:T(8,128)(2,1)}, u32[]{:S(2)}, u32[]{:S(2)}) collective-permute-start(bf16[1,130,4,128]{3,1,2,0:T(8,128)(2,1)S(1)} %pad_maximum_fusion.3), channel_id=1, source_target_pairs={{4,28},{12,36},{20,44},{28,52},{36,60},{44,68},{52,76},{60,84},{68... | collective-permute-start | bytes 399368 | tf_op jit(solution)/shard_map/ppermute | solution.py:20
  181.4 13.5 %collective-permute-start.22 = (bf16[1,130,4,128]{3,1,2,0:T(8,128)(2,1)S(1)}, bf16[1,130,4,128]{3,1,2,0:T(8,128)(2,1)}, u32[]{:S(2)}, u32[]{:S(2)}) collective-permute-start(bf16[1,130,4,128]{3,1,2,0:T(8,128)(2,1)S(1)} %pad_maximum_fusion.3), channel_id=1, source_target_pairs={{4,52},{12,60},{20,68},{28,76},{36,84},{44,92},{52,100},{60,108},{... | collective-permute-start | bytes 399368 | tf_op jit(solution)/shard_map/ppermute | solution.py:20
  197.6 25.7 %collective-permute-start.30 = (bf16[1,130,4,128]{3,1,2,0:T(8,128)(2,1)S(1)}, bf16[1,130,4,128]{3,1,2,0:T(8,128)(2,1)S(1)}, u32[]{:S(2)}, u32[]{:S(2)}) collective-permute-start(bf16[1,130,4,128]{3,1,2,0:T(8,128)(2,1)S(1)} %pad_maximum_fusion.4), channel_id=1, source_target_pairs={{4,100},{12,108},{20,116},{28,124},{36,132},{44,140},{52,148},{60,... | collective-permute-start | bytes 399368 | tf_op jit(solution)/shard_map/ppermute | solution.py:20
  208.5 16.7 %collective-permute-start.29 = (bf16[1,130,4,128]{3,1,2,0:T(8,128)(2,1)S(1)}, bf16[1,130,4,128]{3,1,2,0:T(8,128)(2,1)S(1)}, u32[]{:S(2)}, u32[]{:S(2)}) collective-permute-start(bf16[1,130,4,128]{3,1,2,0:T(8,128)(2,1)S(1)} %pad_maximum_fusion.4), channel_id=1, source_target_pairs={{4,196},{12,204},{20,212},{28,220},{36,228},{44,236},{52,244},{60,... | collective-permute-start | bytes 399368 | tf_op jit(solution)/shard_map/ppermute | solution.py:20
  214.0 12.7 %collective-permute-start.28 = (bf16[1,130,4,128]{3,1,2,0:T(8,128)(2,1)S(1)}, bf16[1,130,4,128]{3,1,2,0:T(8,128)(2,1)S(1)}, u32[]{:S(2)}, u32[]{:S(2)}) collective-permute-start(bf16[1,130,4,128]{3,1,2,0:T(8,128)(2,1)S(1)} %pad_maximum_fusion.4), channel_id=1, source_target_pairs={{4,292},{12,300},{20,308},{28,316},{36,324},{44,332},{52,340},{60,... | collective-permute-start | bytes 399368 | tf_op jit(solution)/shard_map/ppermute | solution.py:20
  220.3 6.4 %collective-permute-start.27 = (bf16[1,130,4,128]{3,1,2,0:T(8,128)(2,1)S(1)}, bf16[1,130,4,128]{3,1,2,0:T(8,128)(2,1)S(1)}, u32[]{:S(2)}, u32[]{:S(2)}) collective-permute-start(bf16[1,130,4,128]{3,1,2,0:T(8,128)(2,1)S(1)} %pad_maximum_fusion.4), channel_id=1, source_target_pairs={{4,388},{12,396},{20,404},{28,412},{36,420},{44,428},{52,436},{60,... | collective-permute-start | bytes 399368 | tf_op jit(solution)/shard_map/ppermute | solution.py:20
  222.0 8.8 %collective-permute-start.26 = (bf16[1,130,4,128]{3,1,2,0:T(8,128)(2,1)S(1)}, bf16[1,130,4,128]{3,1,2,0:T(8,128)(2,1)S(1)}, u32[]{:S(2)}, u32[]{:S(2)}) collective-permute-start(bf16[1,130,4,128]{3,1,2,0:T(8,128)(2,1)S(1)} %pad_maximum_fusion.4), channel_id=1, source_target_pairs={{4,484},{12,492},{20,500},{28,508},{36,516},{44,524},{52,532},{60,... | collective-permute-start | bytes 399368 | tf_op jit(solution)/shard_map/ppermute | solution.py:20
  223.3 9.0 %collective-permute-start.25 = (bf16[1,130,4,128]{3,1,2,0:T(8,128)(2,1)S(1)}, bf16[1,130,4,128]{3,1,2,0:T(8,128)(2,1)S(1)}, u32[]{:S(2)}, u32[]{:S(2)}) collective-permute-start(bf16[1,130,4,128]{3,1,2,0:T(8,128)(2,1)S(1)} %pad_maximum_fusion.4), channel_id=1, source_target_pairs={{4,580},{12,588},{20,596},{28,604},{36,612},{44,620},{52,628},{60,... | collective-permute-start | bytes 399368 | tf_op jit(solution)/shard_map/ppermute | solution.py:20
  225.2 8.6 %collective-permute-start.24 = (bf16[1,130,4,128]{3,1,2,0:T(8,128)(2,1)S(1)}, bf16[1,130,4,128]{3,1,2,0:T(8,128)(2,1)S(1)}, u32[]{:S(2)}, u32[]{:S(2)}) collective-permute-start(bf16[1,130,4,128]{3,1,2,0:T(8,128)(2,1)S(1)} %pad_maximum_fusion.4), channel_id=1, source_target_pairs={{4,676},{12,684},{20,692},{28,700},{36,708},{44,716},{52,724},{60,... | collective-permute-start | bytes 399368 | tf_op jit(solution)/shard_map/ppermute | solution.py:20
  (21 other events, 273.3 us)

commit v8 on v7

--- a/solution.py
+++ b/solution.py
@@ -58,31 +58,18 @@
     base_distance = positions[:, None] - positions[None, :]
     packed = jnp.concatenate([first_keys, window_values], axis=1)
     sections = lax.axis_size("section")
-    plan = [(0, 1)] + [(2 * j, 2 * j + 1) for j in range(1, span_blocks // 2)]
-    plan += [(2 * j, None) for j in range(span_blocks // 2, span_blocks // 2 + 1)]
+    relay = 12
+    bundled = (span_blocks - relay) // 2 + 1
+    plan = [(2 * j, 2 * j + 1) for j in range(relay // 2)]
     running = jnp.zeros((key_heads, group_size, row_count, head_size), jnp.float32)
     totals = jnp.zeros((key_heads, group_size, row_count), jnp.float32)
     best = jnp.full((key_heads, group_size, row_count), -1e30, jnp.float32)
-    for first_distance, second_distance in plan:
-        pairs = []
-        for taken, owner in ((first_distance, 0), (second_distance, 1)):
-            if taken:
-                pairs += [
-                    (i * sections + owner, (i + taken) * sections + owner)
-                    for i in range(shards)
-                    if i + taken < shards
-                ]
-        joined = lax.ppermute(packed, ("ctx", "section"), pairs)
-        if first_distance == 0:
-            joined = jnp.where(section_index == 0, packed, joined)
+
+    def blend(carry, joined, distance_blocks):
+        running, totals, best = carry
         key_block, value_block = joined[:, :key_width], joined[:, key_width:]
-        distance_blocks = jnp.where(
-            section_index == 0,
-            first_distance,
-            span_blocks + 1 if second_distance is None else second_distance,
-        )
         source = shard_index - distance_blocks
-        key_valid = (source >= 0) & (positions < lengths[jnp.maximum(source, 0)])
+        key_valid = (source >= 0) & (positions < lengths[jnp.clip(source, 0, shards - 1)])
         scores = (
             jnp.einsum(
                 "rgjd,kgd->gjrk",
@@ -104,9 +91,41 @@
             value_block.reshape(row_count, key_heads, head_size),
             preferred_element_type=jnp.float32,
         )
-        running = running * factor[..., None] + blended
-        totals = totals * factor + jnp.sum(weights, axis=-1)
-        best = new_best
+        return (
+            running * factor[..., None] + blended,
+            totals * factor + jnp.sum(weights, axis=-1),
+            new_best,
+        )
+
+    def both_pairs(first_distance, second_distance):
+        pairs = []
+        for taken, owner in ((first_distance, 0), (second_distance, 1)):
+            if taken:
+                pairs += [
+                    (i * sections + owner, (i + taken) * sections + owner)
+                    for i in range(shards)
+                    if i + taken < shards
+                ]
+        return pairs
+
+    carry = (running, totals, best)
+    held = []
+    for first_distance, second_distance in plan:
+        joined = lax.ppermute(packed, ("ctx", "section"), both_pairs(first_distance, second_distance))
+        if first_distance == 0:
+            joined = jnp.where(section_index == 0, packed, joined)
+        held.append(joined)
+        carry = blend(carry, joined, jnp.where(section_index == 0, first_distance, second_distance))
+    bundle = lax.ppermute(
+        jnp.concatenate(held[:bundled], axis=1), ("ctx", "section"), both_pairs(relay, relay)
+    )
+    for slot in range(bundled):
+        carry = blend(
+            carry,
+            bundle[:, slot * 2 * key_width:(slot + 1) * 2 * key_width],
+            relay + 2 * slot + jnp.where(section_index == 0, 0, 1),
+        )
+    running, totals, best = carry
     partial = lax.ppermute(
         jnp.concatenate([running, totals[..., None], best[..., None]], axis=-1),
         "section",

time: 237 us -> 206 us (0.87)
  starting transfers between devices: 146 us -> 99.6 us
  waiting for transfers between devices: 42.2 us -> 57 us
    ppermute x9 -> x7, starting transfers between devices: 58.4 us -> 37.9 us  [the longest x6 34.6 us: body(): lax.ppermute(packed, ('ctx', 'section'), both_pairs(first_distance, secon...]
    ppermute x13, starting transfers between devices: 65.1 us -> 50.2 us  [passed_along(): return lax.ppermute(x, ('ctx', 'section'), pairs)]
    ppermute x1, starting transfers between devices: 12.3 us -> 1.32 us  [body(): lax.ppermute(jnp.concatenate([running, totals[..., None], best[..., None]...]
    ppermute x9 -> x7, waiting for transfers between devices: 5.98 us -> 16.2 us  [the longest x6 15.7 us: body(): lax.ppermute(packed, ('ctx', 'section'), both_pairs(first_distance, secon...]
    ppermute x13, waiting for transfers between devices: 10 us -> 14.6 us  [passed_along(): return lax.ppermute(x, ('ctx', 'section'), pairs)]
  transfers between devices with their start and end apart: 31 -> 29, of which waited for: 14 -> 12; matrix products, arithmetic and copies ran while one was open for 10% -> 12% of each run, Pallas kernels for 0% -> 0%
where the time goes in v8:
time: 206 us; the launch traced here: 205 us
  starting transfers between devices  99.6 us (48%)
  waiting for transfers between devices  57 us (28%)
  other arithmetic  25.2 us (12%)
  matrix products  13.8 us (7%)
  local copies, waits for them, and re-layouts  7.06 us (3%)
    ppermute x13, starting transfers between devices, passed_along(): return lax.ppermute(x, ('ctx', 'section'), pairs)  50.2 us
    ppermute x6, starting transfers between devices, body(): lax.ppermute(packed, ('ctx', 'section'), both_pairs(first_distance, secon...  34.6 us
    ppermute x4, waiting for transfers between devices, body(): lax.ppermute(own_hidden, ('section', 'tp'), [(m, members + (m + step) % m...  23 us
    ppermute x6, waiting for transfers between devices, body(): lax.ppermute(packed, ('ctx', 'section'), both_pairs(first_distance, secon...  15.7 us
    ppermute x13, waiting for transfers between devices, passed_along(): return lax.ppermute(x, ('ctx', 'section'), pairs)  14.6 us
    and x9, other arithmetic, blend(): (source >= 0) & (positions < lengths[jnp.clip(source, 0, shards - 1)])  5.68 us
    ppermute x4, starting transfers between devices, body(): lax.ppermute(own_hidden, ('section', 'tp'), [(m, members + (m + step) % m...  5.35 us
  transfers between devices with their start and end apart: 29, of which 12 were waited for; matrix products, arithmetic and copies ran while one was open for 12% of the time, Pallas kernels for 0%

profile of v8, /device:TPU:1, one launch (start us, length us, event | category | flops | bytes accessed | tf_op | source)
XLA Modules:
  0.0 204.7 jit_solution(5053475856949172734)
XLA Ops:
  3.1 1.7 fusion.315
  11.6 3.0 %collective-permute-done = bf16[256,640]{1,0:T(8,128)(2,1)S(1)} collective-permute-done((bf16[256,640]{1,0:T(8,128)(2,1)S(1)}, bf16[256,640]{1,0:T(8,128)(2,1)S(1)}, u32[]{:S(2)}, u32[]{:S(2)}) %collective-permute-start) | collective-permute-done | bytes 327712 | tf_op jit(solution)/shard_map/ppermute | solution.py:52
  16.3 12.1 %collective-permute-start.5 = (bf16[256,256]{1,0:T(8,128)(2,1)S(1)}, bf16[256,256]{1,0:T(8,128)(2,1)S(1)}, u32[]{:S(2)}, u32[]{:S(2)}) collective-permute-start(bf16[256,256]{1,0:T(8,128)(2,1)S(1)} %pad_maximum_fusion.6), channel_id=1, source_target_pairs={{0,64},{8,72},{16,80},{24,88},{32,96},{40,104},{48,112},{56,120},{... | collective-permute-start | bytes 393224 | tf_op jit(solution)/shard_map/ppermute | solution.py:114
  28.4 2.5 %collective-permute-start.4 = (bf16[256,256]{1,0:T(8,128)(2,1)S(1)}, bf16[256,256]{1,0:T(8,128)(2,1)S(1)}, u32[]{:S(2)}, u32[]{:S(2)}) collective-permute-start(bf16[256,256]{1,0:T(8,128)(2,1)S(1)} %pad_maximum_fusion.6), channel_id=1, source_target_pairs={{0,48},{8,56},{16,64},{24,72},{32,80},{40,88},{48,96},{56,104},{64... | collective-permute-start | bytes 393224 | tf_op jit(solution)/shard_map/ppermute | solution.py:114
  30.9 8.6 %collective-permute-start.3 = (bf16[256,256]{1,0:T(8,128)(2,1)S(1)}, bf16[256,256]{1,0:T(8,128)(2,1)S(1)}, u32[]{:S(2)}, u32[]{:S(2)}) collective-permute-start(bf16[256,256]{1,0:T(8,128)(2,1)S(1)} %pad_maximum_fusion.6), channel_id=1, source_target_pairs={{0,32},{8,40},{16,48},{24,56},{32,64},{40,72},{48,80},{56,88},{64,... | collective-permute-start | bytes 393224 | tf_op jit(solution)/shard_map/ppermute | solution.py:114
  40.8 3.1 %collective-permute-start.1 = (bf16[256,256]{1,0:T(8,128)(2,1)S(1)}, bf16[256,256]{1,0:T(8,128)(2,1)S(1)}, u32[]{:S(2)}, u32[]{:S(2)}) collective-permute-start(bf16[256,256]{1,0:T(8,128)(2,1)S(1)} %pad_maximum_fusion.6), channel_id=1, source_target_pairs={{4,12},{12,20},{20,28},{28,36},{36,44},{44,52},{52,60},{60,68},{68... | collective-permute-start | bytes 393224 | tf_op jit(solution)/shard_map/ppermute | solution.py:114
  44.9 15.7 %collective-permute-done.1 = bf16[256,256]{1,0:T(8,128)(2,1)S(1)} collective-permute-done((bf16[256,256]{1,0:T(8,128)(2,1)S(1)}, bf16[256,256]{1,0:T(8,128)(2,1)S(1)}, u32[]{:S(2)}, u32[]{:S(2)}) %collective-permute-start.1) | collective-permute-done | bytes 131104 | tf_op jit(solution)/shard_map/ppermute | solution.py:114
  60.7 7.0 %collective-permute-start.6 = (bf16[256,256]{1,0:T(8,128)(2,1)S(1)}, bf16[256,256]{1,0:T(8,128)(2,1)S(1)}, u32[]{:S(2)}, u32[]{:S(2)}) collective-permute-start(bf16[256,256]{1,0:T(8,128)(2,1)S(1)} %pad_maximum_fusion.6), channel_id=1, source_target_pairs={{0,80},{8,88},{16,96},{24,104},{32,112},{40,120},{48,128},{56,136}... | collective-permute-start | bytes 393224 | tf_op jit(solution)/shard_map/ppermute | solution.py:114
  68.6 3.3 %collective-permute-start.7 = (bf16[256,768]{1,0:T(8,128)(2,1)S(1)}, bf16[256,768]{1,0:T(8,128)(2,1)S(1)}, u32[]{:S(2)}, u32[]{:S(2)}) collective-permute-start(bf16[256,768]{1,0:T(8,128)(2,1)S(1)} %pad_maximum_fusion.1), channel_id=1, source_target_pairs={{0,96},{8,104},{16,112},{24,120},{32,128},{40,136},{48,144},{56,15... | collective-permute-start | bytes 1179656 | tf_op jit(solution)/shard_map/ppermute | solution.py:119
  83.9 3.2 %convolution_convert_fusion = bf16[256,3584]{1,0:T(8,128)(2,1)S(1)} fusion(bf16[256,512]{0,1:T(8,128)(2,1)S(1)} %bitcast.525, bf16[1,512,3584]{2,1,0:T(8,128)(2,1)} %param.14), kind=kOutput, calls=%fused_computation | convolution fusion | flops 940441600 | bytes 5767168 | tf_op jit(solution)/shard_map/dot_general | solution.py:143
  101.4 16.9 %collective-permute-done.15 = bf16[256,896]{1,0:T(8,128)(2,1)S(1)} collective-permute-done((bf16[256,896]{1,0:T(8,128)(2,1)S(1)}, bf16[256,896]{1,0:T(8,128)(2,1)S(1)}, u32[]{:S(2)}, u32[]{:S(2)}) %collective-permute-start.15) | collective-permute-done | bytes 458784 | tf_op jit(solution)/shard_map/ppermute | solution.py:160
  119.6 4.8 %collective-permute-done.13 = bf16[256,896]{1,0:T(8,128)(2,1)S(1)} collective-permute-done((bf16[256,896]{1,0:T(8,128)(2,1)S(1)}, bf16[256,896]{1,0:T(8,128)(2,1)S(1)}, u32[]{:S(2)}, u32[]{:S(2)}) %collective-permute-start.13) | collective-permute-done | bytes 458784 | tf_op jit(solution)/shard_map/ppermute | solution.py:160
  129.4 3.4 %collective-permute-start.18 = (bf16[1,130,4,128]{3,1,2,0:T(8,128)(2,1)S(1)}, bf16[1,130,4,128]{3,1,2,0:T(8,128)(2,1)S(1)}, u32[]{:S(2)}, u32[]{:S(2)}) collective-permute-start(bf16[1,130,4,128]{3,1,2,0:T(8,128)(2,1)S(1)} %pad_maximum_fusion.3), channel_id=1, source_target_pairs={{4,12},{12,20},{20,28},{28,36},{36,44},{44,52},{52,60},{60,68},{68... | collective-permute-start | bytes 399368 | tf_op jit(solution)/shard_map/ppermute | solution.py:20
  132.8 2.8 %collective-permute-start.17 = (bf16[1,130,4,128]{3,1,2,0:T(8,128)(2,1)S(1)}, bf16[1,130,4,128]{3,1,2,0:T(8,128)(2,1)S(1)}, u32[]{:S(2)}, u32[]{:S(2)}) collective-permute-start(bf16[1,130,4,128]{3,1,2,0:T(8,128)(2,1)S(1)} %pad_maximum_fusion.3), channel_id=1, source_target_pairs={{4,20},{12,28},{20,36},{28,44},{36,52},{44,60},{52,68},{60,76},{68... | collective-permute-start | bytes 399368 | tf_op jit(solution)/shard_map/ppermute | solution.py:20
  135.7 2.8 %collective-permute-start.16 = (bf16[1,130,4,128]{3,1,2,0:T(8,128)(2,1)S(1)}, bf16[1,130,4,128]{3,1,2,0:T(8,128)(2,1)S(1)}, u32[]{:S(2)}, u32[]{:S(2)}) collective-permute-start(bf16[1,130,4,128]{3,1,2,0:T(8,128)(2,1)S(1)} %pad_maximum_fusion.3), channel_id=1, source_target_pairs={{4,28},{12,36},{20,44},{28,52},{36,60},{44,68},{52,76},{60,84},{68... | collective-permute-start | bytes 399368 | tf_op jit(solution)/shard_map/ppermute | solution.py:20
  138.7 3.1 %collective-permute-done.16 = bf16[1,130,4,128]{3,1,2,0:T(8,128)(2,1)S(1)} collective-permute-done((bf16[1,130,4,128]{3,1,2,0:T(8,128)(2,1)S(1)}, bf16[1,130,4,128]{3,1,2,0:T(8,128)(2,1)S(1)}, u32[]{:S(2)}, u32[]{:S(2)}) %collective-permute-start.16) | collective-permute-done | bytes 133152 | tf_op jit(solution)/shard_map/ppermute | solution.py:20
  143.2 7.3 %collective-permute-start.21 = (bf16[1,130,4,128]{3,1,2,0:T(8,128)(2,1)S(1)}, bf16[1,130,4,128]{3,1,2,0:T(8,128)(2,1)}, u32[]{:S(2)}, u32[]{:S(2)}) collective-permute-start(bf16[1,130,4,128]{3,1,2,0:T(8,128)(2,1)S(1)} %pad_maximum_fusion.4), channel_id=1, source_target_pairs={{4,28},{12,36},{20,44},{28,52},{36,60},{44,68},{52,76},{60,84},{68... | collective-permute-start | bytes 399368 | tf_op jit(solution)/shard_map/ppermute | solution.py:20
  150.5 10.4 %collective-permute-start.20 = (bf16[1,130,4,128]{3,1,2,0:T(8,128)(2,1)S(1)}, bf16[1,130,4,128]{3,1,2,0:T(8,128)(2,1)}, u32[]{:S(2)}, u32[]{:S(2)}) collective-permute-start(bf16[1,130,4,128]{3,1,2,0:T(8,128)(2,1)S(1)} %pad_maximum_fusion.4), channel_id=1, source_target_pairs={{4,52},{12,60},{20,68},{28,76},{36,84},{44,92},{52,100},{60,108},{... | collective-permute-start | bytes 399368 | tf_op jit(solution)/shard_map/ppermute | solution.py:20
  160.9 1.7 collective-permute-start.19
  165.8 4.7 %collective-permute-done.19 = bf16[1,130,4,128]{3,1,2,0:T(8,128)(2,1)S(1)} collective-permute-done((bf16[1,130,4,128]{3,1,2,0:T(8,128)(2,1)S(1)}, bf16[1,130,4,128]{3,1,2,0:T(8,128)(2,1)S(1)}, u32[]{:S(2)}, u32[]{:S(2)}) %collective-permute-start.19) | collective-permute-done | bytes 133152 | tf_op jit(solution)/shard_map/ppermute | solution.py:20
  172.1 5.1 %collective-permute-start.28 = (bf16[1,130,4,128]{3,1,2,0:T(8,128)(2,1)S(1)}, bf16[1,130,4,128]{3,1,2,0:T(8,128)(2,1)S(1)}, u32[]{:S(2)}, u32[]{:S(2)}) collective-permute-start(bf16[1,130,4,128]{3,1,2,0:T(8,128)(2,1)S(1)} %pad_maximum_fusion.5), channel_id=1, source_target_pairs={{4,100},{12,108},{20,116},{28,124},{36,132},{44,140},{52,148},{60,... | collective-permute-start | bytes 399368 | tf_op jit(solution)/shard_map/ppermute | solution.py:20
  178.0 4.7 %collective-permute-start.27 = (bf16[1,130,4,128]{3,1,2,0:T(8,128)(2,1)S(1)}, bf16[1,130,4,128]{3,1,2,0:T(8,128)(2,1)S(1)}, u32[]{:S(2)}, u32[]{:S(2)}) collective-permute-start(bf16[1,130,4,128]{3,1,2,0:T(8,128)(2,1)S(1)} %pad_maximum_fusion.5), channel_id=1, source_target_pairs={{4,196},{12,204},{20,212},{28,220},{36,228},{44,236},{52,244},{60,... | collective-permute-start | bytes 399368 | tf_op jit(solution)/shard_map/ppermute | solution.py:20
  182.7 6.3 %collective-permute-start.26 = (bf16[1,130,4,128]{3,1,2,0:T(8,128)(2,1)S(1)}, bf16[1,130,4,128]{3,1,2,0:T(8,128)(2,1)S(1)}, u32[]{:S(2)}, u32[]{:S(2)}) collective-permute-start(bf16[1,130,4,128]{3,1,2,0:T(8,128)(2,1)S(1)} %pad_maximum_fusion.5), channel_id=1, source_target_pairs={{4,292},{12,300},{20,308},{28,316},{36,324},{44,332},{52,340},{60,... | collective-permute-start | bytes 399368 | tf_op jit(solution)/shard_map/ppermute | solution.py:20
  195.4 4.0 %collective-permute-done.24 = bf16[1,130,4,128]{3,1,2,0:T(8,128)(2,1)S(1)} collective-permute-done((bf16[1,130,4,128]{3,1,2,0:T(8,128)(2,1)S(1)}, bf16[1,130,4,128]{3,1,2,0:T(8,128)(2,1)S(1)}, u32[]{:S(2)}, u32[]{:S(2)}) %collective-permute-start.24) | collective-permute-done | bytes 133152 | tf_op jit(solution)/shard_map/ppermute | solution.py:20
  (202 shorter events, 64.5 us)
Async XLA Ops:
  1.7 12.9 %collective-permute-start = (bf16[256,640]{1,0:T(8,128)(2,1)S(1)}, bf16[256,640]{1,0:T(8,128)(2,1)S(1)}, u32[]{:S(2)}, u32[]{:S(2)}) collective-permute-start(bf16[256,640]{1,0:T(8,128)(2,1)S(1)} %pad_maximum_fusion.2), channel_id=1, source_target_pairs={{0,4},{1,5},{2,6},{3,7},{8,12},{9,13},{10,14},{11,15},{16,20},{17,... | collective-permute-start | bytes 983048 | tf_op jit(solution)/shard_map/ppermute | solution.py:52
  16.3 57.2 %collective-permute-start.5 = (bf16[256,256]{1,0:T(8,128)(2,1)S(1)}, bf16[256,256]{1,0:T(8,128)(2,1)S(1)}, u32[]{:S(2)}, u32[]{:S(2)}) collective-permute-start(bf16[256,256]{1,0:T(8,128)(2,1)S(1)} %pad_maximum_fusion.6), channel_id=1, source_target_pairs={{0,64},{8,72},{16,80},{24,88},{32,96},{40,104},{48,112},{56,120},{... | collective-permute-start | bytes 393224 | tf_op jit(solution)/shard_map/ppermute | solution.py:114
  28.4 44.5 %collective-permute-start.4 = (bf16[256,256]{1,0:T(8,128)(2,1)S(1)}, bf16[256,256]{1,0:T(8,128)(2,1)S(1)}, u32[]{:S(2)}, u32[]{:S(2)}) collective-permute-start(bf16[256,256]{1,0:T(8,128)(2,1)S(1)} %pad_maximum_fusion.6), channel_id=1, source_target_pairs={{0,48},{8,56},{16,64},{24,72},{32,80},{40,88},{48,96},{56,104},{64... | collective-permute-start | bytes 393224 | tf_op jit(solution)/shard_map/ppermute | solution.py:114
  30.9 37.7 %collective-permute-start.3 = (bf16[256,256]{1,0:T(8,128)(2,1)S(1)}, bf16[256,256]{1,0:T(8,128)(2,1)S(1)}, u32[]{:S(2)}, u32[]{:S(2)}) collective-permute-start(bf16[256,256]{1,0:T(8,128)(2,1)S(1)} %pad_maximum_fusion.6), channel_id=1, source_target_pairs={{0,32},{8,40},{16,48},{24,56},{32,64},{40,72},{48,80},{56,88},{64,... | collective-permute-start | bytes 393224 | tf_op jit(solution)/shard_map/ppermute | solution.py:114
  39.5 29.0 %collective-permute-start.2 = (bf16[256,256]{1,0:T(8,128)(2,1)S(1)}, bf16[256,256]{1,0:T(8,128)(2,1)S(1)}, u32[]{:S(2)}, u32[]{:S(2)}) collective-permute-start(bf16[256,256]{1,0:T(8,128)(2,1)S(1)} %pad_maximum_fusion.6), channel_id=1, source_target_pairs={{0,16},{8,24},{16,32},{24,40},{32,48},{40,56},{48,64},{56,72},{64,... | collective-permute-start | bytes 393224 | tf_op jit(solution)/shard_map/ppermute | solution.py:114
  40.8 19.8 %collective-permute-start.1 = (bf16[256,256]{1,0:T(8,128)(2,1)S(1)}, bf16[256,256]{1,0:T(8,128)(2,1)S(1)}, u32[]{:S(2)}, u32[]{:S(2)}) collective-permute-start(bf16[256,256]{1,0:T(8,128)(2,1)S(1)} %pad_maximum_fusion.6), channel_id=1, source_target_pairs={{4,12},{12,20},{20,28},{28,36},{36,44},{44,52},{52,60},{60,68},{68... | collective-permute-start | bytes 393224 | tf_op jit(solution)/shard_map/ppermute | solution.py:114
  60.7 13.4 %collective-permute-start.6 = (bf16[256,256]{1,0:T(8,128)(2,1)S(1)}, bf16[256,256]{1,0:T(8,128)(2,1)S(1)}, u32[]{:S(2)}, u32[]{:S(2)}) collective-permute-start(bf16[256,256]{1,0:T(8,128)(2,1)S(1)} %pad_maximum_fusion.6), channel_id=1, source_target_pairs={{0,80},{8,88},{16,96},{24,104},{32,112},{40,120},{48,128},{56,136}... | collective-permute-start | bytes 393224 | tf_op jit(solution)/shard_map/ppermute | solution.py:114
  68.6 8.7 %collective-permute-start.7 = (bf16[256,768]{1,0:T(8,128)(2,1)S(1)}, bf16[256,768]{1,0:T(8,128)(2,1)S(1)}, u32[]{:S(2)}, u32[]{:S(2)}) collective-permute-start(bf16[256,768]{1,0:T(8,128)(2,1)S(1)} %pad_maximum_fusion.1), channel_id=1, source_target_pairs={{0,96},{8,104},{16,112},{24,120},{32,128},{40,136},{48,144},{56,15... | collective-permute-start | bytes 1179656 | tf_op jit(solution)/shard_map/ppermute | solution.py:119
  95.1 23.1 %collective-permute-start.15 = (bf16[256,896]{1,0:T(8,128)(2,1)S(1)}, bf16[256,896]{1,0:T(8,128)(2,1)S(1)}, u32[]{:S(2)}, u32[]{:S(2)}) collective-permute-start(bf16[256,896]{1,0:T(8,128)(2,1)S(1)} %add_convert_fusion), channel_id=1, source_target_pairs={{0,7},{1,4},{2,5},{3,6},{8,15},{9,12},{10,13},{11,14},{16,23},{17,... | collective-permute-start | bytes 1376264 | tf_op jit(solution)/shard_map/ppermute | solution.py:160
  96.6 23.0 %collective-permute-start.14 = (bf16[256,896]{1,0:T(8,128)(2,1)S(1)}, bf16[256,896]{1,0:T(8,128)(2,1)S(1)}, u32[]{:S(2)}, u32[]{:S(2)}) collective-permute-start(bf16[256,896]{1,0:T(8,128)(2,1)S(1)} %add_convert_fusion), channel_id=1, source_target_pairs={{0,6},{1,7},{2,4},{3,5},{8,14},{9,15},{10,12},{11,13},{16,22},{17,... | collective-permute-start | bytes 1376264 | tf_op jit(solution)/shard_map/ppermute | solution.py:160
  97.9 26.5 %collective-permute-start.13 = (bf16[256,896]{1,0:T(8,128)(2,1)S(1)}, bf16[256,896]{1,0:T(8,128)(2,1)S(1)}, u32[]{:S(2)}, u32[]{:S(2)}) collective-permute-start(bf16[256,896]{1,0:T(8,128)(2,1)S(1)} %add_convert_fusion), channel_id=1, source_target_pairs={{0,5},{1,6},{2,7},{3,4},{8,13},{9,14},{10,15},{11,12},{16,21},{17,... | collective-permute-start | bytes 1376264 | tf_op jit(solution)/shard_map/ppermute | solution.py:160
  99.2 25.2 %collective-permute-start.12 = (bf16[256,896]{1,0:T(8,128)(2,1)S(1)}, bf16[256,896]{1,0:T(8,128)(2,1)S(1)}, u32[]{:S(2)}, u32[]{:S(2)}) collective-permute-start(bf16[256,896]{1,0:T(8,128)(2,1)S(1)} %add_convert_fusion), channel_id=1, source_target_pairs={{0,4},{1,5},{2,6},{3,7},{8,12},{9,13},{10,14},{11,15},{16,20},{17,... | collective-permute-start | bytes 1376264 | tf_op jit(solution)/shard_map/ppermute | solution.py:160
  129.4 9.2 %collective-permute-start.18 = (bf16[1,130,4,128]{3,1,2,0:T(8,128)(2,1)S(1)}, bf16[1,130,4,128]{3,1,2,0:T(8,128)(2,1)S(1)}, u32[]{:S(2)}, u32[]{:S(2)}) collective-permute-start(bf16[1,130,4,128]{3,1,2,0:T(8,128)(2,1)S(1)} %pad_maximum_fusion.3), channel_id=1, source_target_pairs={{4,12},{12,20},{20,28},{28,36},{36,44},{44,52},{52,60},{60,68},{68... | collective-permute-start | bytes 399368 | tf_op jit(solution)/shard_map/ppermute | solution.py:20
  135.7 6.1 %collective-permute-start.16 = (bf16[1,130,4,128]{3,1,2,0:T(8,128)(2,1)S(1)}, bf16[1,130,4,128]{3,1,2,0:T(8,128)(2,1)S(1)}, u32[]{:S(2)}, u32[]{:S(2)}) collective-permute-start(bf16[1,130,4,128]{3,1,2,0:T(8,128)(2,1)S(1)} %pad_maximum_fusion.3), channel_id=1, source_target_pairs={{4,28},{12,36},{20,44},{28,52},{36,60},{44,68},{52,76},{60,84},{68... | collective-permute-start | bytes 399368 | tf_op jit(solution)/shard_map/ppermute | solution.py:20
  143.2 20.8 %collective-permute-start.21 = (bf16[1,130,4,128]{3,1,2,0:T(8,128)(2,1)S(1)}, bf16[1,130,4,128]{3,1,2,0:T(8,128)(2,1)}, u32[]{:S(2)}, u32[]{:S(2)}) collective-permute-start(bf16[1,130,4,128]{3,1,2,0:T(8,128)(2,1)S(1)} %pad_maximum_fusion.4), channel_id=1, source_target_pairs={{4,28},{12,36},{20,44},{28,52},{36,60},{44,68},{52,76},{60,84},{68... | collective-permute-start | bytes 399368 | tf_op jit(solution)/shard_map/ppermute | solution.py:20
  150.5 14.4 %collective-permute-start.20 = (bf16[1,130,4,128]{3,1,2,0:T(8,128)(2,1)S(1)}, bf16[1,130,4,128]{3,1,2,0:T(8,128)(2,1)}, u32[]{:S(2)}, u32[]{:S(2)}) collective-permute-start(bf16[1,130,4,128]{3,1,2,0:T(8,128)(2,1)S(1)} %pad_maximum_fusion.4), channel_id=1, source_target_pairs={{4,52},{12,60},{20,68},{28,76},{36,84},{44,92},{52,100},{60,108},{... | collective-permute-start | bytes 399368 | tf_op jit(solution)/shard_map/ppermute | solution.py:20
  160.9 9.6 %collective-permute-start.19 = (bf16[1,130,4,128]{3,1,2,0:T(8,128)(2,1)S(1)}, bf16[1,130,4,128]{3,1,2,0:T(8,128)(2,1)S(1)}, u32[]{:S(2)}, u32[]{:S(2)}) collective-permute-start(bf16[1,130,4,128]{3,1,2,0:T(8,128)(2,1)S(1)} %pad_maximum_fusion.4), channel_id=1, source_target_pairs={{4,76},{12,84},{20,92},{28,100},{36,108},{44,116},{52,124},{60,132... | collective-permute-start | bytes 399368 | tf_op jit(solution)/shard_map/ppermute | solution.py:20
  172.1 19.8 %collective-permute-start.28 = (bf16[1,130,4,128]{3,1,2,0:T(8,128)(2,1)S(1)}, bf16[1,130,4,128]{3,1,2,0:T(8,128)(2,1)S(1)}, u32[]{:S(2)}, u32[]{:S(2)}) collective-permute-start(bf16[1,130,4,128]{3,1,2,0:T(8,128)(2,1)S(1)} %pad_maximum_fusion.5), channel_id=1, source_target_pairs={{4,100},{12,108},{20,116},{28,124},{36,132},{44,140},{52,148},{60,... | collective-permute-start | bytes 399368 | tf_op jit(solution)/shard_map/ppermute | solution.py:20
  178.0 15.8 %collective-permute-start.27 = (bf16[1,130,4,128]{3,1,2,0:T(8,128)(2,1)S(1)}, bf16[1,130,4,128]{3,1,2,0:T(8,128)(2,1)S(1)}, u32[]{:S(2)}, u32[]{:S(2)}) collective-permute-start(bf16[1,130,4,128]{3,1,2,0:T(8,128)(2,1)S(1)} %pad_maximum_fusion.5), channel_id=1, source_target_pairs={{4,196},{12,204},{20,212},{28,220},{36,228},{44,236},{52,244},{60,... | collective-permute-start | bytes 399368 | tf_op jit(solution)/shard_map/ppermute | solution.py:20
  182.7 12.6 %collective-permute-start.26 = (bf16[1,130,4,128]{3,1,2,0:T(8,128)(2,1)S(1)}, bf16[1,130,4,128]{3,1,2,0:T(8,128)(2,1)S(1)}, u32[]{:S(2)}, u32[]{:S(2)}) collective-permute-start(bf16[1,130,4,128]{3,1,2,0:T(8,128)(2,1)S(1)} %pad_maximum_fusion.5), channel_id=1, source_target_pairs={{4,292},{12,300},{20,308},{28,316},{36,324},{44,332},{52,340},{60,... | collective-permute-start | bytes 399368 | tf_op jit(solution)/shard_map/ppermute | solution.py:20
  189.0 6.4 %collective-permute-start.25 = (bf16[1,130,4,128]{3,1,2,0:T(8,128)(2,1)S(1)}, bf16[1,130,4,128]{3,1,2,0:T(8,128)(2,1)S(1)}, u32[]{:S(2)}, u32[]{:S(2)}) collective-permute-start(bf16[1,130,4,128]{3,1,2,0:T(8,128)(2,1)S(1)} %pad_maximum_fusion.5), channel_id=1, source_target_pairs={{4,388},{12,396},{20,404},{28,412},{36,420},{44,428},{52,436},{60,... | collective-permute-start | bytes 399368 | tf_op jit(solution)/shard_map/ppermute | solution.py:20
  190.6 8.8 %collective-permute-start.24 = (bf16[1,130,4,128]{3,1,2,0:T(8,128)(2,1)S(1)}, bf16[1,130,4,128]{3,1,2,0:T(8,128)(2,1)S(1)}, u32[]{:S(2)}, u32[]{:S(2)}) collective-permute-start(bf16[1,130,4,128]{3,1,2,0:T(8,128)(2,1)S(1)} %pad_maximum_fusion.5), channel_id=1, source_target_pairs={{4,484},{12,492},{20,500},{28,508},{36,516},{44,524},{52,532},{60,... | collective-permute-start | bytes 399368 | tf_op jit(solution)/shard_map/ppermute | solution.py:20
  191.9 9.0 %collective-permute-start.23 = (bf16[1,130,4,128]{3,1,2,0:T(8,128)(2,1)S(1)}, bf16[1,130,4,128]{3,1,2,0:T(8,128)(2,1)S(1)}, u32[]{:S(2)}, u32[]{:S(2)}) collective-permute-start(bf16[1,130,4,128]{3,1,2,0:T(8,128)(2,1)S(1)} %pad_maximum_fusion.5), channel_id=1, source_target_pairs={{4,580},{12,588},{20,596},{28,604},{36,612},{44,620},{52,628},{60,... | collective-permute-start | bytes 399368 | tf_op jit(solution)/shard_map/ppermute | solution.py:20
  193.8 8.6 %collective-permute-start.22 = (bf16[1,130,4,128]{3,1,2,0:T(8,128)(2,1)S(1)}, bf16[1,130,4,128]{3,1,2,0:T(8,128)(2,1)S(1)}, u32[]{:S(2)}, u32[]{:S(2)}) collective-permute-start(bf16[1,130,4,128]{3,1,2,0:T(8,128)(2,1)S(1)} %pad_maximum_fusion.5), channel_id=1, source_target_pairs={{4,676},{12,684},{20,692},{28,700},{36,708},{44,716},{52,724},{60,... | collective-permute-start | bytes 399368 | tf_op jit(solution)/shard_map/ppermute | solution.py:20
  (19 other events, 242.4 us)

commit v9 on v8

--- a/solution.py
+++ b/solution.py
@@ -60,7 +60,7 @@
     sections = lax.axis_size("section")
     relay = 12
     bundled = (span_blocks - relay) // 2 + 1
-    plan = [(2 * j, 2 * j + 1) for j in range(relay // 2)]
+    plan = [(0, 1), (2, 3), (4, 9), (6, 11), (8, None), (10, None)]
     running = jnp.zeros((key_heads, group_size, row_count, head_size), jnp.float32)
     totals = jnp.zeros((key_heads, group_size, row_count), jnp.float32)
     best = jnp.full((key_heads, group_size, row_count), -1e30, jnp.float32)
@@ -115,16 +115,31 @@
         if first_distance == 0:
             joined = jnp.where(section_index == 0, packed, joined)
         held.append(joined)
+        if second_distance is None:
+            second_distance = span_blocks + 1
         carry = blend(carry, joined, jnp.where(section_index == 0, first_distance, second_distance))
     bundle = lax.ppermute(
         jnp.concatenate(held[:bundled], axis=1), ("ctx", "section"), both_pairs(relay, relay)
     )
-    for slot in range(bundled):
-        carry = blend(
-            carry,
-            bundle[:, slot * 2 * key_width:(slot + 1) * 2 * key_width],
-            relay + 2 * slot + jnp.where(section_index == 0, 0, 1),
-        )
+    forwarded = lax.ppermute(
+        jnp.concatenate(held[2:4], axis=1),
+        ("ctx", "section"),
+        [(i * sections, (i + 1) * sections + 1) for i in range(shards - 1)],
+    )
+    slots = [
+        (bundle, 0, forwarded, 0, relay, 5),
+        (bundle, 1, forwarded, 1, relay + 2, 7),
+        (bundle, 2, bundle, 0, relay + 4, relay + 1),
+        (bundle, 2, bundle, 1, span_blocks + 1, relay + 3),
+    ]
+    width_of = 2 * key_width
+    for first_array, first_slot, second_array, second_slot, first_distance, second_distance in slots:
+        joined = jnp.where(
+            section_index == 0,
+            first_array[:, first_slot * width_of:(first_slot + 1) * width_of],
+            second_array[:, second_slot * width_of:(second_slot + 1) * width_of],
+        )
+        carry = blend(carry, joined, jnp.where(section_index == 0, first_distance, second_distance))
     running, totals, best = carry
     partial = lax.ppermute(
         jnp.concatenate([running, totals[..., None], best[..., None]], axis=-1),

time: 206 us -> 199 us (0.966)
  waiting for transfers between devices: 57 us -> 49.1 us
    ppermute x6, waiting for transfers between devices: 15.7 us -> 4.39 us  [body(): lax.ppermute(packed, ('ctx', 'section'), both_pairs(first_distance, secon...]
    ppermute x6, starting transfers between devices: 34.6 us -> 24.4 us  [body(): lax.ppermute(packed, ('ctx', 'section'), both_pairs(first_distance, secon...]
    ppermute x1, waiting for transfers between devices: 0.49 us -> 7.12 us  [body(): lax.ppermute(jnp.concatenate(held[:bundled], axis=1), ('ctx', 'section'),...]
    ppermute x1, starting transfers between devices: 3.27 us -> 7.91 us  [body(): lax.ppermute(jnp.concatenate(held[:bundled], axis=1), ('ctx', 'section'),...]
    ppermute x13, waiting for transfers between devices: 14.6 us -> 10.7 us  [passed_along(): return lax.ppermute(x, ('ctx', 'section'), pairs)]
    ppermute x1, starting transfers between devices: 1.32 us -> 4.62 us  [body(): lax.ppermute(jnp.concatenate([running, totals[..., None], best[..., None]...]
    and x9 -> x10, other arithmetic: 5.68 us -> 6.33 us  [blend(): (source >= 0) & (positions < lengths[jnp.clip(source, 0, shards - 1)])]
  transfers between devices with their start and end apart: 29 -> 30, of which waited for: 12 -> 10; matrix products, arithmetic and copies ran while one was open for 12% -> 11% of each run, Pallas kernels for 0% -> 0%
where the time goes in v9:
time: 199 us; the launch traced here: 198 us
  starting transfers between devices  98.9 us (50%)
  waiting for transfers between devices  49.1 us (25%)
  other arithmetic  26.1 us (13%)
  matrix products  14.4 us (7%)
  local copies, waits for them, and re-layouts  7.12 us (4%)
  between operations  2.07 us (1%)
    ppermute x13, starting transfers between devices, passed_along(): return lax.ppermute(x, ('ctx', 'section'), pairs)  51.3 us
    ppermute x4, waiting for transfers between devices, body(): lax.ppermute(own_hidden, ('section', 'tp'), [(m, members + (m + step) % m...  24.7 us
    ppermute x6, starting transfers between devices, body(): lax.ppermute(packed, ('ctx', 'section'), both_pairs(first_distance, secon...  24.4 us
    ppermute x13, waiting for transfers between devices, passed_along(): return lax.ppermute(x, ('ctx', 'section'), pairs)  10.7 us
    ppermute x1, starting transfers between devices, body(): lax.ppermute(jnp.concatenate(held[:bundled], axis=1), ('ctx', 'section'),...  7.91 us
    ppermute x1, waiting for transfers between devices, body(): lax.ppermute(jnp.concatenate(held[:bundled], axis=1), ('ctx', 'section'),...  7.12 us
    and x10, other arithmetic, blend(): (source >= 0) & (positions < lengths[jnp.clip(source, 0, shards - 1)])  6.33 us
    ppermute x4, starting transfers between devices, body(): lax.ppermute(own_hidden, ('section', 'tp'), [(m, members + (m + step) % m...  5.17 us
  transfers between devices with their start and end apart: 30, of which 10 were waited for; matrix products, arithmetic and copies ran while one was open for 11% of the time, Pallas kernels for 0%

profile of v9, /device:TPU:1, one launch (start us, length us, event | category | flops | bytes accessed | tf_op | source)
XLA Modules:
  0.0 197.6 jit_solution(9482596901384356367)
XLA Ops:
  3.1 1.8 fusion.330
  12.4 2.1 %collective-permute-done = bf16[256,640]{1,0:T(8,128)(2,1)S(1)} collective-permute-done((bf16[256,640]{1,0:T(8,128)(2,1)S(1)}, bf16[256,640]{1,0:T(8,128)(2,1)S(1)}, u32[]{:S(2)}, u32[]{:S(2)}) %collective-permute-start) | collective-permute-done | bytes 327712 | tf_op jit(solution)/shard_map/ppermute | solution.py:52
  16.3 2.7 %collective-permute-start.1 = (bf16[256,256]{1,0:T(8,128)(2,1)S(1)}, bf16[256,256]{1,0:T(8,128)(2,1)S(1)}, u32[]{:S(2)}, u32[]{:S(2)}) collective-permute-start(bf16[256,256]{1,0:T(8,128)(2,1)S(1)} %pad_maximum_fusion.7), channel_id=1, source_target_pairs={{4,12},{12,20},{20,28},{28,36},{36,44},{44,52},{52,60},{60,68},{68... | collective-permute-start | bytes 393224 | tf_op jit(solution)/shard_map/ppermute | solution.py:114
  19.0 12.2 %collective-permute-start.4 = (bf16[256,256]{1,0:T(8,128)(2,1)S(1)}, bf16[256,256]{1,0:T(8,128)(2,1)S(1)}, u32[]{:S(2)}, u32[]{:S(2)}) collective-permute-start(bf16[256,256]{1,0:T(8,128)(2,1)S(1)} %pad_maximum_fusion.7), channel_id=1, source_target_pairs={{0,48},{8,56},{16,64},{24,72},{32,80},{40,88},{48,96},{56,104},{64... | collective-permute-start | bytes 393224 | tf_op jit(solution)/shard_map/ppermute | solution.py:114
  31.2 4.4 %collective-permute-start.3 = (bf16[256,256]{1,0:T(8,128)(2,1)S(1)}, bf16[256,256]{1,0:T(8,128)(2,1)S(1)}, u32[]{:S(2)}, u32[]{:S(2)}) collective-permute-start(bf16[256,256]{1,0:T(8,128)(2,1)S(1)} %pad_maximum_fusion.7), channel_id=1, source_target_pairs={{0,32},{8,40},{16,48},{24,56},{32,64},{40,72},{48,80},{56,88},{64,... | collective-permute-start | bytes 393224 | tf_op jit(solution)/shard_map/ppermute | solution.py:114
  35.6 3.7 %collective-permute-start.2 = (bf16[256,256]{1,0:T(8,128)(2,1)S(1)}, bf16[256,256]{1,0:T(8,128)(2,1)S(1)}, u32[]{:S(2)}, u32[]{:S(2)}) collective-permute-start(bf16[256,256]{1,0:T(8,128)(2,1)S(1)} %pad_maximum_fusion.7), channel_id=1, source_target_pairs={{0,16},{8,24},{16,32},{24,40},{32,48},{40,56},{48,64},{56,72},{64,... | collective-permute-start | bytes 393224 | tf_op jit(solution)/shard_map/ppermute | solution.py:114
  43.3 4.4 %collective-permute-done.2 = bf16[256,256]{1,0:T(8,128)(2,1)S(1)} collective-permute-done((bf16[256,256]{1,0:T(8,128)(2,1)S(1)}, bf16[256,256]{1,0:T(8,128)(2,1)S(1)}, u32[]{:S(2)}, u32[]{:S(2)}) %collective-permute-start.2) | collective-permute-done | bytes 131104 | tf_op jit(solution)/shard_map/ppermute | solution.py:114
  47.7 7.9 %collective-permute-start.7 = (bf16[256,768]{1,0:T(8,128)(2,1)S(1)}, bf16[256,768]{1,0:T(8,128)(2,1)S(1)}, u32[]{:S(2)}, u32[]{:S(2)}) collective-permute-start(bf16[256,768]{1,0:T(8,128)(2,1)S(1)} %pad_maximum_fusion.1), channel_id=1, source_target_pairs={{0,96},{8,104},{16,112},{24,120},{32,128},{40,136},{48,144},{56,15... | collective-permute-start | bytes 1179656 | tf_op jit(solution)/shard_map/ppermute | solution.py:121
  57.6 7.1 %collective-permute-done.7 = bf16[256,768]{1,0:T(8,128)(2,1)S(1)} collective-permute-done((bf16[256,768]{1,0:T(8,128)(2,1)S(1)}, bf16[256,768]{1,0:T(8,128)(2,1)S(1)}, u32[]{:S(2)}, u32[]{:S(2)}) %collective-permute-start.7) | collective-permute-done | bytes 393248 | tf_op jit(solution)/shard_map/ppermute | solution.py:121
  71.9 4.6 %collective-permute-start.9 = (f32[1,4,256,130]{2,1,3,0:T(4,128)S(1)}, f32[1,4,256,130]{2,1,3,0:T(4,128)S(1)}, u32[]{:S(2)}, u32[]{:S(2)}) collective-permute-start(f32[1,4,256,130]{2,1,3,0:T(4,128)S(1)} %copy.191), channel_id=1, source_target_pairs={{4,0},{5,1},{6,2},{7,3},{12,8},{13,9},{14,10},{15,11},{20,16},{21,... | collective-permute-start | bytes 1597448 | tf_op jit(solution)/shard_map/ppermute | solution.py:144
  78.2 3.2 %convolution_convert_fusion = bf16[256,3584]{1,0:T(8,128)(2,1)S(1)} fusion(bf16[256,512]{0,1:T(8,128)(2,1)S(1)} %bitcast.560, bf16[1,512,3584]{2,1,0:T(8,128)(2,1)} %param.14), kind=kOutput, calls=%fused_computation | convolution fusion | flops 940441600 | bytes 5767168 | tf_op jit(solution)/shard_map/dot_general | solution.py:158
  95.4 17.0 %collective-permute-done.16 = bf16[256,896]{1,0:T(8,128)(2,1)S(1)} collective-permute-done((bf16[256,896]{1,0:T(8,128)(2,1)S(1)}, bf16[256,896]{1,0:T(8,128)(2,1)S(1)}, u32[]{:S(2)}, u32[]{:S(2)}) %collective-permute-start.16) | collective-permute-done | bytes 458784 | tf_op jit(solution)/shard_map/ppermute | solution.py:175
  112.4 2.9 %collective-permute-done.15 = bf16[256,896]{1,0:T(8,128)(2,1)S(1)} collective-permute-done((bf16[256,896]{1,0:T(8,128)(2,1)S(1)}, bf16[256,896]{1,0:T(8,128)(2,1)S(1)}, u32[]{:S(2)}, u32[]{:S(2)}) %collective-permute-start.15) | collective-permute-done | bytes 458784 | tf_op jit(solution)/shard_map/ppermute | solution.py:175
  115.3 4.8 %collective-permute-done.14 = bf16[256,896]{1,0:T(8,128)(2,1)S(1)} collective-permute-done((bf16[256,896]{1,0:T(8,128)(2,1)S(1)}, bf16[256,896]{1,0:T(8,128)(2,1)S(1)}, u32[]{:S(2)}, u32[]{:S(2)}) %collective-permute-start.14) | collective-permute-done | bytes 458784 | tf_op jit(solution)/shard_map/ppermute | solution.py:175
  126.5 3.8 %collective-permute-start.17 = (bf16[1,130,4,128]{3,1,2,0:T(8,128)(2,1)S(1)}, bf16[1,130,4,128]{3,1,2,0:T(8,128)(2,1)S(1)}, u32[]{:S(2)}, u32[]{:S(2)}) collective-permute-start(bf16[1,130,4,128]{3,1,2,0:T(8,128)(2,1)S(1)} %pad_maximum_fusion.4), channel_id=1, source_target_pairs={{4,28},{12,36},{20,44},{28,52},{36,60},{44,68},{52,76},{60,84},{68... | collective-permute-start | bytes 399368 | tf_op jit(solution)/shard_map/ppermute | solution.py:20
  130.3 2.7 %collective-permute-start.18 = (bf16[1,130,4,128]{3,1,2,0:T(8,128)(2,1)S(1)}, bf16[1,130,4,128]{3,1,2,0:T(8,128)(2,1)S(1)}, u32[]{:S(2)}, u32[]{:S(2)}) collective-permute-start(bf16[1,130,4,128]{3,1,2,0:T(8,128)(2,1)S(1)} %pad_maximum_fusion.4), channel_id=1, source_target_pairs={{4,20},{12,28},{20,36},{28,44},{36,52},{44,60},{52,68},{60,76},{68... | collective-permute-start | bytes 399368 | tf_op jit(solution)/shard_map/ppermute | solution.py:20
  133.2 3.8 %collective-permute-done.18 = bf16[1,130,4,128]{3,1,2,0:T(8,128)(2,1)S(1)} collective-permute-done((bf16[1,130,4,128]{3,1,2,0:T(8,128)(2,1)S(1)}, bf16[1,130,4,128]{3,1,2,0:T(8,128)(2,1)S(1)}, u32[]{:S(2)}, u32[]{:S(2)}) %collective-permute-start.18) | collective-permute-done | bytes 133152 | tf_op jit(solution)/shard_map/ppermute | solution.py:20
  138.4 7.2 %collective-permute-start.22 = (bf16[1,130,4,128]{3,1,2,0:T(8,128)(2,1)S(1)}, bf16[1,130,4,128]{3,1,2,0:T(8,128)(2,1)}, u32[]{:S(2)}, u32[]{:S(2)}) collective-permute-start(bf16[1,130,4,128]{3,1,2,0:T(8,128)(2,1)S(1)} %pad_maximum_fusion.5), channel_id=1, source_target_pairs={{4,28},{12,36},{20,44},{28,52},{36,60},{44,68},{52,76},{60,84},{68... | collective-permute-start | bytes 399368 | tf_op jit(solution)/shard_map/ppermute | solution.py:20
  145.6 8.0 %collective-permute-start.20 = (bf16[1,130,4,128]{3,1,2,0:T(8,128)(2,1)S(1)}, bf16[1,130,4,128]{3,1,2,0:T(8,128)(2,1)}, u32[]{:S(2)}, u32[]{:S(2)}) collective-permute-start(bf16[1,130,4,128]{3,1,2,0:T(8,128)(2,1)S(1)} %pad_maximum_fusion.5), channel_id=1, source_target_pairs={{4,76},{12,84},{20,92},{28,100},{36,108},{44,116},{52,124},{60,132... | collective-permute-start | bytes 399368 | tf_op jit(solution)/shard_map/ppermute | solution.py:20
  153.6 4.7 %collective-permute-start.21 = (bf16[1,130,4,128]{3,1,2,0:T(8,128)(2,1)S(1)}, bf16[1,130,4,128]{3,1,2,0:T(8,128)(2,1)S(1)}, u32[]{:S(2)}, u32[]{:S(2)}) collective-permute-start(bf16[1,130,4,128]{3,1,2,0:T(8,128)(2,1)S(1)} %pad_maximum_fusion.5), channel_id=1, source_target_pairs={{4,52},{12,60},{20,68},{28,76},{36,84},{44,92},{52,100},{60,108},{... | collective-permute-start | bytes 399368 | tf_op jit(solution)/shard_map/ppermute | solution.py:20
  163.1 8.8 %collective-permute-start.29 = (bf16[1,130,4,128]{3,1,2,0:T(8,128)(2,1)S(1)}, bf16[1,130,4,128]{3,1,2,0:T(8,128)(2,1)S(1)}, u32[]{:S(2)}, u32[]{:S(2)}) collective-permute-start(bf16[1,130,4,128]{3,1,2,0:T(8,128)(2,1)S(1)} %pad_maximum_fusion.6), channel_id=1, source_target_pairs={{4,100},{12,108},{20,116},{28,124},{36,132},{44,140},{52,148},{60,... | collective-permute-start | bytes 399368 | tf_op jit(solution)/shard_map/ppermute | solution.py:20
  172.7 7.0 %collective-permute-start.28 = (bf16[1,130,4,128]{3,1,2,0:T(8,128)(2,1)S(1)}, bf16[1,130,4,128]{3,1,2,0:T(8,128)(2,1)S(1)}, u32[]{:S(2)}, u32[]{:S(2)}) collective-permute-start(bf16[1,130,4,128]{3,1,2,0:T(8,128)(2,1)S(1)} %pad_maximum_fusion.6), channel_id=1, source_target_pairs={{4,196},{12,204},{20,212},{28,220},{36,228},{44,236},{52,244},{60,... | collective-permute-start | bytes 399368 | tf_op jit(solution)/shard_map/ppermute | solution.py:20
  179.8 2.1 %collective-permute-start.27 = (bf16[1,130,4,128]{3,1,2,0:T(8,128)(2,1)S(1)}, bf16[1,130,4,128]{3,1,2,0:T(8,128)(2,1)S(1)}, u32[]{:S(2)}, u32[]{:S(2)}) collective-permute-start(bf16[1,130,4,128]{3,1,2,0:T(8,128)(2,1)S(1)} %pad_maximum_fusion.6), channel_id=1, source_target_pairs={{4,292},{12,300},{20,308},{28,316},{36,324},{44,332},{52,340},{60,... | collective-permute-start | bytes 399368 | tf_op jit(solution)/shard_map/ppermute | solution.py:20
  188.3 4.0 %collective-permute-done.25 = bf16[1,130,4,128]{3,1,2,0:T(8,128)(2,1)S(1)} collective-permute-done((bf16[1,130,4,128]{3,1,2,0:T(8,128)(2,1)S(1)}, bf16[1,130,4,128]{3,1,2,0:T(8,128)(2,1)S(1)}, u32[]{:S(2)}, u32[]{:S(2)}) %collective-permute-start.25) | collective-permute-done | bytes 133152 | tf_op jit(solution)/shard_map/ppermute | solution.py:20
  (202 shorter events, 64.5 us)
Async XLA Ops:
  1.7 12.9 %collective-permute-start = (bf16[256,640]{1,0:T(8,128)(2,1)S(1)}, bf16[256,640]{1,0:T(8,128)(2,1)S(1)}, u32[]{:S(2)}, u32[]{:S(2)}) collective-permute-start(bf16[256,640]{1,0:T(8,128)(2,1)S(1)} %pad_maximum_fusion.2), channel_id=1, source_target_pairs={{0,4},{1,5},{2,6},{3,7},{8,12},{9,13},{10,14},{11,15},{16,20},{17,... | collective-permute-start | bytes 983048 | tf_op jit(solution)/shard_map/ppermute | solution.py:52
  16.3 26.1 %collective-permute-start.1 = (bf16[256,256]{1,0:T(8,128)(2,1)S(1)}, bf16[256,256]{1,0:T(8,128)(2,1)S(1)}, u32[]{:S(2)}, u32[]{:S(2)}) collective-permute-start(bf16[256,256]{1,0:T(8,128)(2,1)S(1)} %pad_maximum_fusion.7), channel_id=1, source_target_pairs={{4,12},{12,20},{20,28},{28,36},{36,44},{44,52},{52,60},{60,68},{68... | collective-permute-start | bytes 393224 | tf_op jit(solution)/shard_map/ppermute | solution.py:114
  19.0 22.0 %collective-permute-start.4 = (bf16[256,256]{1,0:T(8,128)(2,1)S(1)}, bf16[256,256]{1,0:T(8,128)(2,1)S(1)}, u32[]{:S(2)}, u32[]{:S(2)}) collective-permute-start(bf16[256,256]{1,0:T(8,128)(2,1)S(1)} %pad_maximum_fusion.7), channel_id=1, source_target_pairs={{0,48},{8,56},{16,64},{24,72},{32,80},{40,88},{48,96},{56,104},{64... | collective-permute-start | bytes 393224 | tf_op jit(solution)/shard_map/ppermute | solution.py:114
  31.2 10.5 %collective-permute-start.3 = (bf16[256,256]{1,0:T(8,128)(2,1)S(1)}, bf16[256,256]{1,0:T(8,128)(2,1)S(1)}, u32[]{:S(2)}, u32[]{:S(2)}) collective-permute-start(bf16[256,256]{1,0:T(8,128)(2,1)S(1)} %pad_maximum_fusion.7), channel_id=1, source_target_pairs={{0,32},{8,40},{16,48},{24,56},{32,64},{40,72},{48,80},{56,88},{64,... | collective-permute-start | bytes 393224 | tf_op jit(solution)/shard_map/ppermute | solution.py:114
  35.6 12.1 %collective-permute-start.2 = (bf16[256,256]{1,0:T(8,128)(2,1)S(1)}, bf16[256,256]{1,0:T(8,128)(2,1)S(1)}, u32[]{:S(2)}, u32[]{:S(2)}) collective-permute-start(bf16[256,256]{1,0:T(8,128)(2,1)S(1)} %pad_maximum_fusion.7), channel_id=1, source_target_pairs={{0,16},{8,24},{16,32},{24,40},{32,48},{40,56},{48,64},{56,72},{64,... | collective-permute-start | bytes 393224 | tf_op jit(solution)/shard_map/ppermute | solution.py:114
  39.3 17.6 %collective-permute-start.6 = (bf16[256,256]{1,0:T(8,128)(2,1)S(1)}, bf16[256,256]{1,0:T(8,128)(2,1)S(1)}, u32[]{:S(2)}, u32[]{:S(2)}) collective-permute-start(bf16[256,256]{1,0:T(8,128)(2,1)S(1)} %pad_maximum_fusion.7), channel_id=1, source_target_pairs={{0,80},{8,88},{16,96},{24,104},{32,112},{40,120},{48,128},{56,136}... | collective-permute-start | bytes 393224 | tf_op jit(solution)/shard_map/ppermute | solution.py:114
  41.0 16.3 %collective-permute-start.5 = (bf16[256,256]{1,0:T(8,128)(2,1)S(1)}, bf16[256,256]{1,0:T(8,128)(2,1)S(1)}, u32[]{:S(2)}, u32[]{:S(2)}) collective-permute-start(bf16[256,256]{1,0:T(8,128)(2,1)S(1)} %pad_maximum_fusion.7), channel_id=1, source_target_pairs={{0,64},{8,72},{16,80},{24,88},{32,96},{40,104},{48,112},{56,120},{... | collective-permute-start | bytes 393224 | tf_op jit(solution)/shard_map/ppermute | solution.py:114
  41.7 15.9 %collective-permute-start.8 = (bf16[256,512]{1,0:T(8,128)(2,1)S(1)}, bf16[256,512]{1,0:T(8,128)(2,1)S(1)}, u32[]{:S(2)}, u32[]{:S(2)}) collective-permute-start(bf16[256,512]{1,0:T(8,128)(2,1)S(1)} %pad_maximum_fusion.3), channel_id=1, source_target_pairs={{0,12},{8,20},{16,28},{24,36},{32,44},{40,52},{48,60},{56,68},{64,... | collective-permute-start | bytes 786440 | tf_op jit(solution)/shard_map/ppermute | solution.py:124
  47.7 17.0 %collective-permute-start.7 = (bf16[256,768]{1,0:T(8,128)(2,1)S(1)}, bf16[256,768]{1,0:T(8,128)(2,1)S(1)}, u32[]{:S(2)}, u32[]{:S(2)}) collective-permute-start(bf16[256,768]{1,0:T(8,128)(2,1)S(1)} %pad_maximum_fusion.1), channel_id=1, source_target_pairs={{0,96},{8,104},{16,112},{24,120},{32,128},{40,136},{48,144},{56,15... | collective-permute-start | bytes 1179656 | tf_op jit(solution)/shard_map/ppermute | solution.py:121
  89.3 23.0 %collective-permute-start.16 = (bf16[256,896]{1,0:T(8,128)(2,1)S(1)}, bf16[256,896]{1,0:T(8,128)(2,1)S(1)}, u32[]{:S(2)}, u32[]{:S(2)}) collective-permute-start(bf16[256,896]{1,0:T(8,128)(2,1)S(1)} %add_convert_fusion), channel_id=1, source_target_pairs={{0,7},{1,4},{2,5},{3,6},{8,15},{9,12},{10,13},{11,14},{16,23},{17,... | collective-permute-start | bytes 1376264 | tf_op jit(solution)/shard_map/ppermute | solution.py:175
  90.6 24.7 %collective-permute-start.15 = (bf16[256,896]{1,0:T(8,128)(2,1)S(1)}, bf16[256,896]{1,0:T(8,128)(2,1)S(1)}, u32[]{:S(2)}, u32[]{:S(2)}) collective-permute-start(bf16[256,896]{1,0:T(8,128)(2,1)S(1)} %add_convert_fusion), channel_id=1, source_target_pairs={{0,6},{1,7},{2,4},{3,5},{8,14},{9,15},{10,12},{11,13},{16,22},{17,... | collective-permute-start | bytes 1376264 | tf_op jit(solution)/shard_map/ppermute | solution.py:175
  91.9 28.2 %collective-permute-start.14 = (bf16[256,896]{1,0:T(8,128)(2,1)S(1)}, bf16[256,896]{1,0:T(8,128)(2,1)S(1)}, u32[]{:S(2)}, u32[]{:S(2)}) collective-permute-start(bf16[256,896]{1,0:T(8,128)(2,1)S(1)} %add_convert_fusion), channel_id=1, source_target_pairs={{0,5},{1,6},{2,7},{3,4},{8,13},{9,14},{10,15},{11,12},{16,21},{17,... | collective-permute-start | bytes 1376264 | tf_op jit(solution)/shard_map/ppermute | solution.py:175
  93.2 26.9 %collective-permute-start.13 = (bf16[256,896]{1,0:T(8,128)(2,1)S(1)}, bf16[256,896]{1,0:T(8,128)(2,1)S(1)}, u32[]{:S(2)}, u32[]{:S(2)}) collective-permute-start(bf16[256,896]{1,0:T(8,128)(2,1)S(1)} %add_convert_fusion), channel_id=1, source_target_pairs={{0,4},{1,5},{2,6},{3,7},{8,12},{9,13},{10,14},{11,15},{16,20},{17,... | collective-permute-start | bytes 1376264 | tf_op jit(solution)/shard_map/ppermute | solution.py:175
  125.2 8.0 %collective-permute-start.19 = (bf16[1,130,4,128]{3,1,2,0:T(8,128)(2,1)S(1)}, bf16[1,130,4,128]{3,1,2,0:T(8,128)(2,1)S(1)}, u32[]{:S(2)}, u32[]{:S(2)}) collective-permute-start(bf16[1,130,4,128]{3,1,2,0:T(8,128)(2,1)S(1)} %pad_maximum_fusion.4), channel_id=1, source_target_pairs={{4,12},{12,20},{20,28},{28,36},{36,44},{44,52},{52,60},{60,68},{68... | collective-permute-start | bytes 399368 | tf_op jit(solution)/shard_map/ppermute | solution.py:20
  130.3 6.8 %collective-permute-start.18 = (bf16[1,130,4,128]{3,1,2,0:T(8,128)(2,1)S(1)}, bf16[1,130,4,128]{3,1,2,0:T(8,128)(2,1)S(1)}, u32[]{:S(2)}, u32[]{:S(2)}) collective-permute-start(bf16[1,130,4,128]{3,1,2,0:T(8,128)(2,1)S(1)} %pad_maximum_fusion.4), channel_id=1, source_target_pairs={{4,20},{12,28},{20,36},{28,44},{36,52},{44,60},{52,68},{60,76},{68... | collective-permute-start | bytes 399368 | tf_op jit(solution)/shard_map/ppermute | solution.py:20
  138.4 21.2 %collective-permute-start.22 = (bf16[1,130,4,128]{3,1,2,0:T(8,128)(2,1)S(1)}, bf16[1,130,4,128]{3,1,2,0:T(8,128)(2,1)}, u32[]{:S(2)}, u32[]{:S(2)}) collective-permute-start(bf16[1,130,4,128]{3,1,2,0:T(8,128)(2,1)S(1)} %pad_maximum_fusion.5), channel_id=1, source_target_pairs={{4,28},{12,36},{20,44},{28,52},{36,60},{44,68},{52,76},{60,84},{68... | collective-permute-start | bytes 399368 | tf_op jit(solution)/shard_map/ppermute | solution.py:20
  145.6 14.9 %collective-permute-start.20 = (bf16[1,130,4,128]{3,1,2,0:T(8,128)(2,1)S(1)}, bf16[1,130,4,128]{3,1,2,0:T(8,128)(2,1)}, u32[]{:S(2)}, u32[]{:S(2)}) collective-permute-start(bf16[1,130,4,128]{3,1,2,0:T(8,128)(2,1)S(1)} %pad_maximum_fusion.5), channel_id=1, source_target_pairs={{4,76},{12,84},{20,92},{28,100},{36,108},{44,116},{52,124},{60,132... | collective-permute-start | bytes 399368 | tf_op jit(solution)/shard_map/ppermute | solution.py:20
  153.6 7.9 %collective-permute-start.21 = (bf16[1,130,4,128]{3,1,2,0:T(8,128)(2,1)S(1)}, bf16[1,130,4,128]{3,1,2,0:T(8,128)(2,1)S(1)}, u32[]{:S(2)}, u32[]{:S(2)}) collective-permute-start(bf16[1,130,4,128]{3,1,2,0:T(8,128)(2,1)S(1)} %pad_maximum_fusion.5), channel_id=1, source_target_pairs={{4,52},{12,60},{20,68},{28,76},{36,84},{44,92},{52,100},{60,108},{... | collective-permute-start | bytes 399368 | tf_op jit(solution)/shard_map/ppermute | solution.py:20
  163.1 21.7 %collective-permute-start.29 = (bf16[1,130,4,128]{3,1,2,0:T(8,128)(2,1)S(1)}, bf16[1,130,4,128]{3,1,2,0:T(8,128)(2,1)S(1)}, u32[]{:S(2)}, u32[]{:S(2)}) collective-permute-start(bf16[1,130,4,128]{3,1,2,0:T(8,128)(2,1)S(1)} %pad_maximum_fusion.6), channel_id=1, source_target_pairs={{4,100},{12,108},{20,116},{28,124},{36,132},{44,140},{52,148},{60,... | collective-permute-start | bytes 399368 | tf_op jit(solution)/shard_map/ppermute | solution.py:20
  172.7 14.0 %collective-permute-start.28 = (bf16[1,130,4,128]{3,1,2,0:T(8,128)(2,1)S(1)}, bf16[1,130,4,128]{3,1,2,0:T(8,128)(2,1)S(1)}, u32[]{:S(2)}, u32[]{:S(2)}) collective-permute-start(bf16[1,130,4,128]{3,1,2,0:T(8,128)(2,1)S(1)} %pad_maximum_fusion.6), channel_id=1, source_target_pairs={{4,196},{12,204},{20,212},{28,220},{36,228},{44,236},{52,244},{60,... | collective-permute-start | bytes 399368 | tf_op jit(solution)/shard_map/ppermute | solution.py:20
  179.8 8.5 %collective-permute-start.27 = (bf16[1,130,4,128]{3,1,2,0:T(8,128)(2,1)S(1)}, bf16[1,130,4,128]{3,1,2,0:T(8,128)(2,1)S(1)}, u32[]{:S(2)}, u32[]{:S(2)}) collective-permute-start(bf16[1,130,4,128]{3,1,2,0:T(8,128)(2,1)S(1)} %pad_maximum_fusion.6), channel_id=1, source_target_pairs={{4,292},{12,300},{20,308},{28,316},{36,324},{44,332},{52,340},{60,... | collective-permute-start | bytes 399368 | tf_op jit(solution)/shard_map/ppermute | solution.py:20
  183.5 8.8 %collective-permute-start.25 = (bf16[1,130,4,128]{3,1,2,0:T(8,128)(2,1)S(1)}, bf16[1,130,4,128]{3,1,2,0:T(8,128)(2,1)S(1)}, u32[]{:S(2)}, u32[]{:S(2)}) collective-permute-start(bf16[1,130,4,128]{3,1,2,0:T(8,128)(2,1)S(1)} %pad_maximum_fusion.6), channel_id=1, source_target_pairs={{4,484},{12,492},{20,500},{28,508},{36,516},{44,524},{52,532},{60,... | collective-permute-start | bytes 399368 | tf_op jit(solution)/shard_map/ppermute | solution.py:20
  184.8 9.0 %collective-permute-start.24 = (bf16[1,130,4,128]{3,1,2,0:T(8,128)(2,1)S(1)}, bf16[1,130,4,128]{3,1,2,0:T(8,128)(2,1)S(1)}, u32[]{:S(2)}, u32[]{:S(2)}) collective-permute-start(bf16[1,130,4,128]{3,1,2,0:T(8,128)(2,1)S(1)} %pad_maximum_fusion.6), channel_id=1, source_target_pairs={{4,580},{12,588},{20,596},{28,604},{36,612},{44,620},{52,628},{60,... | collective-permute-start | bytes 399368 | tf_op jit(solution)/shard_map/ppermute | solution.py:20
  186.7 8.6 %collective-permute-start.23 = (bf16[1,130,4,128]{3,1,2,0:T(8,128)(2,1)S(1)}, bf16[1,130,4,128]{3,1,2,0:T(8,128)(2,1)S(1)}, u32[]{:S(2)}, u32[]{:S(2)}) collective-permute-start(bf16[1,130,4,128]{3,1,2,0:T(8,128)(2,1)S(1)} %pad_maximum_fusion.6), channel_id=1, source_target_pairs={{4,676},{12,684},{20,692},{28,700},{36,708},{44,716},{52,724},{60,... | collective-permute-start | bytes 399368 | tf_op jit(solution)/shard_map/ppermute | solution.py:20
  (20 other events, 255.7 us)

commit v10 on v9

--- a/solution.py
+++ b/solution.py
@@ -236,11 +236,11 @@
     total_rows = jnp.broadcast_to(cumulated[-1][:, None, :, None], (key_heads, 1, group_size, head_size))
     own_entry = jnp.concatenate([total_rows, fresh_state], axis=1)
     entry = sent_along(own_entry, 1)
-    for times in range(2, 4):
+    for times in range(2, 5):
         entry = chain(sent_along(own_entry, times), entry)
-    reach = 3
+    reach = 4
     while reach < shards:
-        spread = 4 if reach < 12 else -(-shards // reach)
+        spread = 3 if reach < 12 else -(-shards // reach)
         joined = entry
         for times in range(1, spread):
             joined = chain(sent_along(entry, times * reach), joined)

time: 199 us -> 200 us (level)
  waiting for transfers between devices: 49.1 us -> 54.1 us
  starting transfers between devices: 98.9 us -> 96.4 us
    ppermute x13, waiting for transfers between devices: 10.7 us -> 15.8 us  [passed_along(): return lax.ppermute(x, ('ctx', 'section'), pairs)]
    ppermute x13, starting transfers between devices: 51.3 us -> 48.8 us  [passed_along(): return lax.ppermute(x, ('ctx', 'section'), pairs)]
  transfers between devices with their start and end apart: 30 -> 30, of which waited for: 10 -> 12; matrix products, arithmetic and copies ran while one was open for 11% -> 10% of each run, Pallas kernels for 0% -> 0%
where the time goes in v10:
time: 200 us; the launch traced here: 199 us
  starting transfers between devices  96.4 us (48%)
  waiting for transfers between devices  54.1 us (27%)
  other arithmetic  25.2 us (13%)
  matrix products  13.8 us (7%)
  local copies, waits for them, and re-layouts  7.08 us (4%)
  between operations  2.07 us (1%)
    ppermute x13, starting transfers between devices, passed_along(): return lax.ppermute(x, ('ctx', 'section'), pairs)  48.8 us
    ppermute x4, waiting for transfers between devices, body(): lax.ppermute(own_hidden, ('section', 'tp'), [(m, members + (m + step) % m...  24.7 us
    ppermute x6, starting transfers between devices, body(): lax.ppermute(packed, ('ctx', 'section'), both_pairs(first_distance, secon...  24.4 us
    ppermute x13, waiting for transfers between devices, passed_along(): return lax.ppermute(x, ('ctx', 'section'), pairs)  15.8 us
    ppermute x1, starting transfers between devices, body(): lax.ppermute(jnp.concatenate(held[:bundled], axis=1), ('ctx', 'section'),...  7.91 us
    ppermute x1, waiting for transfers between devices, body(): lax.ppermute(jnp.concatenate(held[:bundled], axis=1), ('ctx', 'section'),...  7.12 us
    and x10, other arithmetic, blend(): (source >= 0) & (positions < lengths[jnp.clip(source, 0, shards - 1)])  6.35 us
    ppermute x4, starting transfers between devices, body(): lax.ppermute(own_hidden, ('section', 'tp'), [(m, members + (m + step) % m...  5.17 us
  transfers between devices with their start and end apart: 30, of which 12 were waited for; matrix products, arithmetic and copies ran while one was open for 10% of the time, Pallas kernels for 0%

profile of v10, /device:TPU:1, one launch (start us, length us, event | category | flops | bytes accessed | tf_op | source)
XLA Modules:
  0.0 198.7 jit_solution(12206672167517748911)
XLA Ops:
  12.4 2.2 %collective-permute-done = bf16[256,640]{1,0:T(8,128)(2,1)S(1)} collective-permute-done((bf16[256,640]{1,0:T(8,128)(2,1)S(1)}, bf16[256,640]{1,0:T(8,128)(2,1)S(1)}, u32[]{:S(2)}, u32[]{:S(2)}) %collective-permute-start) | collective-permute-done | bytes 327712 | tf_op jit(solution)/shard_map/ppermute | solution.py:52
  16.3 2.7 %collective-permute-start.1 = (bf16[256,256]{1,0:T(8,128)(2,1)S(1)}, bf16[256,256]{1,0:T(8,128)(2,1)S(1)}, u32[]{:S(2)}, u32[]{:S(2)}) collective-permute-start(bf16[256,256]{1,0:T(8,128)(2,1)S(1)} %pad_maximum_fusion.7), channel_id=1, source_target_pairs={{4,12},{12,20},{20,28},{28,36},{36,44},{44,52},{52,60},{60,68},{68... | collective-permute-start | bytes 393224 | tf_op jit(solution)/shard_map/ppermute | solution.py:114
  19.0 12.2 %collective-permute-start.4 = (bf16[256,256]{1,0:T(8,128)(2,1)S(1)}, bf16[256,256]{1,0:T(8,128)(2,1)S(1)}, u32[]{:S(2)}, u32[]{:S(2)}) collective-permute-start(bf16[256,256]{1,0:T(8,128)(2,1)S(1)} %pad_maximum_fusion.7), channel_id=1, source_target_pairs={{0,48},{8,56},{16,64},{24,72},{32,80},{40,88},{48,96},{56,104},{64... | collective-permute-start | bytes 393224 | tf_op jit(solution)/shard_map/ppermute | solution.py:114
  31.2 4.4 %collective-permute-start.3 = (bf16[256,256]{1,0:T(8,128)(2,1)S(1)}, bf16[256,256]{1,0:T(8,128)(2,1)S(1)}, u32[]{:S(2)}, u32[]{:S(2)}) collective-permute-start(bf16[256,256]{1,0:T(8,128)(2,1)S(1)} %pad_maximum_fusion.7), channel_id=1, source_target_pairs={{0,32},{8,40},{16,48},{24,56},{32,64},{40,72},{48,80},{56,88},{64,... | collective-permute-start | bytes 393224 | tf_op jit(solution)/shard_map/ppermute | solution.py:114
  35.6 3.7 %collective-permute-start.2 = (bf16[256,256]{1,0:T(8,128)(2,1)S(1)}, bf16[256,256]{1,0:T(8,128)(2,1)S(1)}, u32[]{:S(2)}, u32[]{:S(2)}) collective-permute-start(bf16[256,256]{1,0:T(8,128)(2,1)S(1)} %pad_maximum_fusion.7), channel_id=1, source_target_pairs={{0,16},{8,24},{16,32},{24,40},{32,48},{40,56},{48,64},{56,72},{64,... | collective-permute-start | bytes 393224 | tf_op jit(solution)/shard_map/ppermute | solution.py:114
  43.3 4.4 %collective-permute-done.2 = bf16[256,256]{1,0:T(8,128)(2,1)S(1)} collective-permute-done((bf16[256,256]{1,0:T(8,128)(2,1)S(1)}, bf16[256,256]{1,0:T(8,128)(2,1)S(1)}, u32[]{:S(2)}, u32[]{:S(2)}) %collective-permute-start.2) | collective-permute-done | bytes 131104 | tf_op jit(solution)/shard_map/ppermute | solution.py:114
  47.7 7.9 %collective-permute-start.7 = (bf16[256,768]{1,0:T(8,128)(2,1)S(1)}, bf16[256,768]{1,0:T(8,128)(2,1)S(1)}, u32[]{:S(2)}, u32[]{:S(2)}) collective-permute-start(bf16[256,768]{1,0:T(8,128)(2,1)S(1)} %pad_maximum_fusion.1), channel_id=1, source_target_pairs={{0,96},{8,104},{16,112},{24,120},{32,128},{40,136},{48,144},{56,15... | collective-permute-start | bytes 1179656 | tf_op jit(solution)/shard_map/ppermute | solution.py:121
  57.6 7.1 %collective-permute-done.7 = bf16[256,768]{1,0:T(8,128)(2,1)S(1)} collective-permute-done((bf16[256,768]{1,0:T(8,128)(2,1)S(1)}, bf16[256,768]{1,0:T(8,128)(2,1)S(1)}, u32[]{:S(2)}, u32[]{:S(2)}) %collective-permute-start.7) | collective-permute-done | bytes 393248 | tf_op jit(solution)/shard_map/ppermute | solution.py:121
  71.9 4.6 %collective-permute-start.9 = (f32[1,4,256,130]{2,1,3,0:T(4,128)S(1)}, f32[1,4,256,130]{2,1,3,0:T(4,128)S(1)}, u32[]{:S(2)}, u32[]{:S(2)}) collective-permute-start(f32[1,4,256,130]{2,1,3,0:T(4,128)S(1)} %copy.191), channel_id=1, source_target_pairs={{4,0},{5,1},{6,2},{7,3},{12,8},{13,9},{14,10},{15,11},{20,16},{21,... | collective-permute-start | bytes 1597448 | tf_op jit(solution)/shard_map/ppermute | solution.py:144
  78.2 3.2 %convolution_convert_fusion = bf16[256,3584]{1,0:T(8,128)(2,1)S(1)} fusion(bf16[256,512]{0,1:T(8,128)(2,1)S(1)} %bitcast.560, bf16[1,512,3584]{2,1,0:T(8,128)(2,1)} %param.14), kind=kOutput, calls=%fused_computation | convolution fusion | flops 940441600 | bytes 5767168 | tf_op jit(solution)/shard_map/dot_general | solution.py:158
  95.4 16.9 %collective-permute-done.16 = bf16[256,896]{1,0:T(8,128)(2,1)S(1)} collective-permute-done((bf16[256,896]{1,0:T(8,128)(2,1)S(1)}, bf16[256,896]{1,0:T(8,128)(2,1)S(1)}, u32[]{:S(2)}, u32[]{:S(2)}) %collective-permute-start.16) | collective-permute-done | bytes 458784 | tf_op jit(solution)/shard_map/ppermute | solution.py:175
  112.4 2.9 %collective-permute-done.15 = bf16[256,896]{1,0:T(8,128)(2,1)S(1)} collective-permute-done((bf16[256,896]{1,0:T(8,128)(2,1)S(1)}, bf16[256,896]{1,0:T(8,128)(2,1)S(1)}, u32[]{:S(2)}, u32[]{:S(2)}) %collective-permute-start.15) | collective-permute-done | bytes 458784 | tf_op jit(solution)/shard_map/ppermute | solution.py:175
  115.3 4.8 %collective-permute-done.14 = bf16[256,896]{1,0:T(8,128)(2,1)S(1)} collective-permute-done((bf16[256,896]{1,0:T(8,128)(2,1)S(1)}, bf16[256,896]{1,0:T(8,128)(2,1)S(1)}, u32[]{:S(2)}, u32[]{:S(2)}) %collective-permute-start.14) | collective-permute-done | bytes 458784 | tf_op jit(solution)/shard_map/ppermute | solution.py:175
  126.5 4.6 %collective-permute-start.17 = (bf16[1,130,4,128]{3,1,2,0:T(8,128)(2,1)S(1)}, bf16[1,130,4,128]{3,1,2,0:T(8,128)(2,1)S(1)}, u32[]{:S(2)}, u32[]{:S(2)}) collective-permute-start(bf16[1,130,4,128]{3,1,2,0:T(8,128)(2,1)S(1)} %pad_maximum_fusion.4), channel_id=1, source_target_pairs={{4,36},{12,44},{20,52},{28,60},{36,68},{44,76},{52,84},{60,92},{68... | collective-permute-start | bytes 399368 | tf_op jit(solution)/shard_map/ppermute | solution.py:20
  131.1 3.3 %collective-permute-start.18 = (bf16[1,130,4,128]{3,1,2,0:T(8,128)(2,1)S(1)}, bf16[1,130,4,128]{3,1,2,0:T(8,128)(2,1)S(1)}, u32[]{:S(2)}, u32[]{:S(2)}) collective-permute-start(bf16[1,130,4,128]{3,1,2,0:T(8,128)(2,1)S(1)} %pad_maximum_fusion.4), channel_id=1, source_target_pairs={{4,28},{12,36},{20,44},{28,52},{36,60},{44,68},{52,76},{60,84},{68... | collective-permute-start | bytes 399368 | tf_op jit(solution)/shard_map/ppermute | solution.py:20
  134.4 3.9 %collective-permute-start.19 = (bf16[1,130,4,128]{3,1,2,0:T(8,128)(2,1)S(1)}, bf16[1,130,4,128]{3,1,2,0:T(8,128)(2,1)S(1)}, u32[]{:S(2)}, u32[]{:S(2)}) collective-permute-start(bf16[1,130,4,128]{3,1,2,0:T(8,128)(2,1)S(1)} %pad_maximum_fusion.4), channel_id=1, source_target_pairs={{4,20},{12,28},{20,36},{28,44},{36,52},{44,60},{52,68},{60,76},{68... | collective-permute-start | bytes 399368 | tf_op jit(solution)/shard_map/ppermute | solution.py:20
  138.5 4.7 %collective-permute-done.18 = bf16[1,130,4,128]{3,1,2,0:T(8,128)(2,1)S(1)} collective-permute-done((bf16[1,130,4,128]{3,1,2,0:T(8,128)(2,1)S(1)}, bf16[1,130,4,128]{3,1,2,0:T(8,128)(2,1)S(1)}, u32[]{:S(2)}, u32[]{:S(2)}) %collective-permute-start.18) | collective-permute-done | bytes 133152 | tf_op jit(solution)/shard_map/ppermute | solution.py:20
  146.7 7.4 %collective-permute-start.22 = (bf16[1,130,4,128]{3,1,2,0:T(8,128)(2,1)S(1)}, bf16[1,130,4,128]{3,1,2,0:T(8,128)(2,1)}, u32[]{:S(2)}, u32[]{:S(2)}) collective-permute-start(bf16[1,130,4,128]{3,1,2,0:T(8,128)(2,1)S(1)} %pad_maximum_fusion.5), channel_id=1, source_target_pairs={{4,36},{12,44},{20,52},{28,60},{36,68},{44,76},{52,84},{60,92},{68... | collective-permute-start | bytes 399368 | tf_op jit(solution)/shard_map/ppermute | solution.py:20
  154.1 7.2 %collective-permute-start.21 = (bf16[1,130,4,128]{3,1,2,0:T(8,128)(2,1)S(1)}, bf16[1,130,4,128]{3,1,2,0:T(8,128)(2,1)S(1)}, u32[]{:S(2)}, u32[]{:S(2)}) collective-permute-start(bf16[1,130,4,128]{3,1,2,0:T(8,128)(2,1)S(1)} %pad_maximum_fusion.5), channel_id=1, source_target_pairs={{4,68},{12,76},{20,84},{28,92},{36,100},{44,108},{52,116},{60,124}... | collective-permute-start | bytes 399368 | tf_op jit(solution)/shard_map/ppermute | solution.py:20
  163.0 2.1 %collective-permute-done.21 = bf16[1,130,4,128]{3,1,2,0:T(8,128)(2,1)S(1)} collective-permute-done((bf16[1,130,4,128]{3,1,2,0:T(8,128)(2,1)S(1)}, bf16[1,130,4,128]{3,1,2,0:T(8,128)(2,1)S(1)}, u32[]{:S(2)}, u32[]{:S(2)}) %collective-permute-start.21) | collective-permute-done | bytes 133152 | tf_op jit(solution)/shard_map/ppermute | solution.py:20
  166.7 5.3 %collective-permute-start.29 = (bf16[1,130,4,128]{3,1,2,0:T(8,128)(2,1)S(1)}, bf16[1,130,4,128]{3,1,2,0:T(8,128)(2,1)S(1)}, u32[]{:S(2)}, u32[]{:S(2)}) collective-permute-start(bf16[1,130,4,128]{3,1,2,0:T(8,128)(2,1)S(1)} %pad_maximum_fusion.6), channel_id=1, source_target_pairs={{4,100},{12,108},{20,116},{28,124},{36,132},{44,140},{52,148},{60,... | collective-permute-start | bytes 399368 | tf_op jit(solution)/shard_map/ppermute | solution.py:20
  172.8 6.1 %collective-permute-start.28 = (bf16[1,130,4,128]{3,1,2,0:T(8,128)(2,1)S(1)}, bf16[1,130,4,128]{3,1,2,0:T(8,128)(2,1)S(1)}, u32[]{:S(2)}, u32[]{:S(2)}) collective-permute-start(bf16[1,130,4,128]{3,1,2,0:T(8,128)(2,1)S(1)} %pad_maximum_fusion.6), channel_id=1, source_target_pairs={{4,196},{12,204},{20,212},{28,220},{36,228},{44,236},{52,244},{60,... | collective-permute-start | bytes 399368 | tf_op jit(solution)/shard_map/ppermute | solution.py:20
  178.9 4.1 %collective-permute-start.27 = (bf16[1,130,4,128]{3,1,2,0:T(8,128)(2,1)S(1)}, bf16[1,130,4,128]{3,1,2,0:T(8,128)(2,1)S(1)}, u32[]{:S(2)}, u32[]{:S(2)}) collective-permute-start(bf16[1,130,4,128]{3,1,2,0:T(8,128)(2,1)S(1)} %pad_maximum_fusion.6), channel_id=1, source_target_pairs={{4,292},{12,300},{20,308},{28,316},{36,324},{44,332},{52,340},{60,... | collective-permute-start | bytes 399368 | tf_op jit(solution)/shard_map/ppermute | solution.py:20
  189.4 4.0 %collective-permute-done.25 = bf16[1,130,4,128]{3,1,2,0:T(8,128)(2,1)S(1)} collective-permute-done((bf16[1,130,4,128]{3,1,2,0:T(8,128)(2,1)S(1)}, bf16[1,130,4,128]{3,1,2,0:T(8,128)(2,1)S(1)}, u32[]{:S(2)}, u32[]{:S(2)}) %collective-permute-start.25) | collective-permute-done | bytes 133152 | tf_op jit(solution)/shard_map/ppermute | solution.py:20
  (204 shorter events, 66.9 us)
Async XLA Ops:
  1.7 12.9 %collective-permute-start = (bf16[256,640]{1,0:T(8,128)(2,1)S(1)}, bf16[256,640]{1,0:T(8,128)(2,1)S(1)}, u32[]{:S(2)}, u32[]{:S(2)}) collective-permute-start(bf16[256,640]{1,0:T(8,128)(2,1)S(1)} %pad_maximum_fusion.2), channel_id=1, source_target_pairs={{0,4},{1,5},{2,6},{3,7},{8,12},{9,13},{10,14},{11,15},{16,20},{17,... | collective-permute-start | bytes 983048 | tf_op jit(solution)/shard_map/ppermute | solution.py:52
  16.3 26.1 %collective-permute-start.1 = (bf16[256,256]{1,0:T(8,128)(2,1)S(1)}, bf16[256,256]{1,0:T(8,128)(2,1)S(1)}, u32[]{:S(2)}, u32[]{:S(2)}) collective-permute-start(bf16[256,256]{1,0:T(8,128)(2,1)S(1)} %pad_maximum_fusion.7), channel_id=1, source_target_pairs={{4,12},{12,20},{20,28},{28,36},{36,44},{44,52},{52,60},{60,68},{68... | collective-permute-start | bytes 393224 | tf_op jit(solution)/shard_map/ppermute | solution.py:114
  19.0 22.0 %collective-permute-start.4 = (bf16[256,256]{1,0:T(8,128)(2,1)S(1)}, bf16[256,256]{1,0:T(8,128)(2,1)S(1)}, u32[]{:S(2)}, u32[]{:S(2)}) collective-permute-start(bf16[256,256]{1,0:T(8,128)(2,1)S(1)} %pad_maximum_fusion.7), channel_id=1, source_target_pairs={{0,48},{8,56},{16,64},{24,72},{32,80},{40,88},{48,96},{56,104},{64... | collective-permute-start | bytes 393224 | tf_op jit(solution)/shard_map/ppermute | solution.py:114
  31.2 10.5 %collective-permute-start.3 = (bf16[256,256]{1,0:T(8,128)(2,1)S(1)}, bf16[256,256]{1,0:T(8,128)(2,1)S(1)}, u32[]{:S(2)}, u32[]{:S(2)}) collective-permute-start(bf16[256,256]{1,0:T(8,128)(2,1)S(1)} %pad_maximum_fusion.7), channel_id=1, source_target_pairs={{0,32},{8,40},{16,48},{24,56},{32,64},{40,72},{48,80},{56,88},{64,... | collective-permute-start | bytes 393224 | tf_op jit(solution)/shard_map/ppermute | solution.py:114
  35.6 12.1 %collective-permute-start.2 = (bf16[256,256]{1,0:T(8,128)(2,1)S(1)}, bf16[256,256]{1,0:T(8,128)(2,1)S(1)}, u32[]{:S(2)}, u32[]{:S(2)}) collective-permute-start(bf16[256,256]{1,0:T(8,128)(2,1)S(1)} %pad_maximum_fusion.7), channel_id=1, source_target_pairs={{0,16},{8,24},{16,32},{24,40},{32,48},{40,56},{48,64},{56,72},{64,... | collective-permute-start | bytes 393224 | tf_op jit(solution)/shard_map/ppermute | solution.py:114
  39.3 17.6 %collective-permute-start.6 = (bf16[256,256]{1,0:T(8,128)(2,1)S(1)}, bf16[256,256]{1,0:T(8,128)(2,1)S(1)}, u32[]{:S(2)}, u32[]{:S(2)}) collective-permute-start(bf16[256,256]{1,0:T(8,128)(2,1)S(1)} %pad_maximum_fusion.7), channel_id=1, source_target_pairs={{0,80},{8,88},{16,96},{24,104},{32,112},{40,120},{48,128},{56,136}... | collective-permute-start | bytes 393224 | tf_op jit(solution)/shard_map/ppermute | solution.py:114
  41.0 16.3 %collective-permute-start.5 = (bf16[256,256]{1,0:T(8,128)(2,1)S(1)}, bf16[256,256]{1,0:T(8,128)(2,1)S(1)}, u32[]{:S(2)}, u32[]{:S(2)}) collective-permute-start(bf16[256,256]{1,0:T(8,128)(2,1)S(1)} %pad_maximum_fusion.7), channel_id=1, source_target_pairs={{0,64},{8,72},{16,80},{24,88},{32,96},{40,104},{48,112},{56,120},{... | collective-permute-start | bytes 393224 | tf_op jit(solution)/shard_map/ppermute | solution.py:114
  41.7 15.9 %collective-permute-start.8 = (bf16[256,512]{1,0:T(8,128)(2,1)S(1)}, bf16[256,512]{1,0:T(8,128)(2,1)S(1)}, u32[]{:S(2)}, u32[]{:S(2)}) collective-permute-start(bf16[256,512]{1,0:T(8,128)(2,1)S(1)} %pad_maximum_fusion.3), channel_id=1, source_target_pairs={{0,12},{8,20},{16,28},{24,36},{32,44},{40,52},{48,60},{56,68},{64,... | collective-permute-start | bytes 786440 | tf_op jit(solution)/shard_map/ppermute | solution.py:124
  47.7 17.0 %collective-permute-start.7 = (bf16[256,768]{1,0:T(8,128)(2,1)S(1)}, bf16[256,768]{1,0:T(8,128)(2,1)S(1)}, u32[]{:S(2)}, u32[]{:S(2)}) collective-permute-start(bf16[256,768]{1,0:T(8,128)(2,1)S(1)} %pad_maximum_fusion.1), channel_id=1, source_target_pairs={{0,96},{8,104},{16,112},{24,120},{32,128},{40,136},{48,144},{56,15... | collective-permute-start | bytes 1179656 | tf_op jit(solution)/shard_map/ppermute | solution.py:121
  89.3 23.0 %collective-permute-start.16 = (bf16[256,896]{1,0:T(8,128)(2,1)S(1)}, bf16[256,896]{1,0:T(8,128)(2,1)S(1)}, u32[]{:S(2)}, u32[]{:S(2)}) collective-permute-start(bf16[256,896]{1,0:T(8,128)(2,1)S(1)} %add_convert_fusion), channel_id=1, source_target_pairs={{0,7},{1,4},{2,5},{3,6},{8,15},{9,12},{10,13},{11,14},{16,23},{17,... | collective-permute-start | bytes 1376264 | tf_op jit(solution)/shard_map/ppermute | solution.py:175
  90.6 24.6 %collective-permute-start.15 = (bf16[256,896]{1,0:T(8,128)(2,1)S(1)}, bf16[256,896]{1,0:T(8,128)(2,1)S(1)}, u32[]{:S(2)}, u32[]{:S(2)}) collective-permute-start(bf16[256,896]{1,0:T(8,128)(2,1)S(1)} %add_convert_fusion), channel_id=1, source_target_pairs={{0,6},{1,7},{2,4},{3,5},{8,14},{9,15},{10,12},{11,13},{16,22},{17,... | collective-permute-start | bytes 1376264 | tf_op jit(solution)/shard_map/ppermute | solution.py:175
  91.9 28.1 %collective-permute-start.14 = (bf16[256,896]{1,0:T(8,128)(2,1)S(1)}, bf16[256,896]{1,0:T(8,128)(2,1)S(1)}, u32[]{:S(2)}, u32[]{:S(2)}) collective-permute-start(bf16[256,896]{1,0:T(8,128)(2,1)S(1)} %add_convert_fusion), channel_id=1, source_target_pairs={{0,5},{1,6},{2,7},{3,4},{8,13},{9,14},{10,15},{11,12},{16,21},{17,... | collective-permute-start | bytes 1376264 | tf_op jit(solution)/shard_map/ppermute | solution.py:175
  93.2 26.8 %collective-permute-start.13 = (bf16[256,896]{1,0:T(8,128)(2,1)S(1)}, bf16[256,896]{1,0:T(8,128)(2,1)S(1)}, u32[]{:S(2)}, u32[]{:S(2)}) collective-permute-start(bf16[256,896]{1,0:T(8,128)(2,1)S(1)} %add_convert_fusion), channel_id=1, source_target_pairs={{0,4},{1,5},{2,6},{3,7},{8,12},{9,13},{10,14},{11,15},{16,20},{17,... | collective-permute-start | bytes 1376264 | tf_op jit(solution)/shard_map/ppermute | solution.py:175
  125.1 13.3 %collective-permute-start.20 = (bf16[1,130,4,128]{3,1,2,0:T(8,128)(2,1)S(1)}, bf16[1,130,4,128]{3,1,2,0:T(8,128)(2,1)S(1)}, u32[]{:S(2)}, u32[]{:S(2)}) collective-permute-start(bf16[1,130,4,128]{3,1,2,0:T(8,128)(2,1)S(1)} %pad_maximum_fusion.4), channel_id=1, source_target_pairs={{4,12},{12,20},{20,28},{28,36},{36,44},{44,52},{52,60},{60,68},{68... | collective-permute-start | bytes 399368 | tf_op jit(solution)/shard_map/ppermute | solution.py:20
  126.5 12.0 %collective-permute-start.17 = (bf16[1,130,4,128]{3,1,2,0:T(8,128)(2,1)S(1)}, bf16[1,130,4,128]{3,1,2,0:T(8,128)(2,1)S(1)}, u32[]{:S(2)}, u32[]{:S(2)}) collective-permute-start(bf16[1,130,4,128]{3,1,2,0:T(8,128)(2,1)S(1)} %pad_maximum_fusion.4), channel_id=1, source_target_pairs={{4,36},{12,44},{20,52},{28,60},{36,68},{44,76},{52,84},{60,92},{68... | collective-permute-start | bytes 399368 | tf_op jit(solution)/shard_map/ppermute | solution.py:20
  131.1 12.1 %collective-permute-start.18 = (bf16[1,130,4,128]{3,1,2,0:T(8,128)(2,1)S(1)}, bf16[1,130,4,128]{3,1,2,0:T(8,128)(2,1)S(1)}, u32[]{:S(2)}, u32[]{:S(2)}) collective-permute-start(bf16[1,130,4,128]{3,1,2,0:T(8,128)(2,1)S(1)} %pad_maximum_fusion.4), channel_id=1, source_target_pairs={{4,28},{12,36},{20,44},{28,52},{36,60},{44,68},{52,76},{60,84},{68... | collective-permute-start | bytes 399368 | tf_op jit(solution)/shard_map/ppermute | solution.py:20
  134.4 10.9 %collective-permute-start.19 = (bf16[1,130,4,128]{3,1,2,0:T(8,128)(2,1)S(1)}, bf16[1,130,4,128]{3,1,2,0:T(8,128)(2,1)S(1)}, u32[]{:S(2)}, u32[]{:S(2)}) collective-permute-start(bf16[1,130,4,128]{3,1,2,0:T(8,128)(2,1)S(1)} %pad_maximum_fusion.4), channel_id=1, source_target_pairs={{4,20},{12,28},{20,36},{28,44},{36,52},{44,60},{52,68},{60,76},{68... | collective-permute-start | bytes 399368 | tf_op jit(solution)/shard_map/ppermute | solution.py:20
  146.7 15.3 %collective-permute-start.22 = (bf16[1,130,4,128]{3,1,2,0:T(8,128)(2,1)S(1)}, bf16[1,130,4,128]{3,1,2,0:T(8,128)(2,1)}, u32[]{:S(2)}, u32[]{:S(2)}) collective-permute-start(bf16[1,130,4,128]{3,1,2,0:T(8,128)(2,1)S(1)} %pad_maximum_fusion.5), channel_id=1, source_target_pairs={{4,36},{12,44},{20,52},{28,60},{36,68},{44,76},{52,84},{60,92},{68... | collective-permute-start | bytes 399368 | tf_op jit(solution)/shard_map/ppermute | solution.py:20
  154.1 11.0 %collective-permute-start.21 = (bf16[1,130,4,128]{3,1,2,0:T(8,128)(2,1)S(1)}, bf16[1,130,4,128]{3,1,2,0:T(8,128)(2,1)S(1)}, u32[]{:S(2)}, u32[]{:S(2)}) collective-permute-start(bf16[1,130,4,128]{3,1,2,0:T(8,128)(2,1)S(1)} %pad_maximum_fusion.5), channel_id=1, source_target_pairs={{4,68},{12,76},{20,84},{28,92},{36,100},{44,108},{52,116},{60,124}... | collective-permute-start | bytes 399368 | tf_op jit(solution)/shard_map/ppermute | solution.py:20
  166.7 19.2 %collective-permute-start.29 = (bf16[1,130,4,128]{3,1,2,0:T(8,128)(2,1)S(1)}, bf16[1,130,4,128]{3,1,2,0:T(8,128)(2,1)S(1)}, u32[]{:S(2)}, u32[]{:S(2)}) collective-permute-start(bf16[1,130,4,128]{3,1,2,0:T(8,128)(2,1)S(1)} %pad_maximum_fusion.6), channel_id=1, source_target_pairs={{4,100},{12,108},{20,116},{28,124},{36,132},{44,140},{52,148},{60,... | collective-permute-start | bytes 399368 | tf_op jit(solution)/shard_map/ppermute | solution.py:20
  172.8 15.0 %collective-permute-start.28 = (bf16[1,130,4,128]{3,1,2,0:T(8,128)(2,1)S(1)}, bf16[1,130,4,128]{3,1,2,0:T(8,128)(2,1)S(1)}, u32[]{:S(2)}, u32[]{:S(2)}) collective-permute-start(bf16[1,130,4,128]{3,1,2,0:T(8,128)(2,1)S(1)} %pad_maximum_fusion.6), channel_id=1, source_target_pairs={{4,196},{12,204},{20,212},{28,220},{36,228},{44,236},{52,244},{60,... | collective-permute-start | bytes 399368 | tf_op jit(solution)/shard_map/ppermute | solution.py:20
  178.9 10.4 %collective-permute-start.27 = (bf16[1,130,4,128]{3,1,2,0:T(8,128)(2,1)S(1)}, bf16[1,130,4,128]{3,1,2,0:T(8,128)(2,1)S(1)}, u32[]{:S(2)}, u32[]{:S(2)}) collective-permute-start(bf16[1,130,4,128]{3,1,2,0:T(8,128)(2,1)S(1)} %pad_maximum_fusion.6), channel_id=1, source_target_pairs={{4,292},{12,300},{20,308},{28,316},{36,324},{44,332},{52,340},{60,... | collective-permute-start | bytes 399368 | tf_op jit(solution)/shard_map/ppermute | solution.py:20
  184.6 8.8 %collective-permute-start.25 = (bf16[1,130,4,128]{3,1,2,0:T(8,128)(2,1)S(1)}, bf16[1,130,4,128]{3,1,2,0:T(8,128)(2,1)S(1)}, u32[]{:S(2)}, u32[]{:S(2)}) collective-permute-start(bf16[1,130,4,128]{3,1,2,0:T(8,128)(2,1)S(1)} %pad_maximum_fusion.6), channel_id=1, source_target_pairs={{4,484},{12,492},{20,500},{28,508},{36,516},{44,524},{52,532},{60,... | collective-permute-start | bytes 399368 | tf_op jit(solution)/shard_map/ppermute | solution.py:20
  185.9 9.0 %collective-permute-start.24 = (bf16[1,130,4,128]{3,1,2,0:T(8,128)(2,1)S(1)}, bf16[1,130,4,128]{3,1,2,0:T(8,128)(2,1)S(1)}, u32[]{:S(2)}, u32[]{:S(2)}) collective-permute-start(bf16[1,130,4,128]{3,1,2,0:T(8,128)(2,1)S(1)} %pad_maximum_fusion.6), channel_id=1, source_target_pairs={{4,580},{12,588},{20,596},{28,604},{36,612},{44,620},{52,628},{60,... | collective-permute-start | bytes 399368 | tf_op jit(solution)/shard_map/ppermute | solution.py:20
  (21 other events, 300.5 us)

commit v11 on v9

--- a/solution.py
+++ b/solution.py
@@ -60,7 +60,7 @@
     sections = lax.axis_size("section")
     relay = 12
     bundled = (span_blocks - relay) // 2 + 1
-    plan = [(0, 1), (2, 3), (4, 9), (6, 11), (8, None), (10, None)]
+    plan = [(0, 1), (2, 3), (4, 9), (6, 11), (8, None)]
     running = jnp.zeros((key_heads, group_size, row_count, head_size), jnp.float32)
     totals = jnp.zeros((key_heads, group_size, row_count), jnp.float32)
     best = jnp.full((key_heads, group_size, row_count), -1e30, jnp.float32)
@@ -126,11 +126,16 @@
         ("ctx", "section"),
         [(i * sections, (i + 1) * sections + 1) for i in range(shards - 1)],
     )
+    returned = lax.ppermute(
+        held[2],
+        ("ctx", "section"),
+        [(i * sections + 1, (i + 1) * sections) for i in range(shards - 1)],
+    )
     slots = [
         (bundle, 0, forwarded, 0, relay, 5),
         (bundle, 1, forwarded, 1, relay + 2, 7),
         (bundle, 2, bundle, 0, relay + 4, relay + 1),
-        (bundle, 2, bundle, 1, span_blocks + 1, relay + 3),
+        (returned, 0, bundle, 1, 10, relay + 3),
     ]
     width_of = 2 * key_width
     for first_array, first_slot, second_array, second_slot, first_distance, second_distance in slots:

time: 199 us -> 200 us (level)
  waiting for transfers between devices: 49.1 us -> 51.6 us
    ppermute x1, starting transfers between devices: 4.62 us -> 1.45 us  [body(): lax.ppermute(jnp.concatenate([running, totals[..., None], best[..., None]...]
    ppermute x6 -> x5, waiting for transfers between devices: 4.39 us -> 7.48 us  [body(): lax.ppermute(packed, ('ctx', 'section'), both_pairs(first_distance, secon...]
    ppermute x0 -> x1, starting transfers between devices: none -> 2.88 us  [body(): lax.ppermute(held[2], ('ctx', 'section'), [(i * sections + 1, (i + 1) * s...]
    ppermute x1, waiting for transfers between devices: 7.12 us -> 4.29 us  [body(): lax.ppermute(jnp.concatenate(held[:bundled], axis=1), ('ctx', 'section'),...]
    ppermute x6 -> x5, starting transfers between devices: 24.4 us -> 22.3 us  [body(): lax.ppermute(packed, ('ctx', 'section'), both_pairs(first_distance, secon...]
    and x10 -> x9, other arithmetic: 6.33 us -> 5.73 us  [blend(): (source >= 0) & (positions < lengths[jnp.clip(source, 0, shards - 1)])]
  transfers between devices with their start and end apart: 30 -> 30, of which waited for: 10 -> 13; matrix products, arithmetic and copies ran while one was open for 11% -> 10% of each run, Pallas kernels for 0% -> 0%
where the time goes in v11:
time: 200 us; the launch traced here: 198 us
  starting transfers between devices  99 us (50%)
  waiting for transfers between devices  51.6 us (26%)
  other arithmetic  25.1 us (13%)
  matrix products  13.8 us (7%)
  local copies, waits for them, and re-layouts  7.05 us (4%)
  between operations  2.01 us (1%)
    ppermute x13, starting transfers between devices, passed_along(): return lax.ppermute(x, ('ctx', 'section'), pairs)  52.5 us
    ppermute x4, waiting for transfers between devices, body(): lax.ppermute(own_hidden, ('section', 'tp'), [(m, members + (m + step) % m...  24.7 us
    ppermute x5, starting transfers between devices, body(): lax.ppermute(packed, ('ctx', 'section'), both_pairs(first_distance, secon...  22.3 us
    ppermute x13, waiting for transfers between devices, passed_along(): return lax.ppermute(x, ('ctx', 'section'), pairs)  11.3 us
    ppermute x1, starting transfers between devices, body(): lax.ppermute(jnp.concatenate(held[:bundled], axis=1), ('ctx', 'section'),...  9.15 us
    ppermute x5, waiting for transfers between devices, body(): lax.ppermute(packed, ('ctx', 'section'), both_pairs(first_distance, secon...  7.48 us
    and x9, other arithmetic, blend(): (source >= 0) & (positions < lengths[jnp.clip(source, 0, shards - 1)])  5.73 us
    ppermute x4, starting transfers between devices, body(): lax.ppermute(own_hidden, ('section', 'tp'), [(m, members + (m + step) % m...  5.17 us
  transfers between devices with their start and end apart: 30, of which 13 were waited for; matrix products, arithmetic and copies ran while one was open for 10% of the time, Pallas kernels for 0%

profile of v11, /device:TPU:1, one launch (start us, length us, event | category | flops | bytes accessed | tf_op | source)
XLA Modules:
  0.0 198.5 jit_solution(8109215351240262545)
XLA Ops:
  3.0 1.7 fusion.309
  11.6 2.9 %collective-permute-done = bf16[256,640]{1,0:T(8,128)(2,1)S(1)} collective-permute-done((bf16[256,640]{1,0:T(8,128)(2,1)S(1)}, bf16[256,640]{1,0:T(8,128)(2,1)S(1)}, u32[]{:S(2)}, u32[]{:S(2)}) %collective-permute-start) | collective-permute-done | bytes 327712 | tf_op jit(solution)/shard_map/ppermute | solution.py:52
  16.3 12.2 %collective-permute-start.4 = (bf16[256,256]{1,0:T(8,128)(2,1)S(1)}, bf16[256,256]{1,0:T(8,128)(2,1)S(1)}, u32[]{:S(2)}, u32[]{:S(2)}) collective-permute-start(bf16[256,256]{1,0:T(8,128)(2,1)S(1)} %pad_maximum_fusion.7), channel_id=1, source_target_pairs={{0,48},{8,56},{16,64},{24,72},{32,80},{40,88},{48,96},{56,104},{64... | collective-permute-start | bytes 393224 | tf_op jit(solution)/shard_map/ppermute | solution.py:114
  28.5 3.2 %collective-permute-start.3 = (bf16[256,256]{1,0:T(8,128)(2,1)S(1)}, bf16[256,256]{1,0:T(8,128)(2,1)S(1)}, u32[]{:S(2)}, u32[]{:S(2)}) collective-permute-start(bf16[256,256]{1,0:T(8,128)(2,1)S(1)} %pad_maximum_fusion.7), channel_id=1, source_target_pairs={{0,32},{8,40},{16,48},{24,56},{32,64},{40,72},{48,80},{56,88},{64,... | collective-permute-start | bytes 393224 | tf_op jit(solution)/shard_map/ppermute | solution.py:114
  31.7 4.9 %collective-permute-start.2 = (bf16[256,256]{1,0:T(8,128)(2,1)S(1)}, bf16[256,256]{1,0:T(8,128)(2,1)S(1)}, u32[]{:S(2)}, u32[]{:S(2)}) collective-permute-start(bf16[256,256]{1,0:T(8,128)(2,1)S(1)} %pad_maximum_fusion.7), channel_id=1, source_target_pairs={{0,16},{8,24},{16,32},{24,40},{32,48},{40,56},{48,64},{56,72},{64,... | collective-permute-start | bytes 393224 | tf_op jit(solution)/shard_map/ppermute | solution.py:114
  40.3 7.5 %collective-permute-done.1 = bf16[256,256]{1,0:T(8,128)(2,1)S(1)} collective-permute-done((bf16[256,256]{1,0:T(8,128)(2,1)S(1)}, bf16[256,256]{1,0:T(8,128)(2,1)S(1)}, u32[]{:S(2)}, u32[]{:S(2)}) %collective-permute-start.1) | collective-permute-done | bytes 131104 | tf_op jit(solution)/shard_map/ppermute | solution.py:114
  48.7 9.2 %collective-permute-start.6 = (bf16[256,768]{1,0:T(8,128)(2,1)S(1)}, bf16[256,768]{1,0:T(8,128)(2,1)S(1)}, u32[]{:S(2)}, u32[]{:S(2)}) collective-permute-start(bf16[256,768]{1,0:T(8,128)(2,1)S(1)} %pad_maximum_fusion.1), channel_id=1, source_target_pairs={{0,96},{8,104},{16,112},{24,120},{32,128},{40,136},{48,144},{56,15... | collective-permute-start | bytes 1179656 | tf_op jit(solution)/shard_map/ppermute | solution.py:121
  58.2 2.9 %collective-permute-start.8 = (bf16[256,256]{1,0:T(8,128)(2,1)S(1)}, bf16[256,256]{1,0:T(8,128)(2,1)S(1)}, u32[]{:S(2)}, u32[]{:S(2)}) collective-permute-start(bf16[256,256]{1,0:T(8,128)(2,1)S(1)} %collective-permute-done.3), channel_id=1, source_target_pairs={{4,8},{12,16},{20,24},{28,32},{36,40},{44,48},{52,56},{60,64},{68,... | collective-permute-start | bytes 393224 | tf_op jit(solution)/shard_map/ppermute | solution.py:129
  63.0 4.3 %collective-permute-done.6 = bf16[256,768]{1,0:T(8,128)(2,1)S(1)} collective-permute-done((bf16[256,768]{1,0:T(8,128)(2,1)S(1)}, bf16[256,768]{1,0:T(8,128)(2,1)S(1)}, u32[]{:S(2)}, u32[]{:S(2)}) %collective-permute-start.6) | collective-permute-done | bytes 393248 | tf_op jit(solution)/shard_map/ppermute | solution.py:121
  77.1 3.2 %convolution_convert_fusion = bf16[256,3584]{1,0:T(8,128)(2,1)S(1)} fusion(bf16[256,512]{0,1:T(8,128)(2,1)S(1)} %bitcast.525, bf16[1,512,3584]{2,1,0:T(8,128)(2,1)} %param.14), kind=kOutput, calls=%fused_computation | convolution fusion | flops 940441600 | bytes 5767168 | tf_op jit(solution)/shard_map/dot_general | solution.py:163
  94.4 17.0 %collective-permute-done.16 = bf16[256,896]{1,0:T(8,128)(2,1)S(1)} collective-permute-done((bf16[256,896]{1,0:T(8,128)(2,1)S(1)}, bf16[256,896]{1,0:T(8,128)(2,1)S(1)}, u32[]{:S(2)}, u32[]{:S(2)}) %collective-permute-start.16) | collective-permute-done | bytes 458784 | tf_op jit(solution)/shard_map/ppermute | solution.py:180
  111.4 2.9 %collective-permute-done.15 = bf16[256,896]{1,0:T(8,128)(2,1)S(1)} collective-permute-done((bf16[256,896]{1,0:T(8,128)(2,1)S(1)}, bf16[256,896]{1,0:T(8,128)(2,1)S(1)}, u32[]{:S(2)}, u32[]{:S(2)}) %collective-permute-start.15) | collective-permute-done | bytes 458784 | tf_op jit(solution)/shard_map/ppermute | solution.py:180
  114.3 4.8 %collective-permute-done.14 = bf16[256,896]{1,0:T(8,128)(2,1)S(1)} collective-permute-done((bf16[256,896]{1,0:T(8,128)(2,1)S(1)}, bf16[256,896]{1,0:T(8,128)(2,1)S(1)}, u32[]{:S(2)}, u32[]{:S(2)}) %collective-permute-start.14) | collective-permute-done | bytes 458784 | tf_op jit(solution)/shard_map/ppermute | solution.py:180
  125.4 3.7 %collective-permute-start.17 = (bf16[1,130,4,128]{3,1,2,0:T(8,128)(2,1)S(1)}, bf16[1,130,4,128]{3,1,2,0:T(8,128)(2,1)S(1)}, u32[]{:S(2)}, u32[]{:S(2)}) collective-permute-start(bf16[1,130,4,128]{3,1,2,0:T(8,128)(2,1)S(1)} %pad_maximum_fusion.4), channel_id=1, source_target_pairs={{4,28},{12,36},{20,44},{28,52},{36,60},{44,68},{52,76},{60,84},{68... | collective-permute-start | bytes 399368 | tf_op jit(solution)/shard_map/ppermute | solution.py:20
  129.1 4.1 %collective-permute-start.18 = (bf16[1,130,4,128]{3,1,2,0:T(8,128)(2,1)S(1)}, bf16[1,130,4,128]{3,1,2,0:T(8,128)(2,1)S(1)}, u32[]{:S(2)}, u32[]{:S(2)}) collective-permute-start(bf16[1,130,4,128]{3,1,2,0:T(8,128)(2,1)S(1)} %pad_maximum_fusion.4), channel_id=1, source_target_pairs={{4,20},{12,28},{20,36},{28,44},{36,52},{44,60},{52,68},{60,76},{68... | collective-permute-start | bytes 399368 | tf_op jit(solution)/shard_map/ppermute | solution.py:20
  133.4 2.7 %collective-permute-done.18 = bf16[1,130,4,128]{3,1,2,0:T(8,128)(2,1)S(1)} collective-permute-done((bf16[1,130,4,128]{3,1,2,0:T(8,128)(2,1)S(1)}, bf16[1,130,4,128]{3,1,2,0:T(8,128)(2,1)S(1)}, u32[]{:S(2)}, u32[]{:S(2)}) %collective-permute-start.18) | collective-permute-done | bytes 133152 | tf_op jit(solution)/shard_map/ppermute | solution.py:20
  137.4 7.4 %collective-permute-start.22 = (bf16[1,130,4,128]{3,1,2,0:T(8,128)(2,1)S(1)}, bf16[1,130,4,128]{3,1,2,0:T(8,128)(2,1)}, u32[]{:S(2)}, u32[]{:S(2)}) collective-permute-start(bf16[1,130,4,128]{3,1,2,0:T(8,128)(2,1)S(1)} %pad_maximum_fusion.5), channel_id=1, source_target_pairs={{4,28},{12,36},{20,44},{28,52},{36,60},{44,68},{52,76},{60,84},{68... | collective-permute-start | bytes 399368 | tf_op jit(solution)/shard_map/ppermute | solution.py:20
  144.8 7.0 %collective-permute-start.20 = (bf16[1,130,4,128]{3,1,2,0:T(8,128)(2,1)S(1)}, bf16[1,130,4,128]{3,1,2,0:T(8,128)(2,1)}, u32[]{:S(2)}, u32[]{:S(2)}) collective-permute-start(bf16[1,130,4,128]{3,1,2,0:T(8,128)(2,1)S(1)} %pad_maximum_fusion.5), channel_id=1, source_target_pairs={{4,76},{12,84},{20,92},{28,100},{36,108},{44,116},{52,124},{60,132... | collective-permute-start | bytes 399368 | tf_op jit(solution)/shard_map/ppermute | solution.py:20
  151.9 6.6 %collective-permute-start.21 = (bf16[1,130,4,128]{3,1,2,0:T(8,128)(2,1)S(1)}, bf16[1,130,4,128]{3,1,2,0:T(8,128)(2,1)S(1)}, u32[]{:S(2)}, u32[]{:S(2)}) collective-permute-start(bf16[1,130,4,128]{3,1,2,0:T(8,128)(2,1)S(1)} %pad_maximum_fusion.5), channel_id=1, source_target_pairs={{4,52},{12,60},{20,68},{28,76},{36,84},{44,92},{52,100},{60,108},{... | collective-permute-start | bytes 399368 | tf_op jit(solution)/shard_map/ppermute | solution.py:20
  161.7 1.7 collective-permute-done.21
  165.1 6.8 %collective-permute-start.29 = (bf16[1,130,4,128]{3,1,2,0:T(8,128)(2,1)S(1)}, bf16[1,130,4,128]{3,1,2,0:T(8,128)(2,1)S(1)}, u32[]{:S(2)}, u32[]{:S(2)}) collective-permute-start(bf16[1,130,4,128]{3,1,2,0:T(8,128)(2,1)S(1)} %pad_maximum_fusion.6), channel_id=1, source_target_pairs={{4,100},{12,108},{20,116},{28,124},{36,132},{44,140},{52,148},{60,... | collective-permute-start | bytes 399368 | tf_op jit(solution)/shard_map/ppermute | solution.py:20
  172.8 6.0 %collective-permute-start.28 = (bf16[1,130,4,128]{3,1,2,0:T(8,128)(2,1)S(1)}, bf16[1,130,4,128]{3,1,2,0:T(8,128)(2,1)S(1)}, u32[]{:S(2)}, u32[]{:S(2)}) collective-permute-start(bf16[1,130,4,128]{3,1,2,0:T(8,128)(2,1)S(1)} %pad_maximum_fusion.6), channel_id=1, source_target_pairs={{4,196},{12,204},{20,212},{28,220},{36,228},{44,236},{52,244},{60,... | collective-permute-start | bytes 399368 | tf_op jit(solution)/shard_map/ppermute | solution.py:20
  178.8 3.9 %collective-permute-start.27 = (bf16[1,130,4,128]{3,1,2,0:T(8,128)(2,1)S(1)}, bf16[1,130,4,128]{3,1,2,0:T(8,128)(2,1)S(1)}, u32[]{:S(2)}, u32[]{:S(2)}) collective-permute-start(bf16[1,130,4,128]{3,1,2,0:T(8,128)(2,1)S(1)} %pad_maximum_fusion.6), channel_id=1, source_target_pairs={{4,292},{12,300},{20,308},{28,316},{36,324},{44,332},{52,340},{60,... | collective-permute-start | bytes 399368 | tf_op jit(solution)/shard_map/ppermute | solution.py:20
  189.1 4.0 %collective-permute-done.25 = bf16[1,130,4,128]{3,1,2,0:T(8,128)(2,1)S(1)} collective-permute-done((bf16[1,130,4,128]{3,1,2,0:T(8,128)(2,1)S(1)}, bf16[1,130,4,128]{3,1,2,0:T(8,128)(2,1)S(1)}, u32[]{:S(2)}, u32[]{:S(2)}) %collective-permute-start.25) | collective-permute-done | bytes 133152 | tf_op jit(solution)/shard_map/ppermute | solution.py:20
  (198 shorter events, 65.8 us)
Async XLA Ops:
  1.7 12.9 %collective-permute-start = (bf16[256,640]{1,0:T(8,128)(2,1)S(1)}, bf16[256,640]{1,0:T(8,128)(2,1)S(1)}, u32[]{:S(2)}, u32[]{:S(2)}) collective-permute-start(bf16[256,640]{1,0:T(8,128)(2,1)S(1)} %pad_maximum_fusion.2), channel_id=1, source_target_pairs={{0,4},{1,5},{2,6},{3,7},{8,12},{9,13},{10,14},{11,15},{16,20},{17,... | collective-permute-start | bytes 983048 | tf_op jit(solution)/shard_map/ppermute | solution.py:52
  16.3 23.3 %collective-permute-start.4 = (bf16[256,256]{1,0:T(8,128)(2,1)S(1)}, bf16[256,256]{1,0:T(8,128)(2,1)S(1)}, u32[]{:S(2)}, u32[]{:S(2)}) collective-permute-start(bf16[256,256]{1,0:T(8,128)(2,1)S(1)} %pad_maximum_fusion.7), channel_id=1, source_target_pairs={{0,48},{8,56},{16,64},{24,72},{32,80},{40,88},{48,96},{56,104},{64... | collective-permute-start | bytes 393224 | tf_op jit(solution)/shard_map/ppermute | solution.py:114
  28.5 11.1 %collective-permute-start.3 = (bf16[256,256]{1,0:T(8,128)(2,1)S(1)}, bf16[256,256]{1,0:T(8,128)(2,1)S(1)}, u32[]{:S(2)}, u32[]{:S(2)}) collective-permute-start(bf16[256,256]{1,0:T(8,128)(2,1)S(1)} %pad_maximum_fusion.7), channel_id=1, source_target_pairs={{0,32},{8,40},{16,48},{24,56},{32,64},{40,72},{48,80},{56,88},{64,... | collective-permute-start | bytes 393224 | tf_op jit(solution)/shard_map/ppermute | solution.py:114
  31.7 17.0 %collective-permute-start.2 = (bf16[256,256]{1,0:T(8,128)(2,1)S(1)}, bf16[256,256]{1,0:T(8,128)(2,1)S(1)}, u32[]{:S(2)}, u32[]{:S(2)}) collective-permute-start(bf16[256,256]{1,0:T(8,128)(2,1)S(1)} %pad_maximum_fusion.7), channel_id=1, source_target_pairs={{0,16},{8,24},{16,32},{24,40},{32,48},{40,56},{48,64},{56,72},{64,... | collective-permute-start | bytes 393224 | tf_op jit(solution)/shard_map/ppermute | solution.py:114
  36.6 11.2 %collective-permute-start.1 = (bf16[256,256]{1,0:T(8,128)(2,1)S(1)}, bf16[256,256]{1,0:T(8,128)(2,1)S(1)}, u32[]{:S(2)}, u32[]{:S(2)}) collective-permute-start(bf16[256,256]{1,0:T(8,128)(2,1)S(1)} %pad_maximum_fusion.7), channel_id=1, source_target_pairs={{4,12},{12,20},{20,28},{28,36},{36,44},{44,52},{52,60},{60,68},{68... | collective-permute-start | bytes 393224 | tf_op jit(solution)/shard_map/ppermute | solution.py:114
  37.9 24.1 %collective-permute-start.5 = (bf16[256,256]{1,0:T(8,128)(2,1)S(1)}, bf16[256,256]{1,0:T(8,128)(2,1)S(1)}, u32[]{:S(2)}, u32[]{:S(2)}) collective-permute-start(bf16[256,256]{1,0:T(8,128)(2,1)S(1)} %pad_maximum_fusion.7), channel_id=1, source_target_pairs={{0,64},{8,72},{16,80},{24,88},{32,96},{40,104},{48,112},{56,120},{... | collective-permute-start | bytes 393224 | tf_op jit(solution)/shard_map/ppermute | solution.py:114
  39.6 23.4 %collective-permute-start.7 = (bf16[256,512]{1,0:T(8,128)(2,1)S(1)}, bf16[256,512]{1,0:T(8,128)(2,1)S(1)}, u32[]{:S(2)}, u32[]{:S(2)}) collective-permute-start(bf16[256,512]{1,0:T(8,128)(2,1)S(1)} %pad_maximum_fusion.3), channel_id=1, source_target_pairs={{0,12},{8,20},{16,28},{24,36},{32,44},{40,52},{48,60},{56,68},{64,... | collective-permute-start | bytes 786440 | tf_op jit(solution)/shard_map/ppermute | solution.py:124
  48.7 18.6 %collective-permute-start.6 = (bf16[256,768]{1,0:T(8,128)(2,1)S(1)}, bf16[256,768]{1,0:T(8,128)(2,1)S(1)}, u32[]{:S(2)}, u32[]{:S(2)}) collective-permute-start(bf16[256,768]{1,0:T(8,128)(2,1)S(1)} %pad_maximum_fusion.1), channel_id=1, source_target_pairs={{0,96},{8,104},{16,112},{24,120},{32,128},{40,136},{48,144},{56,15... | collective-permute-start | bytes 1179656 | tf_op jit(solution)/shard_map/ppermute | solution.py:121
  88.3 23.1 %collective-permute-start.16 = (bf16[256,896]{1,0:T(8,128)(2,1)S(1)}, bf16[256,896]{1,0:T(8,128)(2,1)S(1)}, u32[]{:S(2)}, u32[]{:S(2)}) collective-permute-start(bf16[256,896]{1,0:T(8,128)(2,1)S(1)} %add_convert_fusion), channel_id=1, source_target_pairs={{0,7},{1,4},{2,5},{3,6},{8,15},{9,12},{10,13},{11,14},{16,23},{17,... | collective-permute-start | bytes 1376264 | tf_op jit(solution)/shard_map/ppermute | solution.py:180
  89.6 24.7 %collective-permute-start.15 = (bf16[256,896]{1,0:T(8,128)(2,1)S(1)}, bf16[256,896]{1,0:T(8,128)(2,1)S(1)}, u32[]{:S(2)}, u32[]{:S(2)}) collective-permute-start(bf16[256,896]{1,0:T(8,128)(2,1)S(1)} %add_convert_fusion), channel_id=1, source_target_pairs={{0,6},{1,7},{2,4},{3,5},{8,14},{9,15},{10,12},{11,13},{16,22},{17,... | collective-permute-start | bytes 1376264 | tf_op jit(solution)/shard_map/ppermute | solution.py:180
  90.9 28.2 %collective-permute-start.14 = (bf16[256,896]{1,0:T(8,128)(2,1)S(1)}, bf16[256,896]{1,0:T(8,128)(2,1)S(1)}, u32[]{:S(2)}, u32[]{:S(2)}) collective-permute-start(bf16[256,896]{1,0:T(8,128)(2,1)S(1)} %add_convert_fusion), channel_id=1, source_target_pairs={{0,5},{1,6},{2,7},{3,4},{8,13},{9,14},{10,15},{11,12},{16,21},{17,... | collective-permute-start | bytes 1376264 | tf_op jit(solution)/shard_map/ppermute | solution.py:180
  92.2 26.9 %collective-permute-start.13 = (bf16[256,896]{1,0:T(8,128)(2,1)S(1)}, bf16[256,896]{1,0:T(8,128)(2,1)S(1)}, u32[]{:S(2)}, u32[]{:S(2)}) collective-permute-start(bf16[256,896]{1,0:T(8,128)(2,1)S(1)} %add_convert_fusion), channel_id=1, source_target_pairs={{0,4},{1,5},{2,6},{3,7},{8,12},{9,13},{10,14},{11,15},{16,20},{17,... | collective-permute-start | bytes 1376264 | tf_op jit(solution)/shard_map/ppermute | solution.py:180
  124.1 9.2 %collective-permute-start.19 = (bf16[1,130,4,128]{3,1,2,0:T(8,128)(2,1)S(1)}, bf16[1,130,4,128]{3,1,2,0:T(8,128)(2,1)S(1)}, u32[]{:S(2)}, u32[]{:S(2)}) collective-permute-start(bf16[1,130,4,128]{3,1,2,0:T(8,128)(2,1)S(1)} %pad_maximum_fusion.4), channel_id=1, source_target_pairs={{4,12},{12,20},{20,28},{28,36},{36,44},{44,52},{52,60},{60,68},{68... | collective-permute-start | bytes 399368 | tf_op jit(solution)/shard_map/ppermute | solution.py:20
  125.4 7.9 %collective-permute-start.17 = (bf16[1,130,4,128]{3,1,2,0:T(8,128)(2,1)S(1)}, bf16[1,130,4,128]{3,1,2,0:T(8,128)(2,1)S(1)}, u32[]{:S(2)}, u32[]{:S(2)}) collective-permute-start(bf16[1,130,4,128]{3,1,2,0:T(8,128)(2,1)S(1)} %pad_maximum_fusion.4), channel_id=1, source_target_pairs={{4,28},{12,36},{20,44},{28,52},{36,60},{44,68},{52,76},{60,84},{68... | collective-permute-start | bytes 399368 | tf_op jit(solution)/shard_map/ppermute | solution.py:20
  129.1 6.9 %collective-permute-start.18 = (bf16[1,130,4,128]{3,1,2,0:T(8,128)(2,1)S(1)}, bf16[1,130,4,128]{3,1,2,0:T(8,128)(2,1)S(1)}, u32[]{:S(2)}, u32[]{:S(2)}) collective-permute-start(bf16[1,130,4,128]{3,1,2,0:T(8,128)(2,1)S(1)} %pad_maximum_fusion.4), channel_id=1, source_target_pairs={{4,20},{12,28},{20,36},{28,44},{36,52},{44,60},{52,68},{60,76},{68... | collective-permute-start | bytes 399368 | tf_op jit(solution)/shard_map/ppermute | solution.py:20
  137.4 22.5 %collective-permute-start.22 = (bf16[1,130,4,128]{3,1,2,0:T(8,128)(2,1)S(1)}, bf16[1,130,4,128]{3,1,2,0:T(8,128)(2,1)}, u32[]{:S(2)}, u32[]{:S(2)}) collective-permute-start(bf16[1,130,4,128]{3,1,2,0:T(8,128)(2,1)S(1)} %pad_maximum_fusion.5), channel_id=1, source_target_pairs={{4,28},{12,36},{20,44},{28,52},{36,60},{44,68},{52,76},{60,84},{68... | collective-permute-start | bytes 399368 | tf_op jit(solution)/shard_map/ppermute | solution.py:20
  144.8 16.0 %collective-permute-start.20 = (bf16[1,130,4,128]{3,1,2,0:T(8,128)(2,1)S(1)}, bf16[1,130,4,128]{3,1,2,0:T(8,128)(2,1)}, u32[]{:S(2)}, u32[]{:S(2)}) collective-permute-start(bf16[1,130,4,128]{3,1,2,0:T(8,128)(2,1)S(1)} %pad_maximum_fusion.5), channel_id=1, source_target_pairs={{4,76},{12,84},{20,92},{28,100},{36,108},{44,116},{52,124},{60,132... | collective-permute-start | bytes 399368 | tf_op jit(solution)/shard_map/ppermute | solution.py:20
  151.9 11.6 %collective-permute-start.21 = (bf16[1,130,4,128]{3,1,2,0:T(8,128)(2,1)S(1)}, bf16[1,130,4,128]{3,1,2,0:T(8,128)(2,1)S(1)}, u32[]{:S(2)}, u32[]{:S(2)}) collective-permute-start(bf16[1,130,4,128]{3,1,2,0:T(8,128)(2,1)S(1)} %pad_maximum_fusion.5), channel_id=1, source_target_pairs={{4,52},{12,60},{20,68},{28,76},{36,84},{44,92},{52,100},{60,108},{... | collective-permute-start | bytes 399368 | tf_op jit(solution)/shard_map/ppermute | solution.py:20
  165.1 20.6 %collective-permute-start.29 = (bf16[1,130,4,128]{3,1,2,0:T(8,128)(2,1)S(1)}, bf16[1,130,4,128]{3,1,2,0:T(8,128)(2,1)S(1)}, u32[]{:S(2)}, u32[]{:S(2)}) collective-permute-start(bf16[1,130,4,128]{3,1,2,0:T(8,128)(2,1)S(1)} %pad_maximum_fusion.6), channel_id=1, source_target_pairs={{4,100},{12,108},{20,116},{28,124},{36,132},{44,140},{52,148},{60,... | collective-permute-start | bytes 399368 | tf_op jit(solution)/shard_map/ppermute | solution.py:20
  172.8 14.8 %collective-permute-start.28 = (bf16[1,130,4,128]{3,1,2,0:T(8,128)(2,1)S(1)}, bf16[1,130,4,128]{3,1,2,0:T(8,128)(2,1)S(1)}, u32[]{:S(2)}, u32[]{:S(2)}) collective-permute-start(bf16[1,130,4,128]{3,1,2,0:T(8,128)(2,1)S(1)} %pad_maximum_fusion.6), channel_id=1, source_target_pairs={{4,196},{12,204},{20,212},{28,220},{36,228},{44,236},{52,244},{60,... | collective-permute-start | bytes 399368 | tf_op jit(solution)/shard_map/ppermute | solution.py:20
  178.8 10.3 %collective-permute-start.27 = (bf16[1,130,4,128]{3,1,2,0:T(8,128)(2,1)S(1)}, bf16[1,130,4,128]{3,1,2,0:T(8,128)(2,1)S(1)}, u32[]{:S(2)}, u32[]{:S(2)}) collective-permute-start(bf16[1,130,4,128]{3,1,2,0:T(8,128)(2,1)S(1)} %pad_maximum_fusion.6), channel_id=1, source_target_pairs={{4,292},{12,300},{20,308},{28,316},{36,324},{44,332},{52,340},{60,... | collective-permute-start | bytes 399368 | tf_op jit(solution)/shard_map/ppermute | solution.py:20
  184.4 8.8 %collective-permute-start.25 = (bf16[1,130,4,128]{3,1,2,0:T(8,128)(2,1)S(1)}, bf16[1,130,4,128]{3,1,2,0:T(8,128)(2,1)S(1)}, u32[]{:S(2)}, u32[]{:S(2)}) collective-permute-start(bf16[1,130,4,128]{3,1,2,0:T(8,128)(2,1)S(1)} %pad_maximum_fusion.6), channel_id=1, source_target_pairs={{4,484},{12,492},{20,500},{28,508},{36,516},{44,524},{52,532},{60,... | collective-permute-start | bytes 399368 | tf_op jit(solution)/shard_map/ppermute | solution.py:20
  185.7 9.0 %collective-permute-start.24 = (bf16[1,130,4,128]{3,1,2,0:T(8,128)(2,1)S(1)}, bf16[1,130,4,128]{3,1,2,0:T(8,128)(2,1)S(1)}, u32[]{:S(2)}, u32[]{:S(2)}) collective-permute-start(bf16[1,130,4,128]{3,1,2,0:T(8,128)(2,1)S(1)} %pad_maximum_fusion.6), channel_id=1, source_target_pairs={{4,580},{12,588},{20,596},{28,604},{36,612},{44,620},{52,628},{60,... | collective-permute-start | bytes 399368 | tf_op jit(solution)/shard_map/ppermute | solution.py:20
  187.6 8.6 %collective-permute-start.23 = (bf16[1,130,4,128]{3,1,2,0:T(8,128)(2,1)S(1)}, bf16[1,130,4,128]{3,1,2,0:T(8,128)(2,1)S(1)}, u32[]{:S(2)}, u32[]{:S(2)}) collective-permute-start(bf16[1,130,4,128]{3,1,2,0:T(8,128)(2,1)S(1)} %pad_maximum_fusion.6), channel_id=1, source_target_pairs={{4,676},{12,684},{20,692},{28,700},{36,708},{44,716},{52,724},{60,... | collective-permute-start | bytes 399368 | tf_op jit(solution)/shard_map/ppermute | solution.py:20
  (20 other events, 252.3 us)
